TPU v7x, 128 devices: a whole 4x4x4 slice. The times are simulated.
128 devices in a mesh: expert: 128 (over y, z, x, core).
Axes of the slice: x: 4, y: 4, z: 4, core: 2. Of those that a mesh axis runs over, the one named last changes fastest.
Arguments:
- tokens: bfloat16 [8192, 3584], P('expert'), may hold values from -6 to 6
- expert_ids: int32 [8192, 8], P('expert'), may hold values from 0 to 127, all different within a row; in each aligned block of 64 rows (0 to 63, 64 to 127, ...) at most 6 rows name the same one
- gate_weights: float32 [8192, 8], P('expert'), may hold values from 0.05 to 1
- host: int32 [128], replicated, may hold values from 0 to 127, each once
- w_in: bfloat16 [128, 2, 3584, 2, 512], P('expert'), may hold values from -0.09375 to 0.09375
- w_out: bfloat16 [128, 2, 512, 3584], P('expert'), may hold values from -0.1875 to 0.1875
Outputs:
- moe_out: bfloat16 [8192, 3584], P('expert')
Inputs may be any that keep to these rules, and one draw needn't show every extreme that they name: `expert_ids`: each row names 8 different experts; in the rows of one device no expert is named more than 6 times, a bound that some block reaches. A permutation: device d holds the weights of expert host[d].
All inputs are finite; a program needn't handle non-finite values.
Results may differ from a plain program's by a relative error of at most 0.011.
Values may be sent and summed in bfloat16 or wider, within the bound.
No kernel may reach another device: no remote copies, remote signals or barrier semaphores. Data moves between devices by JAX's collectives and lax.ppermute only.
A program may use at most 192 MiB of HBM per device.

v0:
```python
import jax
import jax.numpy as jnp
from jax import lax
from jax.sharding import PartitionSpec as P

MOST = 6


def expert_ffn(rows, first_weights, second_weights):
    projected = jnp.einsum(
        "esd,hdgu->eshgu", rows, first_weights, preferred_element_type=jnp.float32
    )
    hidden = (jax.nn.silu(projected[:, :, :, 0]) * projected[:, :, :, 1]).astype(jnp.bfloat16)
    output = jnp.einsum(
        "eshu,hud->esd", hidden, second_weights, preferred_element_type=jnp.float32
    )
    return output.astype(jnp.bfloat16)


def local(tokens, expert_ids, gate_weights, host, w_in, w_out):
    experts = lax.axis_size("expert")
    tok_dev, top_count = expert_ids.shape
    d_model = tokens.shape[1]
    slot_count = MOST
    capacity = experts * slot_count
    expert_range = jnp.arange(experts, dtype=jnp.int32)
    placed = (host[:, None] == expert_range[None, :]).astype(jnp.int32)
    holder = jnp.sum(placed * expert_range[:, None], axis=0)
    flat_experts = expert_ids.reshape(-1)
    onehot = (flat_experts[:, None] == expert_range[None, :]).astype(jnp.int32)
    within = jnp.sum(jnp.cumsum(onehot, axis=0) * onehot, axis=1) - 1
    target = jnp.sum(onehot * holder[None, :], axis=1)
    position = (target * slot_count + within).reshape(tok_dev, top_count)
    slots = jnp.arange(capacity, dtype=jnp.int32)
    hit = position[None, :, :] == slots[:, None, None]
    dispatch = jnp.any(hit, axis=2).astype(jnp.bfloat16).reshape(experts, slot_count, tok_dev)
    outgoing = jnp.einsum(
        "esk,kd->esd", dispatch, tokens, preferred_element_type=jnp.float32
    ).astype(jnp.bfloat16)
    received = lax.all_to_all(
        outgoing,
        "expert",
        split_axis=0,
        concat_axis=0,
        tiled=True,
    )
    expert_out = expert_ffn(received, w_in[0], w_out[0])
    answered = lax.all_to_all(
        expert_out,
        "expert",
        split_axis=0,
        concat_axis=0,
        tiled=True,
    )
    combine = jnp.sum(
        jnp.where(hit, gate_weights[None, :, :], jnp.float32(0.0)), axis=2
    ).T.reshape(tok_dev, experts, slot_count)
    combine_hi = combine.astype(jnp.bfloat16)
    combine_lo = (combine - combine_hi.astype(jnp.float32)).astype(jnp.bfloat16)
    weighted = jnp.einsum(
        "tes,esd->td", combine_hi, answered, preferred_element_type=jnp.float32
    ) + jnp.einsum("tes,esd->td", combine_lo, answered, preferred_element_type=jnp.float32)
    return weighted.astype(jnp.bfloat16)


def solution(mesh):
    in_specs = (
        P("expert", None),
        P("expert", None),
        P("expert", None),
        P(),
        P("expert", None, None, None, None),
        P("expert", None, None, None),
    )
    out_specs = P("expert", None)
    return jax.shard_map(local, mesh=mesh, in_specs=in_specs, out_specs=out_specs, check_vma=False)
```

profile of v0, /device:TPU:1, one launch (start us, length us, event | category | flops | bytes accessed | tf_op | source)
XLA Modules:
  0.0 247.6 jit_solution(15812741072538505735)
XLA Ops:
  0.0 0.0 copy-start
  0.0 0.8 copy.47
  0.8 0.1 eq.58
  0.9 0.1 eq.51
  1.0 0.1 copy.49
  1.1 0.2 fusion.16
  1.4 0.8 select_reduce_fusion.2
  2.2 0.3 select_reduce_fusion.1
  2.5 0.1 add.25
  2.6 0.5 fusion.12
  3.2 0.2 copy.54
  3.4 0.1 reshape.45
  3.5 0.0 copy-done
  3.5 1.6 convolution_convert_fusion
  5.1 3.1 %copy.56 = bf16[128,6,3584]{2,1,0:T(8,128)(2,1)S(1)} copy(bf16[128,6,3584]{2,0,1:T(8,128)(2,1)S(1)} %convolution_convert_fusion) | data formatting | bytes 11010048 | tf_op jit(solution)/shard_map/convert_element_type | solution.py:39
  8.1 97.8 %all_to_all.10 = bf16[128,6,3584]{2,1,0:T(8,128)(2,1)S(1)} all-to-all(bf16[128,6,3584]{2,1,0:T(8,128)(2,1)S(1)} %copy.56), channel_id=1, replica_groups=mesh['expert'=128] {'expert'}, dimensions={0} | all-to-all | bytes 11010048 | tf_op jit(solution)/shard_map/all_to_all | solution.py:40
  106.0 16.7 %fusion = f32[128,6,2,2,512]{4,0,3,2,1:T(8,128)} fusion(bf16[2,3584,2,512]{3,2,1,0:T(2,128)(2,1)} %bitcast.45, bf16[128,6,3584,1,1]{2,1,0,4,3:T(8,128)(2,1)S(1)} %bitcast.40), kind=kOutput, calls=%fused_computation | convolution fusion | flops 11274289152 | bytes 26476544 | tf_op jit(solution)/shard_map/esd,hdgu->eshgu/dot_general | solution.py:10
  122.7 10.8 %bitcast_convert_fusion = bf16[128,6,3584]{2,0,1:T(8,128)(2,1)S(1)} fusion(bf16[1,2,512,3584]{3,2,1,0:T(8,128)(2,1)} %param.11, f32[128,6,2,2,512]{4,0,3,2,1:T(8,128)} %fusion), kind=kOutput, calls=%fused_computation.3 | convolution fusion | flops 5644615680 | bytes 19136512 | tf_op jit(solution)/shard_map/eshu,hud->esd/dot_general | solution.py:14
  133.5 6.1 %copy.59 = bf16[128,6,3584]{2,1,0:T(8,128)(2,1)} copy(bf16[128,6,3584]{2,0,1:T(8,128)(2,1)S(1)} %bitcast_convert_fusion) | data formatting | bytes 11010048 | tf_op jit(solution)/shard_map/convert_element_type | solution.py:17
  139.6 0.0 copy-start.2
  139.6 5.8 %all-to-all-start.1 = ((bf16[128,6,3584]{2,1,0:T(8,128)(2,1)}), bf16[128,6,3584]{2,1,0:T(8,128)(2,1)}, u32[]{:S(2)}, u32[]{:S(2)}) async-start(bf16[128,6,3584]{2,1,0:T(8,128)(2,1)} %copy.59), calls=%async_computation.1 | async-start | bytes 14680064 | tf_op jit(solution)/shard_map/all_to_all | solution.py:48
  145.4 0.0 copy-done.2
  145.4 0.1 copy.51
  145.5 0.5 select_reduce_fusion
  146.0 0.2 copy.52
  146.2 0.1 reshape.44
  146.2 0.0 copy-start.1
  146.3 0.2 copy.53
  146.4 87.7 %all-to-all-done.1 = bf16[128,6,3584]{2,1,0:T(8,128)(2,1)} async-done(((bf16[128,6,3584]{2,1,0:T(8,128)(2,1)}), bf16[128,6,3584]{2,1,0:T(8,128)(2,1)}, u32[]{:S(2)}, u32[]{:S(2)}) %all-to-all-start.1) | async-done | bytes 5505056 | tf_op jit(solution)/shard_map/all_to_all | solution.py:48
  234.1 6.3 %convolution_bitcast_fusion.1 = f32[64,3584]{1,0:T(8,128)S(1)} fusion(bf16[128,6,3584]{2,1,0:T(8,128)(2,1)} %all-to-all-done.1, f32[64,128,6]{1,0,2:T(8,128)S(1)} %copy.53), kind=kOutput, calls=%fused_computation.9 | convolution fusion | flops 352370688 | bytes 6619136 | tf_op jit(solution)/shard_map/tes,esd->td/dot_general | solution.py:60
  240.4 7.1 %fusion.6 = bf16[64,3584]{1,0:T(8,128)(2,1)} fusion(f32[64,3584]{1,0:T(8,128)S(1)} %convolution_bitcast_fusion.1, bf16[128,6,3584]{2,1,0:T(8,128)(2,1)} %all-to-all-done.1, f32[64,128,6]{1,0,2:T(8,128)S(1)} %copy.53), kind=kOutput, calls=%fused_computation.10 | convolution fusion | flops 352976896 | bytes 7077888 | tf_op jit(solution)/shard_map/tes,esd->td/dot_general | solution.py:62
  247.6 0.0 copy-done.1
  (7 shorter events, 0.1 us)
Async XLA Ops:
  0.0 3.5 %copy-start = (bf16[64,3584]{1,0:T(8,128)(2,1)S(1)}, bf16[64,3584]{1,0:T(8,128)(2,1)}, u32[]{:S(2)}) copy-start(bf16[64,3584]{1,0:T(8,128)(2,1)} %param.6) | copy-start | bytes 1376260
  139.6 5.8 %copy-start.2 = (f32[64,8]{0,1:T(8,128)S(1)}, f32[64,8]{0,1:T(8,128)}, u32[]{:S(2)}) copy-start(f32[64,8]{0,1:T(8,128)} %param.8) | copy-start | bytes 6148
  139.6 94.5 %all-to-all-start.1 = ((bf16[128,6,3584]{2,1,0:T(8,128)(2,1)}), bf16[128,6,3584]{2,1,0:T(8,128)(2,1)}, u32[]{:S(2)}, u32[]{:S(2)}) async-start(bf16[128,6,3584]{2,1,0:T(8,128)(2,1)} %copy.59), calls=%async_computation.1 | async-start | bytes 14680064 | tf_op jit(solution)/shard_map/all_to_all | solution.py:48
  146.2 101.3 %copy-start.1 = (bf16[64,3584]{1,0:T(8,128)(2,1)S(1)}, bf16[64,3584]{1,0:T(8,128)(2,1)}, u32[]{:S(2)}) copy-start(bf16[64,3584]{1,0:T(8,128)(2,1)} %param.6) | copy-start | bytes 1376260
where the time goes:
time: 250 us; the launch traced here: 248 us
  blocking collectives  97.8 us (39%)
  waiting for transfers between devices  87.7 us (35%)
  matrix products  42.5 us (17%)
  local copies, waits for them, and re-layouts  11.2 us (4%)
  starting transfers between devices  5.75 us (2%)
    all_to_all x1, blocking collectives, local(): lax.all_to_all(outgoing, 'expert', split_axis=0, concat_axis=0, tiled=True)  97.8 us
    all_to_all x1, waiting for transfers between devices, local(): lax.all_to_all(expert_out, 'expert', split_axis=0, concat_axis=0, tiled=T...  87.7 us
    dot_general x1, matrix products, expert_ffn(): jnp.einsum('esd,hdgu->eshgu', rows, first_weights, preferred_element_type...  16.7 us
    dot_general x1, matrix products, expert_ffn(): jnp.einsum('eshu,hud->esd', hidden, second_weights, preferred_element_typ...  10.8 us
    dot_general x1, matrix products, local(): jnp.einsum('tes,esd->td', combine_lo, answered, preferred_element_type=jn...  7.14 us
    dot_general x1, matrix products, local(): jnp.einsum('tes,esd->td', combine_hi, answered, preferred_element_type=jn...  6.3 us
    convert_element_type x1, local copies, waits for them, and re-layouts, expert_ffn(): return output.astype(jnp.bfloat16)  6.1 us
    all_to_all x1, starting transfers between devices, local(): lax.all_to_all(expert_out, 'expert', split_axis=0, concat_axis=0, tiled=T...  5.75 us
  transfers between devices with their start and end apart: 1, of which 1 were waited for; matrix products, arithmetic and copies ran while one was open for 0% of the time, Pallas kernels for 0%

commit v1 on v0

--- a/solution.py
+++ b/solution.py
@@ -8,11 +8,11 @@
 
 def expert_ffn(rows, first_weights, second_weights):
     projected = jnp.einsum(
-        "esd,hdgu->eshgu", rows, first_weights, preferred_element_type=jnp.float32
+        "rd,hdgu->rhgu", rows, first_weights, preferred_element_type=jnp.float32
     )
-    hidden = (jax.nn.silu(projected[:, :, :, 0]) * projected[:, :, :, 1]).astype(jnp.bfloat16)
+    hidden = (jax.nn.silu(projected[:, :, 0]) * projected[:, :, 1]).astype(jnp.bfloat16)
     output = jnp.einsum(
-        "eshu,hud->esd", hidden, second_weights, preferred_element_type=jnp.float32
+        "rhu,hud->rd", hidden, second_weights, preferred_element_type=jnp.float32
     )
     return output.astype(jnp.bfloat16)
 
@@ -33,33 +33,35 @@
     position = (target * slot_count + within).reshape(tok_dev, top_count)
     slots = jnp.arange(capacity, dtype=jnp.int32)
     hit = position[None, :, :] == slots[:, None, None]
-    dispatch = jnp.any(hit, axis=2).astype(jnp.bfloat16).reshape(experts, slot_count, tok_dev)
-    outgoing = jnp.einsum(
-        "esk,kd->esd", dispatch, tokens, preferred_element_type=jnp.float32
-    ).astype(jnp.bfloat16)
+    dispatch = jnp.any(hit, axis=2).astype(jnp.bfloat16)
+    outgoing = jnp.dot(dispatch, tokens, preferred_element_type=jnp.float32).astype(jnp.bfloat16)
+    lane_rows = slot_count * d_model // 128
     received = lax.all_to_all(
-        outgoing,
+        outgoing.reshape(experts, lane_rows, 128),
         "expert",
         split_axis=0,
         concat_axis=0,
         tiled=True,
     )
-    expert_out = expert_ffn(received, w_in[0], w_out[0])
+    expert_out = expert_ffn(received.reshape(capacity, d_model), w_in[0], w_out[0])
     answered = lax.all_to_all(
-        expert_out,
+        expert_out.reshape(experts, lane_rows, 128),
         "expert",
         split_axis=0,
         concat_axis=0,
         tiled=True,
-    )
+    ).reshape(capacity, d_model)
     combine = jnp.sum(
         jnp.where(hit, gate_weights[None, :, :], jnp.float32(0.0)), axis=2
-    ).T.reshape(tok_dev, experts, slot_count)
+    ).T
     combine_hi = combine.astype(jnp.bfloat16)
     combine_lo = (combine - combine_hi.astype(jnp.float32)).astype(jnp.bfloat16)
-    weighted = jnp.einsum(
-        "tes,esd->td", combine_hi, answered, preferred_element_type=jnp.float32
-    ) + jnp.einsum("tes,esd->td", combine_lo, answered, preferred_element_type=jnp.float32)
+    both = jnp.dot(
+        jnp.concatenate([combine_hi, combine_lo], axis=0),
+        answered,
+        preferred_element_type=jnp.float32,
+    )
+    weighted = both[:tok_dev] + both[tok_dev:]
     return weighted.astype(jnp.bfloat16)
 
 

time: 250 us -> 235 us (0.940)
  local copies, waits for them, and re-layouts: 11.2 us -> 44.9 us
  waiting for transfers between devices: 87.7 us -> 66.1 us
  blocking collectives: 97.8 us -> 78.6 us
  matrix products: 42.5 us -> 34.9 us
    reshape x3 -> x4, local copies, waits for them, and re-layouts: 0.32 us -> 43.6 us  [the longest x1 11.2 us: local(): expert_out.reshape(experts, lane_rows, 128)]
    all_to_all x1, waiting for transfers between devices: 87.7 us -> 66.1 us  [local(): lax.all_to_all(expert_out.reshape(experts, lane_rows, 128), 'expert', spl...]
    all_to_all x1, blocking collectives: 97.8 us -> 78.6 us  [local(): lax.all_to_all(outgoing.reshape(experts, lane_rows, 128), 'expert', split...]
    convert_element_type x2 -> x0, local copies, waits for them, and re-layouts: 9.17 us -> none  [the longest x1 6.1 us: expert_ffn(): return output.astype(jnp.bfloat16)]
    dot_general x5 -> x4, matrix products: 42.5 us -> 34.9 us  [the longest x1 16.6 us: expert_ffn(): jnp.einsum('rd,hdgu->rhgu', rows, first_weights, preferred_element_type=j...]
where the time goes in v1:
time: 235 us; the launch traced here: 234 us
  blocking collectives  78.6 us (33%)
  waiting for transfers between devices  66.1 us (28%)
  local copies, waits for them, and re-layouts  44.9 us (19%)
  matrix products  34.9 us (15%)
  starting transfers between devices  5.63 us (2%)
  other arithmetic  3.28 us (1%)
    all_to_all x1, blocking collectives, local(): lax.all_to_all(outgoing.reshape(experts, lane_rows, 128), 'expert', split...  78.6 us
    all_to_all x1, waiting for transfers between devices, local(): lax.all_to_all(expert_out.reshape(experts, lane_rows, 128), 'expert', spl...  66.1 us
    dot_general x1, matrix products, expert_ffn(): jnp.einsum('rd,hdgu->rhgu', rows, first_weights, preferred_element_type=j...  16.6 us
    reshape x1, local copies, waits for them, and re-layouts, local(): expert_out.reshape(experts, lane_rows, 128)  11.2 us
    reshape x1, local copies, waits for them, and re-layouts, local(): outgoing.reshape(experts, lane_rows, 128)  11.1 us
    dot_general x1, matrix products, expert_ffn(): jnp.einsum('rhu,hud->rd', hidden, second_weights, preferred_element_type=...  10.8 us
    reshape x1, local copies, waits for them, and re-layouts, local(): answered = lax.all_to_all(expert_out.reshape(experts, lane_rows, 128), 'e...  10.7 us
    reshape x1, local copies, waits for them, and re-layouts, local(): received.reshape(capacity, d_model)  10.6 us
  transfers between devices with their start and end apart: 1, of which 1 were waited for; matrix products, arithmetic and copies ran while one was open for 0% of the time, Pallas kernels for 0%

profile of v1, /device:TPU:1, one launch (start us, length us, event | category | flops | bytes accessed | tf_op | source)
XLA Modules:
  0.0 233.6 jit_solution(2600845368514495589)
XLA Ops:
  0.0 0.0 copy-start
  0.0 0.8 copy.15
  0.8 0.1 eq.51
  0.9 0.1 eq.58
  1.0 0.8 select_reduce_fusion.2
  1.8 0.1 copy.17
  1.9 0.2 fusion.10
  2.2 0.3 select_reduce_fusion.1
  2.5 0.1 add.25
  2.6 0.5 fusion.7
  3.2 0.0 copy-done
  3.2 4.1 %convolution_convert_fusion = bf16[768,3584]{1,0:T(8,128)(2,1)} fusion(pred[768,64]{0,1:T(8,128)(4,1)S(1)} %fusion.7, bf16[64,3584]{1,0:T(8,128)(2,1)S(1)} %copy-done), kind=kOutput, calls=%fused_computation.4 | convolution fusion | flops 355074048 | bytes 6012928 | tf_op jit(solution)/shard_map/dot_general | solution.py:37
  7.3 11.1 %reshape.50 = bf16[128,168,128]{2,1,0:T(8,128)(2,1)} reshape(bf16[768,3584]{1,0:T(8,128)(2,1)} %convolution_convert_fusion) | data formatting | bytes 11010048 | tf_op jit(solution)/shard_map/reshape | solution.py:40
  18.4 78.6 %all_to_all.10 = bf16[128,168,128]{2,1,0:T(8,128)(2,1)} all-to-all(bf16[128,168,128]{2,1,0:T(8,128)(2,1)} %reshape.50), channel_id=1, replica_groups=mesh['expert'=128] {'expert'}, dimensions={0} | all-to-all | bytes 11010048 | tf_op jit(solution)/shard_map/all_to_all | solution.py:39
  97.0 10.6 %reshape.54 = bf16[768,3584,1,1]{1,0,2,3:T(8,128)(2,1)} reshape(bf16[128,168,128]{2,1,0:T(8,128)(2,1)} %all_to_all.10) | data formatting | bytes 11010048 | tf_op jit(solution)/shard_map/reshape | solution.py:46
  107.6 16.6 %fusion = f32[768,2,2,512]{3,0,2,1:T(8,128)S(1)} fusion(bf16[2,3584,2,512]{3,2,1,0:T(2,128)(2,1)} %bitcast.35, bf16[768,3584,1,1]{1,0,2,3:T(8,128)(2,1)} %reshape.54), kind=kOutput, calls=%fused_computation | convolution fusion | flops 11274289152 | bytes 26476544 | tf_op jit(solution)/shard_map/rd,hdgu->rhgu/dot_general | solution.py:10
  124.2 10.8 %bitcast_convert_fusion = bf16[768,3584]{1,0:T(8,128)(2,1)} fusion(bf16[1,2,512,3584]{3,2,1,0:T(8,128)(2,1)} %param.11, f32[768,2,2,512]{3,0,2,1:T(8,128)S(1)} %fusion), kind=kOutput, calls=%fused_computation.2 | convolution fusion | flops 5644615680 | bytes 19136512 | tf_op jit(solution)/shard_map/rhu,hud->rd/dot_general | solution.py:14
  135.0 11.2 %reshape.52 = bf16[128,168,128]{2,1,0:T(8,128)(2,1)} reshape(bf16[768,3584]{1,0:T(8,128)(2,1)} %bitcast_convert_fusion) | data formatting | bytes 11010048 | tf_op jit(solution)/shard_map/reshape | solution.py:48
  146.1 0.0 copy-start.2
  146.1 5.6 %all-to-all-start.1 = ((bf16[128,168,128]{2,1,0:T(8,128)(2,1)}), bf16[128,168,128]{2,1,0:T(8,128)(2,1)}, u32[]{:S(2)}, u32[]{:S(2)}) async-start(bf16[128,168,128]{2,1,0:T(8,128)(2,1)} %reshape.52), calls=%async_computation.1 | async-start | bytes 11010048 | tf_op jit(solution)/shard_map/all_to_all | solution.py:47
  151.8 0.0 copy-done.2
  151.8 0.1 copy.19
  151.8 0.5 select_reduce_fusion
  152.4 66.1 %all-to-all-done.1 = bf16[128,168,128]{2,1,0:T(8,128)(2,1)} async-done(((bf16[128,168,128]{2,1,0:T(8,128)(2,1)}), bf16[128,168,128]{2,1,0:T(8,128)(2,1)}, u32[]{:S(2)}, u32[]{:S(2)}) %all-to-all-start.1) | async-done | bytes 5505056 | tf_op jit(solution)/shard_map/all_to_all | solution.py:47
  218.6 10.7 %reshape.53 = bf16[768,3584]{1,0:T(8,128)(2,1)} reshape(bf16[128,168,128]{2,1,0:T(8,128)(2,1)} %all-to-all-done.1) | data formatting | bytes 11010048 | tf_op jit(solution)/shard_map/reshape | solution.py:53
  229.2 0.0 copy-start.1
  229.2 3.5 %fusion.12 = f32[128,3584]{1,0:T(8,128)S(1)} fusion(bf16[768,3584]{1,0:T(8,128)(2,1)} %reshape.53, bf16[64,768]{1,0:T(8,128)(2,1)S(1)} %get-tuple-element.7, bf16[64,768]{1,0:T(8,128)(2,1)S(1)} %get-tuple-element.8), kind=kOutput, calls=%fused_computation.21 | convolution fusion | flops 705036288 | bytes 7536640 | tf_op jit(solution)/shard_map/dot_general | solution.py:59
  232.7 0.9 fusion.8
  233.6 0.0 copy-done.1
  (8 shorter events, 0.1 us)
Async XLA Ops:
  0.0 3.2 %copy-start = (bf16[64,3584]{1,0:T(8,128)(2,1)S(1)}, bf16[64,3584]{1,0:T(8,128)(2,1)}, u32[]{:S(2)}) copy-start(bf16[64,3584]{1,0:T(8,128)(2,1)} %param.6) | copy-start | bytes 1376260
  146.1 5.6 %copy-start.2 = (f32[64,8]{0,1:T(8,128)S(1)}, f32[64,8]{0,1:T(8,128)}, u32[]{:S(2)}) copy-start(f32[64,8]{0,1:T(8,128)} %param.8) | copy-start | bytes 6148
  146.1 72.4 %all-to-all-start.1 = ((bf16[128,168,128]{2,1,0:T(8,128)(2,1)}), bf16[128,168,128]{2,1,0:T(8,128)(2,1)}, u32[]{:S(2)}, u32[]{:S(2)}) async-start(bf16[128,168,128]{2,1,0:T(8,128)(2,1)} %reshape.52), calls=%async_computation.1 | async-start | bytes 11010048 | tf_op jit(solution)/shard_map/all_to_all | solution.py:47
  229.2 4.4 %copy-start.1 = (bf16[64,3584]{1,0:T(8,128)(2,1)S(1)}, bf16[64,3584]{1,0:T(8,128)(2,1)}, u32[]{:S(2)}) copy-start(bf16[64,3584]{1,0:T(8,128)(2,1)} %param.6) | copy-start | bytes 1376260

commit v2 on v1

v2 whole, which is shorter than its diff:
```python
import jax
import jax.numpy as jnp
from jax import lax
from jax.sharding import PartitionSpec as P

MOST = 6
CHUNK = 2


def expert_ffn(rows, first_weights, second_weights):
    projected = jnp.einsum(
        "rd,hdgu->rhgu", rows, first_weights, preferred_element_type=jnp.float32
    )
    hidden = (jax.nn.silu(projected[:, :, 0]) * projected[:, :, 1]).astype(jnp.bfloat16)
    output = jnp.einsum(
        "rhu,hud->rd", hidden, second_weights, preferred_element_type=jnp.float32
    )
    return output.astype(jnp.bfloat16)


def local(tokens, expert_ids, gate_weights, host, w_in, w_out):
    experts = lax.axis_size("expert")
    tok_dev, top_count = expert_ids.shape
    d_model = tokens.shape[1]
    slot_count = MOST
    capacity = experts * slot_count
    expert_range = jnp.arange(experts, dtype=jnp.int32)
    placed = (host[:, None] == expert_range[None, :]).astype(jnp.int32)
    holder = jnp.sum(placed * expert_range[:, None], axis=0)
    flat_experts = expert_ids.reshape(-1)
    onehot = (flat_experts[:, None] == expert_range[None, :]).astype(jnp.int32)
    within = jnp.sum(jnp.cumsum(onehot, axis=0) * onehot, axis=1) - 1
    target = jnp.sum(onehot * holder[None, :], axis=1)
    chunk_rows = experts * CHUNK
    lane_rows = CHUNK * d_model // 128
    chunk_of = (within // CHUNK).reshape(tok_dev, top_count)
    row_of = (target * CHUNK + within % CHUNK).reshape(tok_dev, top_count)
    rows = jnp.arange(chunk_rows, dtype=jnp.int32)
    both = None
    for chunk in range(slot_count // CHUNK):
        hit = (row_of[None, :, :] == rows[:, None, None]) & (chunk_of == chunk)[None, :, :]
        dispatch = jnp.any(hit, axis=2).astype(jnp.bfloat16)
        outgoing = jnp.dot(dispatch, tokens, preferred_element_type=jnp.float32).astype(jnp.bfloat16)
        received = lax.all_to_all(
            outgoing.reshape(experts, lane_rows, 128),
            "expert",
            split_axis=0,
            concat_axis=0,
            tiled=True,
        )
        expert_out = expert_ffn(received.reshape(chunk_rows, d_model), w_in[0], w_out[0])
        answered = lax.all_to_all(
            expert_out.reshape(experts, lane_rows, 128),
            "expert",
            split_axis=0,
            concat_axis=0,
            tiled=True,
        ).reshape(chunk_rows, d_model)
        combine = jnp.sum(
            jnp.where(hit, gate_weights[None, :, :], jnp.float32(0.0)), axis=2
        ).T
        combine_hi = combine.astype(jnp.bfloat16)
        combine_lo = (combine - combine_hi.astype(jnp.float32)).astype(jnp.bfloat16)
        part = jnp.dot(
            jnp.concatenate([combine_hi, combine_lo], axis=0),
            answered,
            preferred_element_type=jnp.float32,
        )
        both = part if both is None else both + part
    weighted = both[:tok_dev] + both[tok_dev:]
    return weighted.astype(jnp.bfloat16)


def solution(mesh):
    in_specs = (
        P("expert", None),
        P("expert", None),
        P("expert", None),
        P(),
        P("expert", None, None, None, None),
        P("expert", None, None, None),
    )
    out_specs = P("expert", None)
    return jax.shard_map(local, mesh=mesh, in_specs=in_specs, out_specs=out_specs, check_vma=False)
```

time: 235 us -> 223 us (0.949)
  blocking collectives: 78.6 us -> 0 us
  starting transfers between devices: 5.63 us -> 37.5 us
  matrix products: 34.9 us -> 50.5 us
  local copies, waits for them, and re-layouts: 44.9 us -> 58 us
  waiting for transfers between devices: 66.1 us -> 72.2 us
    all_to_all x1 -> x0, blocking collectives: 78.6 us -> none  [local(): lax.all_to_all(outgoing.reshape(experts, lane_rows, 128), 'expert', split...]
    all_to_all x0 -> x3, waiting for transfers between devices: none -> 41.9 us  [local(): lax.all_to_all(outgoing.reshape(experts, lane_rows, 128), 'expert', split...]
    all_to_all x1 -> x3, waiting for transfers between devices: 66.1 us -> 30.3 us  [local(): lax.all_to_all(expert_out.reshape(experts, lane_rows, 128), 'expert', spl...]
    all_to_all x0 -> x3, starting transfers between devices: none -> 20.3 us  [local(): lax.all_to_all(outgoing.reshape(experts, lane_rows, 128), 'expert', split...]
    all_to_all x1 -> x3, starting transfers between devices: 5.63 us -> 17.2 us  [local(): lax.all_to_all(expert_out.reshape(experts, lane_rows, 128), 'expert', spl...]
    dot_general x1 -> x3, matrix products: 10.8 us -> 18.3 us  [expert_ffn(): jnp.einsum('rhu,hud->rd', hidden, second_weights, preferred_element_type=...]
    dot_general x1 -> x3, matrix products: 16.6 us -> 23.6 us  [expert_ffn(): jnp.einsum('rd,hdgu->rhgu', rows, first_weights, preferred_element_type=j...]
    unnamed x9 -> x19, local copies, waits for them, and re-layouts: 0.93 us -> 7.06 us
  transfers between devices with their start and end apart: 1 -> 6, of which waited for: 1 -> 6; matrix products, arithmetic and copies ran while one was open for 0% -> 42% of each run, Pallas kernels for 0% -> 0%
where the time goes in v2:
time: 223 us; the launch traced here: 222 us
  waiting for transfers between devices  72.2 us (32%)
  local copies, waits for them, and re-layouts  58 us (26%)
  matrix products  50.5 us (23%)
  starting transfers between devices  37.5 us (17%)
  other arithmetic  3.67 us (2%)
    all_to_all x3, waiting for transfers between devices, local(): lax.all_to_all(outgoing.reshape(experts, lane_rows, 128), 'expert', split...  41.9 us
    all_to_all x3, waiting for transfers between devices, local(): lax.all_to_all(expert_out.reshape(experts, lane_rows, 128), 'expert', spl...  30.3 us
    dot_general x3, matrix products, expert_ffn(): jnp.einsum('rd,hdgu->rhgu', rows, first_weights, preferred_element_type=j...  23.6 us
    all_to_all x3, starting transfers between devices, local(): lax.all_to_all(outgoing.reshape(experts, lane_rows, 128), 'expert', split...  20.3 us
    dot_general x3, matrix products, expert_ffn(): jnp.einsum('rhu,hud->rd', hidden, second_weights, preferred_element_type=...  18.3 us
    all_to_all x3, starting transfers between devices, local(): lax.all_to_all(expert_out.reshape(experts, lane_rows, 128), 'expert', spl...  17.2 us
    reshape x3, local copies, waits for them, and re-layouts, local(): received.reshape(chunk_rows, d_model)  13.5 us
    reshape x3, local copies, waits for them, and re-layouts, local(): expert_out.reshape(experts, lane_rows, 128)  12.6 us
  transfers between devices with their start and end apart: 6, of which 6 were waited for; matrix products, arithmetic and copies ran while one was open for 42% of the time, Pallas kernels for 0%

profile of v2, /device:TPU:1, one launch (start us, length us, event | category | flops | bytes accessed | tf_op | source)
XLA Modules:
  0.0 222.0 jit_solution(1676427944007589760)
XLA Ops:
  4.0 3.3 %reshape.115 = bf16[128,56,128]{2,1,0:T(8,128)(2,1)} reshape(bf16[256,3584]{1,0:T(8,128)(2,1)S(1)} %convolution_convert_fusion.2) | data formatting | bytes 3670016 | tf_op jit(solution)/shard_map/reshape | solution.py:45
  7.3 11.5 %all-to-all-start = ((bf16[128,56,128]{2,1,0:T(8,128)(2,1)}), bf16[128,56,128]{2,1,0:T(8,128)(2,1)S(1)}, u32[]{:S(2)}, u32[]{:S(2)}) async-start(bf16[128,56,128]{2,1,0:T(8,128)(2,1)} %reshape.115), calls=%async_computation | async-start | bytes 3670016 | tf_op jit(solution)/shard_map/all_to_all | solution.py:44
  20.7 4.7 %reshape.119 = bf16[128,56,128]{2,1,0:T(8,128)(2,1)} reshape(bf16[256,3584]{1,0:T(8,128)(2,1)} %convolution_convert_fusion.1) | data formatting | bytes 3670016 | tf_op jit(solution)/shard_map/reshape | solution.py:45
  25.4 21.0 %all-to-all-done = bf16[128,56,128]{2,1,0:T(8,128)(2,1)S(1)} async-done(((bf16[128,56,128]{2,1,0:T(8,128)(2,1)}), bf16[128,56,128]{2,1,0:T(8,128)(2,1)S(1)}, u32[]{:S(2)}, u32[]{:S(2)}) %all-to-all-start) | async-done | bytes 1835040 | tf_op jit(solution)/shard_map/all_to_all | solution.py:44
  47.7 4.4 %all-to-all-start.2 = ((bf16[128,56,128]{2,1,0:T(8,128)(2,1)}), bf16[128,56,128]{2,1,0:T(8,128)(2,1)S(1)}, u32[]{:S(2)}, u32[]{:S(2)}) async-start(bf16[128,56,128]{2,1,0:T(8,128)(2,1)} %reshape.119), calls=%async_computation.2 | async-start | bytes 3670016 | tf_op jit(solution)/shard_map/all_to_all | solution.py:44
  52.1 2.0 convolution_convert_fusion
  54.1 4.6 %reshape.123 = bf16[128,56,128]{2,1,0:T(8,128)(2,1)} reshape(bf16[256,3584]{1,0:T(8,128)(2,1)} %convolution_convert_fusion) | data formatting | bytes 3670016 | tf_op jit(solution)/shard_map/reshape | solution.py:45
  58.7 4.5 %reshape.127 = bf16[256,3584,1,1]{1,0,2,3:T(8,128)(2,1)} reshape(bf16[128,56,128]{2,1,0:T(8,128)(2,1)} %copy-done.5) | data formatting | bytes 3670016 | tf_op jit(solution)/shard_map/reshape | solution.py:51
  63.2 16.7 %all-to-all-done.2 = bf16[128,56,128]{2,1,0:T(8,128)(2,1)S(1)} async-done(((bf16[128,56,128]{2,1,0:T(8,128)(2,1)}), bf16[128,56,128]{2,1,0:T(8,128)(2,1)S(1)}, u32[]{:S(2)}, u32[]{:S(2)}) %all-to-all-start.2) | async-done | bytes 1835040 | tf_op jit(solution)/shard_map/all_to_all | solution.py:44
  81.1 4.4 %all-to-all-start.4 = ((bf16[128,56,128]{2,1,0:T(8,128)(2,1)}), bf16[128,56,128]{2,1,0:T(8,128)(2,1)S(1)}, u32[]{:S(2)}, u32[]{:S(2)}) async-start(bf16[128,56,128]{2,1,0:T(8,128)(2,1)} %reshape.123), calls=%async_computation.4 | async-start | bytes 3670016 | tf_op jit(solution)/shard_map/all_to_all | solution.py:44
  85.6 7.9 %fusion.4 = f32[256,2,2,512]{3,0,2,1:T(8,128)S(1)} fusion(bf16[2,3584,2,512]{3,2,1,0:T(2,128)(2,1)} %bitcast.91, bf16[256,3584,1,1]{1,0,2,3:T(8,128)(2,1)} %reshape.127), kind=kOutput, calls=%fused_computation.4 | convolution fusion | flops 3758096384 | bytes 18612224 | tf_op jit(solution)/shard_map/rd,hdgu->rhgu/dot_general | solution.py:11
  93.4 6.5 %fusion.27 = bf16[256,3584]{1,0:T(8,128)(2,1)} fusion(bf16[1,2,512,3584]{3,2,1,0:T(8,128)(2,1)} %param.11, f32[256,2,2,512]{3,0,2,1:T(8,128)S(1)} %fusion.4), kind=kOutput, calls=%fused_computation.17 | convolution fusion | flops 1881538560 | bytes 11272192 | tf_op jit(solution)/shard_map/rhu,hud->rd/dot_general | solution.py:15
  99.9 4.7 %reshape.117 = bf16[128,56,128]{2,1,0:T(8,128)(2,1)} reshape(bf16[256,3584]{1,0:T(8,128)(2,1)} %fusion.27) | data formatting | bytes 3670016 | tf_op jit(solution)/shard_map/reshape | solution.py:53
  104.6 4.5 %reshape.129 = bf16[256,3584,1,1]{1,0,2,3:T(8,128)(2,1)} reshape(bf16[128,56,128]{2,1,0:T(8,128)(2,1)} %copy-done.4) | data formatting | bytes 3670016 | tf_op jit(solution)/shard_map/reshape | solution.py:51
  109.1 4.2 %all-to-all-done.4 = bf16[128,56,128]{2,1,0:T(8,128)(2,1)S(1)} async-done(((bf16[128,56,128]{2,1,0:T(8,128)(2,1)}), bf16[128,56,128]{2,1,0:T(8,128)(2,1)S(1)}, u32[]{:S(2)}, u32[]{:S(2)}) %all-to-all-start.4) | async-done | bytes 1835040 | tf_op jit(solution)/shard_map/all_to_all | solution.py:44
  114.6 5.7 %all-to-all-start.1 = ((bf16[128,56,128]{2,1,0:T(8,128)(2,1)}), bf16[128,56,128]{2,1,0:T(8,128)(2,1)S(1)}, u32[]{:S(2)}, u32[]{:S(2)}) async-start(bf16[128,56,128]{2,1,0:T(8,128)(2,1)} %reshape.117), calls=%async_computation.1 | async-start | bytes 3670016 | tf_op jit(solution)/shard_map/all_to_all | solution.py:52
  120.3 7.9 %fusion.2 = f32[256,2,2,512]{3,0,2,1:T(8,128)S(1)} fusion(bf16[2,3584,2,512]{3,2,1,0:T(2,128)(2,1)} %bitcast.92, bf16[256,3584,1,1]{1,0,2,3:T(8,128)(2,1)} %reshape.129), kind=kOutput, calls=%fused_computation.2 | convolution fusion | flops 3758096384 | bytes 18612224 | tf_op jit(solution)/shard_map/rd,hdgu->rhgu/dot_general | solution.py:11
  128.2 6.5 %fusion.24 = bf16[256,3584]{1,0:T(8,128)(2,1)} fusion(bf16[1,2,512,3584]{3,2,1,0:T(8,128)(2,1)} %param.11, f32[256,2,2,512]{3,0,2,1:T(8,128)S(1)} %fusion.2), kind=kOutput, calls=%fused_computation.16 | convolution fusion | flops 1881538560 | bytes 11272192 | tf_op jit(solution)/shard_map/rhu,hud->rd/dot_general | solution.py:15
  134.7 4.6 %reshape.121 = bf16[128,56,128]{2,1,0:T(8,128)(2,1)} reshape(bf16[256,3584]{1,0:T(8,128)(2,1)} %fusion.24) | data formatting | bytes 3670016 | tf_op jit(solution)/shard_map/reshape | solution.py:53
  139.3 4.5 %reshape.131 = bf16[256,3584,1,1]{1,0,2,3:T(8,128)(2,1)} reshape(bf16[128,56,128]{2,1,0:T(8,128)(2,1)} %copy-done.3) | data formatting | bytes 3670016 | tf_op jit(solution)/shard_map/reshape | solution.py:51
  143.9 4.1 %all-to-all-done.1 = bf16[128,56,128]{2,1,0:T(8,128)(2,1)S(1)} async-done(((bf16[128,56,128]{2,1,0:T(8,128)(2,1)}), bf16[128,56,128]{2,1,0:T(8,128)(2,1)S(1)}, u32[]{:S(2)}, u32[]{:S(2)}) %all-to-all-start.1) | async-done | bytes 1835040 | tf_op jit(solution)/shard_map/all_to_all | solution.py:52
  149.2 6.1 %all-to-all-start.3 = ((bf16[128,56,128]{2,1,0:T(8,128)(2,1)}), bf16[128,56,128]{2,1,0:T(8,128)(2,1)}, u32[]{:S(2)}, u32[]{:S(2)}) async-start(bf16[128,56,128]{2,1,0:T(8,128)(2,1)} %reshape.121), calls=%async_computation.3 | async-start | bytes 3670016 | tf_op jit(solution)/shard_map/all_to_all | solution.py:52
  155.3 7.9 %fusion = f32[256,2,2,512]{3,0,2,1:T(8,128)S(1)} fusion(bf16[2,3584,2,512]{3,2,1,0:T(2,128)(2,1)} %bitcast.93, bf16[256,3584,1,1]{1,0,2,3:T(8,128)(2,1)} %reshape.131), kind=kOutput, calls=%fused_computation | convolution fusion | flops 3758096384 | bytes 18612224 | tf_op jit(solution)/shard_map/rd,hdgu->rhgu/dot_general | solution.py:11
  163.2 5.2 %fusion.21 = bf16[256,3584]{1,0:T(8,128)(2,1)S(1)} fusion(bf16[1,2,512,3584]{3,2,1,0:T(8,128)(2,1)} %param.11, f32[256,2,2,512]{3,0,2,1:T(8,128)S(1)} %fusion), kind=kOutput, calls=%fused_computation.15 | convolution fusion | flops 1881538560 | bytes 11272192 | tf_op jit(solution)/shard_map/rhu,hud->rd/dot_general | solution.py:15
  168.4 3.3 %reshape.125 = bf16[128,56,128]{2,1,0:T(8,128)(2,1)} reshape(bf16[256,3584]{1,0:T(8,128)(2,1)S(1)} %fusion.21) | data formatting | bytes 3670016 | tf_op jit(solution)/shard_map/reshape | solution.py:53
  171.7 11.0 %all-to-all-done.3 = bf16[128,56,128]{2,1,0:T(8,128)(2,1)} async-done(((bf16[128,56,128]{2,1,0:T(8,128)(2,1)}), bf16[128,56,128]{2,1,0:T(8,128)(2,1)}, u32[]{:S(2)}, u32[]{:S(2)}) %all-to-all-start.3) | async-done | bytes 1835040 | tf_op jit(solution)/shard_map/all_to_all | solution.py:52
  182.7 5.4 %all-to-all-start.5 = ((bf16[128,56,128]{2,1,0:T(8,128)(2,1)}), bf16[128,56,128]{2,1,0:T(8,128)(2,1)}, u32[]{:S(2)}, u32[]{:S(2)}) async-start(bf16[128,56,128]{2,1,0:T(8,128)(2,1)} %reshape.125), calls=%async_computation.5 | async-start | bytes 3670016 | tf_op jit(solution)/shard_map/all_to_all | solution.py:52
  189.1 3.6 %reshape.118 = bf16[256,3584]{1,0:T(8,128)(2,1)S(1)} reshape(bf16[128,56,128]{2,1,0:T(8,128)(2,1)} %copy-done.2) | data formatting | bytes 3670016 | tf_op jit(solution)/shard_map/reshape | solution.py:58
  192.7 4.5 %reshape.122 = bf16[256,3584]{1,0:T(8,128)(2,1)} reshape(bf16[128,56,128]{2,1,0:T(8,128)(2,1)} %all-to-all-done.3) | data formatting | bytes 3670016 | tf_op jit(solution)/shard_map/reshape | solution.py:58
  200.4 15.2 %all-to-all-done.5 = bf16[128,56,128]{2,1,0:T(8,128)(2,1)} async-done(((bf16[128,56,128]{2,1,0:T(8,128)(2,1)}), bf16[128,56,128]{2,1,0:T(8,128)(2,1)}, u32[]{:S(2)}, u32[]{:S(2)}) %all-to-all-start.5) | async-done | bytes 1835040 | tf_op jit(solution)/shard_map/all_to_all | solution.py:52
  215.6 3.6 %reshape.126 = bf16[256,3584]{1,0:T(8,128)(2,1)S(1)} reshape(bf16[128,56,128]{2,1,0:T(8,128)(2,1)} %all-to-all-done.5) | data formatting | bytes 3670016 | tf_op jit(solution)/shard_map/reshape | solution.py:58
  219.2 2.0 convolution_add_fusion
  (46 shorter events, 15.9 us)
Async XLA Ops:
  0.0 3.3 %copy-start = (bf16[64,3584]{1,0:T(8,128)(2,1)S(1)}, bf16[64,3584]{1,0:T(8,128)(2,1)}, u32[]{:S(2)}) copy-start(bf16[64,3584]{1,0:T(8,128)(2,1)} %param.6) | copy-start | bytes 1376260
  7.3 39.1 %all-to-all-start = ((bf16[128,56,128]{2,1,0:T(8,128)(2,1)}), bf16[128,56,128]{2,1,0:T(8,128)(2,1)S(1)}, u32[]{:S(2)}, u32[]{:S(2)}) async-start(bf16[128,56,128]{2,1,0:T(8,128)(2,1)} %reshape.115), calls=%async_computation | async-start | bytes 3670016 | tf_op jit(solution)/shard_map/all_to_all | solution.py:44
  46.4 1.3 copy-start.5
  47.7 32.2 %all-to-all-start.2 = ((bf16[128,56,128]{2,1,0:T(8,128)(2,1)}), bf16[128,56,128]{2,1,0:T(8,128)(2,1)S(1)}, u32[]{:S(2)}, u32[]{:S(2)}) async-start(bf16[128,56,128]{2,1,0:T(8,128)(2,1)} %reshape.119), calls=%async_computation.2 | async-start | bytes 3670016 | tf_op jit(solution)/shard_map/all_to_all | solution.py:44
  79.9 1.3 copy-start.4
  81.1 32.2 %all-to-all-start.4 = ((bf16[128,56,128]{2,1,0:T(8,128)(2,1)}), bf16[128,56,128]{2,1,0:T(8,128)(2,1)S(1)}, u32[]{:S(2)}, u32[]{:S(2)}) async-start(bf16[128,56,128]{2,1,0:T(8,128)(2,1)} %reshape.123), calls=%async_computation.4 | async-start | bytes 3670016 | tf_op jit(solution)/shard_map/all_to_all | solution.py:44
  113.3 1.3 copy-start.3
  114.6 33.4 %all-to-all-start.1 = ((bf16[128,56,128]{2,1,0:T(8,128)(2,1)}), bf16[128,56,128]{2,1,0:T(8,128)(2,1)S(1)}, u32[]{:S(2)}, u32[]{:S(2)}) async-start(bf16[128,56,128]{2,1,0:T(8,128)(2,1)} %reshape.117), calls=%async_computation.1 | async-start | bytes 3670016 | tf_op jit(solution)/shard_map/all_to_all | solution.py:52
  148.0 1.3 copy-start.2
  149.2 33.4 %all-to-all-start.3 = ((bf16[128,56,128]{2,1,0:T(8,128)(2,1)}), bf16[128,56,128]{2,1,0:T(8,128)(2,1)}, u32[]{:S(2)}, u32[]{:S(2)}) async-start(bf16[128,56,128]{2,1,0:T(8,128)(2,1)} %reshape.121), calls=%async_computation.3 | async-start | bytes 3670016 | tf_op jit(solution)/shard_map/all_to_all | solution.py:52
  171.7 16.4 %copy-start.7 = (f32[64,8]{0,1:T(8,128)S(1)}, f32[64,8]{0,1:T(8,128)}, u32[]{:S(2)}) copy-start(f32[64,8]{0,1:T(8,128)} %param.8) | copy-start | bytes 6148
  182.7 32.9 %all-to-all-start.5 = ((bf16[128,56,128]{2,1,0:T(8,128)(2,1)}), bf16[128,56,128]{2,1,0:T(8,128)(2,1)}, u32[]{:S(2)}, u32[]{:S(2)}) async-start(bf16[128,56,128]{2,1,0:T(8,128)(2,1)} %reshape.125), calls=%async_computation.5 | async-start | bytes 3670016 | tf_op jit(solution)/shard_map/all_to_all | solution.py:52
  197.2 1.5 copy-start.6
  219.2 2.9 %copy-start.1 = (bf16[64,3584]{1,0:T(8,128)(2,1)S(1)}, bf16[64,3584]{1,0:T(8,128)(2,1)}, u32[]{:S(2)}) copy-start(bf16[64,3584]{1,0:T(8,128)(2,1)} %param.6) | copy-start | bytes 1376260

commit v3 on v2

--- a/solution.py
+++ b/solution.py
@@ -5,6 +5,7 @@
 
 MOST = 6
 CHUNK = 2
+PIECES = 4
 
 
 def expert_ffn(rows, first_weights, second_weights):
@@ -32,17 +33,21 @@
     within = jnp.sum(jnp.cumsum(onehot, axis=0) * onehot, axis=1) - 1
     target = jnp.sum(onehot * holder[None, :], axis=1)
     chunk_rows = experts * CHUNK
-    lane_rows = CHUNK * d_model // 128
+    piece = d_model // PIECES
     chunk_of = (within // CHUNK).reshape(tok_dev, top_count)
     row_of = (target * CHUNK + within % CHUNK).reshape(tok_dev, top_count)
     rows = jnp.arange(chunk_rows, dtype=jnp.int32)
+    same_piece = jnp.eye(PIECES, dtype=jnp.bool_)
+    token_pieces = tokens.reshape(tok_dev * PIECES, piece)
     both = None
     for chunk in range(slot_count // CHUNK):
         hit = (row_of[None, :, :] == rows[:, None, None]) & (chunk_of == chunk)[None, :, :]
-        dispatch = jnp.any(hit, axis=2).astype(jnp.bfloat16)
-        outgoing = jnp.dot(dispatch, tokens, preferred_element_type=jnp.float32).astype(jnp.bfloat16)
+        taken = jnp.any(hit, axis=2)
+        dispatch = (taken[:, None, :, None] & same_piece[None, :, None, :]).astype(jnp.bfloat16)
+        dispatch = dispatch.reshape(chunk_rows * PIECES, tok_dev * PIECES)
+        outgoing = jnp.dot(dispatch, token_pieces, preferred_element_type=jnp.float32).astype(jnp.bfloat16)
         received = lax.all_to_all(
-            outgoing.reshape(experts, lane_rows, 128),
+            outgoing.reshape(experts, CHUNK * PIECES, piece),
             "expert",
             split_axis=0,
             concat_axis=0,
@@ -50,24 +55,25 @@
         )
         expert_out = expert_ffn(received.reshape(chunk_rows, d_model), w_in[0], w_out[0])
         answered = lax.all_to_all(
-            expert_out.reshape(experts, lane_rows, 128),
+            expert_out.reshape(experts, CHUNK * PIECES, piece),
             "expert",
             split_axis=0,
             concat_axis=0,
             tiled=True,
-        ).reshape(chunk_rows, d_model)
+        ).reshape(chunk_rows * PIECES, piece)
         combine = jnp.sum(
             jnp.where(hit, gate_weights[None, :, :], jnp.float32(0.0)), axis=2
         ).T
         combine_hi = combine.astype(jnp.bfloat16)
         combine_lo = (combine - combine_hi.astype(jnp.float32)).astype(jnp.bfloat16)
-        part = jnp.dot(
-            jnp.concatenate([combine_hi, combine_lo], axis=0),
-            answered,
-            preferred_element_type=jnp.float32,
-        )
+        stacked = jnp.concatenate([combine_hi, combine_lo], axis=0)
+        spread = jnp.where(
+            same_piece[None, :, None, :], stacked[:, None, :, None], jnp.bfloat16(0)
+        ).reshape(2 * tok_dev * PIECES, chunk_rows * PIECES)
+        part = jnp.dot(spread, answered, preferred_element_type=jnp.float32)
         both = part if both is None else both + part
-    weighted = both[:tok_dev] + both[tok_dev:]
+    half = tok_dev * PIECES
+    weighted = (both[:half] + both[half:]).reshape(tok_dev, d_model)
     return weighted.astype(jnp.bfloat16)
 
 

time: 223 us -> 501 us (2.25); the launches traced: 222 us -> 493 us
  local copies, waits for them, and re-layouts: 58 us -> 313 us
  waiting for transfers between devices: 72.2 us -> 21.8 us
  other arithmetic: 3.67 us -> 49.8 us
  starting transfers between devices: 37.5 us -> 47.7 us
  matrix products: 50.5 us -> 60.3 us
    select_n x0 -> x3, local copies, waits for them, and re-layouts: none -> 195 us  [local(): jnp.where(same_piece[None, :, None, :], stacked[:, None, :, None], jnp.bf...]
    and x0 -> x3, local copies, waits for them, and re-layouts: none -> 92.5 us  [local(): taken[:, None, :, None] & same_piece[None, :, None, :]]
    all_to_all x6, waiting for transfers between devices: 72.2 us -> 21.8 us  [the longest x3 14.8 us: local(): lax.all_to_all(expert_out.reshape(experts, CHUNK * PIECES, piece), 'exper...]
    select_n x0 -> x1, other arithmetic: none -> 31.8 us  [local(): jnp.where(same_piece[None, :, None, :], stacked[:, None, :, None], jnp.bf...]
    reshape x9 -> x4, local copies, waits for them, and re-layouts: 36.9 us -> 12 us  [the longest x3 11.7 us: local(): expert_out.reshape(experts, CHUNK * PIECES, piece)]
    and x0 -> x1, other arithmetic: none -> 15 us  [local(): taken[:, None, :, None] & same_piece[None, :, None, :]]
    all_to_all x6, starting transfers between devices: 37.5 us -> 47.7 us  [the longest x3 31.7 us: local(): lax.all_to_all(outgoing.reshape(experts, CHUNK * PIECES, piece), 'expert'...]
    dot_general x6, matrix products: 8.65 us -> 17.2 us  [the longest x3 11.3 us: local(): part = jnp.dot(spread, answered, preferred_element_type=jnp.float32)]
  transfers between devices with their start and end apart: 6 -> 6, of which waited for: 6 -> 3; matrix products, arithmetic and copies ran while one was open for 42% -> 74% of each run, Pallas kernels for 0% -> 0%
where the time goes in v3:
time: 501 us; the launch traced here: 493 us
  local copies, waits for them, and re-layouts  313 us (62%)
  matrix products  60.3 us (12%)
  other arithmetic  49.8 us (10%)
  starting transfers between devices  47.7 us (10%)
  waiting for transfers between devices  21.8 us (4%)
    select_n x3, local copies, waits for them, and re-layouts, local(): jnp.where(same_piece[None, :, None, :], stacked[:, None, :, None], jnp.bf...  195 us
    and x3, local copies, waits for them, and re-layouts, local(): taken[:, None, :, None] & same_piece[None, :, None, :]  92.5 us
    select_n x1, other arithmetic, local(): jnp.where(same_piece[None, :, None, :], stacked[:, None, :, None], jnp.bf...  31.8 us
    all_to_all x3, starting transfers between devices, local(): lax.all_to_all(outgoing.reshape(experts, CHUNK * PIECES, piece), 'expert'...  31.7 us
    dot_general x3, matrix products, expert_ffn(): jnp.einsum('rd,hdgu->rhgu', rows, first_weights, preferred_element_type=j...  23.6 us
    dot_general x3, matrix products, expert_ffn(): jnp.einsum('rhu,hud->rd', hidden, second_weights, preferred_element_type=...  19.5 us
    all_to_all x3, starting transfers between devices, local(): lax.all_to_all(expert_out.reshape(experts, CHUNK * PIECES, piece), 'exper...  15.9 us
    and x1, other arithmetic, local(): taken[:, None, :, None] & same_piece[None, :, None, :]  15 us
  transfers between devices with their start and end apart: 6, of which 3 were waited for; matrix products, arithmetic and copies ran while one was open for 74% of the time, Pallas kernels for 0%

profile of v3, /device:TPU:1, one launch (start us, length us, event | category | flops | bytes accessed | tf_op | source)
XLA Modules:
  0.0 493.4 jit_solution(8948017321253436170)
XLA Ops:
  3.7 15.0 %broadcast_and_fusion.2 = (pred[256,4,64,4]{3,2,1,0:T(32,128)(4,1)}, pred[256,4,64,4]{3,2,1,0:T(32,128)(4,1)}, pred[256,4,64,4]{3,2,1,0:T(32,128)(4,1)}) fusion(pred[4,4]{1,0:T(4,128)(4,1)S(1)} %iota_compare_fusion.5, pred[256,64]{1,0:T(8,128)(4,1)S(1)} %copy.24, pred[256,64]{1,0:T(8,128)(4,1)S(1)} %copy.26, pred[256,64]{1,0:T(8,128)(4,1)S(1)} %copy.28), kind=kLoop, calls=%fused_computation.5 | loop fusion | flops 786432 | bytes 835600 | tf_op jit(solution)/shard_map/and | solution.py:46
  18.7 30.9 %and.144 = pred[1024,256]{1,0:T(32,128)(4,1)S(1)} reshape(pred[256,4,64,4]{3,2,1,0:T(32,128)(4,1)} %get-tuple-element.24) | data formatting | bytes 524288 | tf_op jit(solution)/shard_map/and | solution.py:46
  51.9 11.5 %all-to-all-start.2 = ((bf16[128,8,896]{2,1,0:T(8,128)(2,1)}), bf16[128,8,896]{2,1,0:T(8,128)(2,1)S(1)}, u32[]{:S(2)}, u32[]{:S(2)}) async-start(bf16[128,8,896]{2,1,0:T(8,128)(2,1)} %convert_bitcast_fusion.1), calls=%async_computation.2 | async-start | bytes 3670016 | tf_op jit(solution)/shard_map/all_to_all | solution.py:49
  63.3 30.8 %and.149 = pred[1024,256]{1,0:T(32,128)(4,1)S(1)} reshape(pred[256,4,64,4]{3,2,1,0:T(32,128)(4,1)} %get-tuple-element.25) | data formatting | bytes 524288 | tf_op jit(solution)/shard_map/and | solution.py:46
  97.4 10.1 %all-to-all-start.4 = ((bf16[128,8,896]{2,1,0:T(8,128)(2,1)}), bf16[128,8,896]{2,1,0:T(8,128)(2,1)S(1)}, u32[]{:S(2)}, u32[]{:S(2)}) async-start(bf16[128,8,896]{2,1,0:T(8,128)(2,1)} %convert_bitcast_fusion), calls=%async_computation.4 | async-start | bytes 3670016 | tf_op jit(solution)/shard_map/all_to_all | solution.py:49
  107.6 30.8 %and.139 = pred[1024,256]{1,0:T(32,128)(4,1)S(1)} reshape(pred[256,4,64,4]{3,2,1,0:T(32,128)(4,1)} %get-tuple-element.23) | data formatting | bytes 524288 | tf_op jit(solution)/shard_map/and | solution.py:46
  141.3 3.9 reshape.226
  145.2 10.2 %all-to-all-start = ((bf16[128,8,896]{2,1,0:T(8,128)(2,1)}), bf16[128,8,896]{2,1,0:T(8,128)(2,1)}, u32[]{:S(2)}, u32[]{:S(2)}) async-start(bf16[128,8,896]{2,1,0:T(8,128)(2,1)} %convert_bitcast_fusion.2), calls=%async_computation | async-start | bytes 3670016 | tf_op jit(solution)/shard_map/all_to_all | solution.py:49
  155.4 7.9 %fusion.2 = f32[256,2,2,512]{3,0,2,1:T(8,128)S(1)} fusion(bf16[2,3584,2,512]{3,2,1,0:T(2,128)(2,1)} %bitcast.120, bf16[256,3584,1,1]{1,0,2,3:T(8,128)(2,1)} %reshape.226), kind=kOutput, calls=%fused_computation.8 | convolution fusion | flops 3758096384 | bytes 18612224 | tf_op jit(solution)/shard_map/rd,hdgu->rhgu/dot_general | solution.py:12
  163.2 6.5 %fusion.24 = bf16[256,3584]{1,0:T(8,128)(2,1)} fusion(bf16[1,2,512,3584]{3,2,1,0:T(8,128)(2,1)} %param.11, f32[256,2,2,512]{3,0,2,1:T(8,128)S(1)} %fusion.2), kind=kOutput, calls=%fused_computation.22 | convolution fusion | flops 1881538560 | bytes 11272192 | tf_op jit(solution)/shard_map/rhu,hud->rd/dot_general | solution.py:16
  169.8 3.9 reshape.218
  173.7 2.1 reshape.228
  175.7 7.0 %all-to-all-done = bf16[128,8,896]{2,1,0:T(8,128)(2,1)} async-done(((bf16[128,8,896]{2,1,0:T(8,128)(2,1)}), bf16[128,8,896]{2,1,0:T(8,128)(2,1)}, u32[]{:S(2)}, u32[]{:S(2)}) %all-to-all-start) | async-done | bytes 1835040 | tf_op jit(solution)/shard_map/all_to_all | solution.py:49
  182.7 4.7 all-to-all-start.3
  187.5 7.9 %fusion = f32[256,2,2,512]{3,0,2,1:T(8,128)S(1)} fusion(bf16[2,3584,2,512]{3,2,1,0:T(2,128)(2,1)} %bitcast.121, bf16[256,3584,1,1]{1,0,2,3:T(8,128)(2,1)} %reshape.228), kind=kOutput, calls=%fused_computation.6 | convolution fusion | flops 3758096384 | bytes 18612224 | tf_op jit(solution)/shard_map/rd,hdgu->rhgu/dot_general | solution.py:12
  195.3 6.5 %fusion.21 = bf16[256,3584]{1,0:T(8,128)(2,1)} fusion(bf16[1,2,512,3584]{3,2,1,0:T(8,128)(2,1)} %param.11, f32[256,2,2,512]{3,0,2,1:T(8,128)S(1)} %fusion), kind=kOutput, calls=%fused_computation.21 | convolution fusion | flops 1881538560 | bytes 11272192 | tf_op jit(solution)/shard_map/rhu,hud->rd/dot_general | solution.py:16
  201.8 3.9 reshape.222
  205.7 3.9 reshape.224
  209.7 5.5 %all-to-all-done.3 = bf16[128,8,896]{2,1,0:T(8,128)(2,1)S(1)} async-done(((bf16[128,8,896]{2,1,0:T(8,128)(2,1)}), bf16[128,8,896]{2,1,0:T(8,128)(2,1)S(1)}, u32[]{:S(2)}, u32[]{:S(2)}) %all-to-all-start.3) | async-done | bytes 1835040 | tf_op jit(solution)/shard_map/all_to_all | solution.py:57
  215.1 5.4 %all-to-all-start.5 = ((bf16[128,8,896]{2,1,0:T(8,128)(2,1)}), bf16[128,8,896]{2,1,0:T(8,128)(2,1)}, u32[]{:S(2)}, u32[]{:S(2)}) async-start(bf16[128,8,896]{2,1,0:T(8,128)(2,1)} %reshape.222), calls=%async_computation.5 | async-start | bytes 3670016 | tf_op jit(solution)/shard_map/all_to_all | solution.py:57
  220.5 7.9 %fusion.4 = f32[256,2,2,512]{3,0,2,1:T(8,128)S(1)} fusion(bf16[2,3584,2,512]{3,2,1,0:T(2,128)(2,1)} %bitcast.122, bf16[256,3584,1,1]{1,0,2,3:T(8,128)(2,1)} %reshape.224), kind=kOutput, calls=%fused_computation.10 | convolution fusion | flops 3758096384 | bytes 18612224 | tf_op jit(solution)/shard_map/rd,hdgu->rhgu/dot_general | solution.py:12
  228.4 6.5 %fusion.27 = bf16[256,3584]{1,0:T(8,128)(2,1)} fusion(bf16[1,2,512,3584]{3,2,1,0:T(8,128)(2,1)} %param.11, f32[256,2,2,512]{3,0,2,1:T(8,128)S(1)} %fusion.4), kind=kOutput, calls=%fused_computation.23 | convolution fusion | flops 1881538560 | bytes 11272192 | tf_op jit(solution)/shard_map/rhu,hud->rd/dot_general | solution.py:16
  234.9 3.9 reshape.214
  238.8 9.3 %all-to-all-done.5 = bf16[128,8,896]{2,1,0:T(8,128)(2,1)} async-done(((bf16[128,8,896]{2,1,0:T(8,128)(2,1)}), bf16[128,8,896]{2,1,0:T(8,128)(2,1)}, u32[]{:S(2)}, u32[]{:S(2)}) %all-to-all-start.5) | async-done | bytes 1835040 | tf_op jit(solution)/shard_map/all_to_all | solution.py:57
  248.0 5.8 %all-to-all-start.1 = ((bf16[128,8,896]{2,1,0:T(8,128)(2,1)}), bf16[128,8,896]{2,1,0:T(8,128)(2,1)}, u32[]{:S(2)}, u32[]{:S(2)}) async-start(bf16[128,8,896]{2,1,0:T(8,128)(2,1)} %reshape.214), calls=%async_computation.1 | async-start | bytes 3670016 | tf_op jit(solution)/shard_map/all_to_all | solution.py:57
  253.9 31.8 %broadcast_select_fusion.2 = (bf16[128,4,256,4]{3,2,1,0:T(8,128)(2,1)}, bf16[128,4,256,4]{3,2,1,0:T(8,128)(2,1)}, bf16[128,4,256,4]{3,2,1,0:T(8,128)(2,1)}) fusion(pred[4,4]{1,0:T(4,128)(4,1)S(1)} %iota_compare_fusion.5, bf16[128,256]{1,0:T(8,128)(2,1)S(1)} %pad_maximum_fusion, bf16[128,256]{1,0:T(8,128)(2,1)S(1)} %pad_maximum_fusion.1, ...), kind=kLoop, calls=%fused_computation.2 | loop fusion | flops 1572864 | bytes 3342352 | tf_op jit(solution)/shard_map/jit(_where)/select_n | solution.py:70
  285.7 65.2 %select_n.84 = bf16[512,1024]{1,0:T(8,128)(2,1)} reshape(bf16[128,4,256,4]{3,2,1,0:T(8,128)(2,1)} %get-tuple-element.27) | data formatting | bytes 2097152 | tf_op jit(solution)/shard_map/jit(_where)/select_n | solution.py:70
  350.9 65.2 %select_n.87 = bf16[512,1024]{1,0:T(8,128)(2,1)} reshape(bf16[128,4,256,4]{3,2,1,0:T(8,128)(2,1)} %get-tuple-element.28) | data formatting | bytes 2097152 | tf_op jit(solution)/shard_map/jit(_where)/select_n | solution.py:70
  416.1 64.4 %select_n.81 = bf16[512,1024]{1,0:T(8,128)(2,1)S(1)} reshape(bf16[128,4,256,4]{3,2,1,0:T(8,128)(2,1)} %get-tuple-element.26) | data formatting | bytes 2097152 | tf_op jit(solution)/shard_map/jit(_where)/select_n | solution.py:70
  480.5 3.8 fusion.33
  484.3 4.1 fusion.30
  488.5 3.3 add_add_fusion
  (51 shorter events, 13.2 us)
Async XLA Ops:
  18.7 30.9 %copy-start.2 = (bf16[64,3584]{1,0:T(8,128)(2,1)S(1)}, bf16[64,3584]{1,0:T(8,128)(2,1)}, u32[]{:S(2)}) copy-start(bf16[64,3584]{1,0:T(8,128)(2,1)} %param.6) | copy-start | bytes 1376260
  51.9 44.3 %all-to-all-start.2 = ((bf16[128,8,896]{2,1,0:T(8,128)(2,1)}), bf16[128,8,896]{2,1,0:T(8,128)(2,1)S(1)}, u32[]{:S(2)}, u32[]{:S(2)}) async-start(bf16[128,8,896]{2,1,0:T(8,128)(2,1)} %convert_bitcast_fusion.1), calls=%async_computation.2 | async-start | bytes 3670016 | tf_op jit(solution)/shard_map/all_to_all | solution.py:49
  96.2 11.3 %copy-start.3 = (f32[64,8]{0,1:T(8,128)S(1)}, f32[64,8]{0,1:T(8,128)}, u32[]{:S(2)}) copy-start(f32[64,8]{0,1:T(8,128)} %param.8) | copy-start | bytes 6148
  96.2 1.2 copy-start
  97.4 47.8 %all-to-all-start.4 = ((bf16[128,8,896]{2,1,0:T(8,128)(2,1)}), bf16[128,8,896]{2,1,0:T(8,128)(2,1)S(1)}, u32[]{:S(2)}, u32[]{:S(2)}) async-start(bf16[128,8,896]{2,1,0:T(8,128)(2,1)} %convert_bitcast_fusion), calls=%async_computation.4 | async-start | bytes 3670016 | tf_op jit(solution)/shard_map/all_to_all | solution.py:49
  145.2 37.5 %all-to-all-start = ((bf16[128,8,896]{2,1,0:T(8,128)(2,1)}), bf16[128,8,896]{2,1,0:T(8,128)(2,1)}, u32[]{:S(2)}, u32[]{:S(2)}) async-start(bf16[128,8,896]{2,1,0:T(8,128)(2,1)} %convert_bitcast_fusion.2), calls=%async_computation | async-start | bytes 3670016 | tf_op jit(solution)/shard_map/all_to_all | solution.py:49
  182.7 32.4 %all-to-all-start.3 = ((bf16[128,8,896]{2,1,0:T(8,128)(2,1)}), bf16[128,8,896]{2,1,0:T(8,128)(2,1)S(1)}, u32[]{:S(2)}, u32[]{:S(2)}) async-start(bf16[128,8,896]{2,1,0:T(8,128)(2,1)} %reshape.218), calls=%async_computation.3 | async-start | bytes 3670016 | tf_op jit(solution)/shard_map/all_to_all | solution.py:57
  215.1 32.9 %all-to-all-start.5 = ((bf16[128,8,896]{2,1,0:T(8,128)(2,1)}), bf16[128,8,896]{2,1,0:T(8,128)(2,1)}, u32[]{:S(2)}, u32[]{:S(2)}) async-start(bf16[128,8,896]{2,1,0:T(8,128)(2,1)} %reshape.222), calls=%async_computation.5 | async-start | bytes 3670016 | tf_op jit(solution)/shard_map/all_to_all | solution.py:57
  248.0 240.4 %all-to-all-start.1 = ((bf16[128,8,896]{2,1,0:T(8,128)(2,1)}), bf16[128,8,896]{2,1,0:T(8,128)(2,1)}, u32[]{:S(2)}, u32[]{:S(2)}) async-start(bf16[128,8,896]{2,1,0:T(8,128)(2,1)} %reshape.214), calls=%async_computation.1 | async-start | bytes 3670016 | tf_op jit(solution)/shard_map/all_to_all | solution.py:57
  480.5 3.8 copy-start.1
  484.3 4.1 copy-start.4

commit v4 on v3

--- a/solution.py
+++ b/solution.py
@@ -36,15 +36,26 @@
     piece = d_model // PIECES
     chunk_of = (within // CHUNK).reshape(tok_dev, top_count)
     row_of = (target * CHUNK + within % CHUNK).reshape(tok_dev, top_count)
-    rows = jnp.arange(chunk_rows, dtype=jnp.int32)
-    same_piece = jnp.eye(PIECES, dtype=jnp.bool_)
     token_pieces = tokens.reshape(tok_dev * PIECES, piece)
+    piece_rows = jnp.arange(tok_dev * PIECES, dtype=jnp.int32)
+    piece_cols = jnp.arange(chunk_rows * PIECES, dtype=jnp.int32)
+    same_piece = (piece_rows[:, None] % PIECES) == (piece_cols[None, :] % PIECES)
+    slot_col = piece_cols[None, :] // PIECES
+    chunk_rep = jnp.repeat(chunk_of, PIECES, axis=0)
+    row_rep = jnp.repeat(row_of, PIECES, axis=0)
+    gate_rep = jnp.repeat(gate_weights, PIECES, axis=0)
     both = None
     for chunk in range(slot_count // CHUNK):
-        hit = (row_of[None, :, :] == rows[:, None, None]) & (chunk_of == chunk)[None, :, :]
-        taken = jnp.any(hit, axis=2)
-        dispatch = (taken[:, None, :, None] & same_piece[None, :, None, :]).astype(jnp.bfloat16)
-        dispatch = dispatch.reshape(chunk_rows * PIECES, tok_dev * PIECES)
+        slot_id = jnp.where(chunk_rep == chunk, row_rep, -1)
+        taken = jnp.zeros((tok_dev * PIECES, chunk_rows * PIECES), jnp.bool_)
+        combine = jnp.zeros((tok_dev * PIECES, chunk_rows * PIECES), jnp.float32)
+        for k in range(top_count):
+            match = slot_id[:, k : k + 1] == slot_col
+            taken = taken | match
+            combine = combine + jnp.where(match, gate_rep[:, k : k + 1], jnp.float32(0.0))
+        taken = taken & same_piece
+        combine = jnp.where(same_piece, combine, jnp.float32(0.0))
+        dispatch = taken.T.astype(jnp.bfloat16)
         outgoing = jnp.dot(dispatch, token_pieces, preferred_element_type=jnp.float32).astype(jnp.bfloat16)
         received = lax.all_to_all(
             outgoing.reshape(experts, CHUNK * PIECES, piece),
@@ -61,16 +72,10 @@
             concat_axis=0,
             tiled=True,
         ).reshape(chunk_rows * PIECES, piece)
-        combine = jnp.sum(
-            jnp.where(hit, gate_weights[None, :, :], jnp.float32(0.0)), axis=2
-        ).T
         combine_hi = combine.astype(jnp.bfloat16)
         combine_lo = (combine - combine_hi.astype(jnp.float32)).astype(jnp.bfloat16)
         stacked = jnp.concatenate([combine_hi, combine_lo], axis=0)
-        spread = jnp.where(
-            same_piece[None, :, None, :], stacked[:, None, :, None], jnp.bfloat16(0)
-        ).reshape(2 * tok_dev * PIECES, chunk_rows * PIECES)
-        part = jnp.dot(spread, answered, preferred_element_type=jnp.float32)
+        part = jnp.dot(stacked, answered, preferred_element_type=jnp.float32)
         both = part if both is None else both + part
     half = tok_dev * PIECES
     weighted = (both[:half] + both[half:]).reshape(tok_dev, d_model)

time: 501 us -> 215 us (0.43); the launches traced: 493 us -> 214 us
  local copies, waits for them, and re-layouts: 313 us -> 27.2 us
  waiting for transfers between devices: 21.8 us -> 85.1 us
  other arithmetic: 49.8 us -> 4.33 us
  starting transfers between devices: 47.7 us -> 35.5 us
    select_n x3 -> x0, local copies, waits for them, and re-layouts: 195 us -> none  [local(): jnp.where(same_piece[None, :, None, :], stacked[:, None, :, None], jnp.bf...]
    and x3 -> x0, local copies, waits for them, and re-layouts: 92.5 us -> none  [local(): taken[:, None, :, None] & same_piece[None, :, None, :]]
    all_to_all x3, waiting for transfers between devices: 7.02 us -> 51.5 us  [local(): lax.all_to_all(outgoing.reshape(experts, CHUNK * PIECES, piece), 'expert'...]
    select_n x1 -> x3, other arithmetic: 31.8 us -> 0.12 us  [the longest x1 0.12 us: local(): slot_id = jnp.where(chunk_rep == chunk, row_rep, -1)]
    all_to_all x3, waiting for transfers between devices: 14.8 us -> 33.6 us  [local(): lax.all_to_all(expert_out.reshape(experts, CHUNK * PIECES, piece), 'exper...]
    and x1 -> x0, other arithmetic: 15 us -> none  [local(): taken[:, None, :, None] & same_piece[None, :, None, :]]
    all_to_all x3, starting transfers between devices: 31.7 us -> 21.3 us  [local(): lax.all_to_all(outgoing.reshape(experts, CHUNK * PIECES, piece), 'expert'...]
  transfers between devices with their start and end apart: 6 -> 6, of which waited for: 3 -> 6; matrix products, arithmetic and copies ran while one was open for 74% -> 38% of each run, Pallas kernels for 0% -> 0%
where the time goes in v4:
time: 215 us; the launch traced here: 214 us
  waiting for transfers between devices  85.1 us (40%)
  matrix products  62 us (29%)
  starting transfers between devices  35.5 us (17%)
  local copies, waits for them, and re-layouts  27.2 us (13%)
  other arithmetic  4.33 us (2%)
    all_to_all x3, waiting for transfers between devices, local(): lax.all_to_all(outgoing.reshape(experts, CHUNK * PIECES, piece), 'expert'...  51.5 us
    all_to_all x3, waiting for transfers between devices, local(): lax.all_to_all(expert_out.reshape(experts, CHUNK * PIECES, piece), 'exper...  33.6 us
    dot_general x3, matrix products, expert_ffn(): jnp.einsum('rd,hdgu->rhgu', rows, first_weights, preferred_element_type=j...  23.6 us
    all_to_all x3, starting transfers between devices, local(): lax.all_to_all(outgoing.reshape(experts, CHUNK * PIECES, piece), 'expert'...  21.3 us
    dot_general x3, matrix products, expert_ffn(): jnp.einsum('rhu,hud->rd', hidden, second_weights, preferred_element_type=...  19.6 us
    all_to_all x3, starting transfers between devices, local(): lax.all_to_all(expert_out.reshape(experts, CHUNK * PIECES, piece), 'exper...  14.2 us
    reshape x3, local copies, waits for them, and re-layouts, local(): expert_out.reshape(experts, CHUNK * PIECES, piece)  11.7 us
    dot_general x3, matrix products, local(): part = jnp.dot(stacked, answered, preferred_element_type=jnp.float32)  9.98 us
  transfers between devices with their start and end apart: 6, of which 6 were waited for; matrix products, arithmetic and copies ran while one was open for 38% of the time, Pallas kernels for 0%

profile of v4, /device:TPU:1, one launch (start us, length us, event | category | flops | bytes accessed | tf_op | source)
XLA Modules:
  0.0 214.5 jit_solution(3039586892857700286)
XLA Ops:
  1.0 1.3 reshape.158
  4.1 3.0 %convert_bitcast_fusion = bf16[128,8,896]{2,1,0:T(8,128)(2,1)} fusion(bf16[256,896]{1,0:T(8,128)(2,1)S(1)} %reshape.158, s32[1024]{0:T(1024)S(1)} %get-tuple-element.54, s32[1024]{0:T(1024)S(1)} %get-tuple-element.55, s32[256]{0:T(256)S(1)} %get-tuple-element.30, s32[256]{0:T(256)S(1)} %get-tuple-element.31, s32[256]{0:T(256)S(1)} %get-tuple-element.32, ...), kind=kOutput, calls=%fused_computation.33 | convolution fusion | flops 475136000 | bytes 2311168 | tf_op jit(solution)/shard_map/dot_general | solution.py:59
  7.1 11.5 %all-to-all-start.4 = ((bf16[128,8,896]{2,1,0:T(8,128)(2,1)}), bf16[128,8,896]{2,1,0:T(8,128)(2,1)S(1)}, u32[]{:S(2)}, u32[]{:S(2)}) async-start(bf16[128,8,896]{2,1,0:T(8,128)(2,1)} %convert_bitcast_fusion), calls=%async_computation.4 | async-start | bytes 3670016 | tf_op jit(solution)/shard_map/all_to_all | solution.py:60
  19.2 3.0 %convert_bitcast_fusion.1 = bf16[128,8,896]{2,1,0:T(8,128)(2,1)} fusion(bf16[256,896]{1,0:T(8,128)(2,1)S(1)} %reshape.158, s32[1024]{0:T(1024)S(1)} %get-tuple-element.54, s32[1024]{0:T(1024)S(1)} %get-tuple-element.55, s32[256]{0:T(256)S(1)} %get-tuple-element.14, s32[256]{0:T(256)S(1)} %get-tuple-element.15, s32[256]{0:T(256)S(1)} %get-tuple-element.16, ...), kind=kOutput, calls=%fused_computation.35 | convolution fusion | flops 475136000 | bytes 2311168 | tf_op jit(solution)/shard_map/dot_general | solution.py:59
  22.2 24.1 %all-to-all-done.4 = bf16[128,8,896]{2,1,0:T(8,128)(2,1)S(1)} async-done(((bf16[128,8,896]{2,1,0:T(8,128)(2,1)}), bf16[128,8,896]{2,1,0:T(8,128)(2,1)S(1)}, u32[]{:S(2)}, u32[]{:S(2)}) %all-to-all-start.4) | async-done | bytes 1835040 | tf_op jit(solution)/shard_map/all_to_all | solution.py:60
  46.3 5.4 %all-to-all-start.2 = ((bf16[128,8,896]{2,1,0:T(8,128)(2,1)}), bf16[128,8,896]{2,1,0:T(8,128)(2,1)}, u32[]{:S(2)}, u32[]{:S(2)}) async-start(bf16[128,8,896]{2,1,0:T(8,128)(2,1)} %convert_bitcast_fusion.1), calls=%async_computation.2 | async-start | bytes 3670016 | tf_op jit(solution)/shard_map/all_to_all | solution.py:60
  52.3 3.0 %convert_bitcast_fusion.2 = bf16[128,8,896]{2,1,0:T(8,128)(2,1)} fusion(bf16[256,896]{1,0:T(8,128)(2,1)S(1)} %reshape.158, s32[1024]{0:T(1024)S(1)} %get-tuple-element.54, s32[1024]{0:T(1024)S(1)} %get-tuple-element.55, s32[256]{0:T(256)S(1)} %get-tuple-element.6, s32[256]{0:T(256)S(1)} %get-tuple-element.7, s32[256]{0:T(256)S(1)} %get-tuple-element.8, ...), kind=kOutput, calls=%fused_computation.36 | convolution fusion | flops 475136000 | bytes 2311168 | tf_op jit(solution)/shard_map/dot_general | solution.py:59
  55.3 2.1 reshape.175
  57.3 21.8 %all-to-all-done.2 = bf16[128,8,896]{2,1,0:T(8,128)(2,1)} async-done(((bf16[128,8,896]{2,1,0:T(8,128)(2,1)}), bf16[128,8,896]{2,1,0:T(8,128)(2,1)}, u32[]{:S(2)}, u32[]{:S(2)}) %all-to-all-start.2) | async-done | bytes 1835040 | tf_op jit(solution)/shard_map/all_to_all | solution.py:60
  79.2 4.4 %all-to-all-start = ((bf16[128,8,896]{2,1,0:T(8,128)(2,1)}), bf16[128,8,896]{2,1,0:T(8,128)(2,1)S(1)}, u32[]{:S(2)}, u32[]{:S(2)}) async-start(bf16[128,8,896]{2,1,0:T(8,128)(2,1)} %convert_bitcast_fusion.2), calls=%async_computation | async-start | bytes 3670016 | tf_op jit(solution)/shard_map/all_to_all | solution.py:60
  83.6 7.9 %fusion = f32[256,2,2,512]{3,0,2,1:T(8,128)S(1)} fusion(bf16[2,3584,2,512]{3,2,1,0:T(2,128)(2,1)} %bitcast.92, bf16[256,3584,1,1]{1,0,2,3:T(8,128)(2,1)} %reshape.175), kind=kOutput, calls=%fused_computation | convolution fusion | flops 3758096384 | bytes 18612224 | tf_op jit(solution)/shard_map/rd,hdgu->rhgu/dot_general | solution.py:12
  91.5 6.5 %fusion.21 = bf16[256,3584]{1,0:T(8,128)(2,1)} fusion(bf16[1,2,512,3584]{3,2,1,0:T(8,128)(2,1)} %param.11, f32[256,2,2,512]{3,0,2,1:T(8,128)S(1)} %fusion), kind=kOutput, calls=%fused_computation.15 | convolution fusion | flops 1881538560 | bytes 11272192 | tf_op jit(solution)/shard_map/rhu,hud->rd/dot_general | solution.py:16
  98.0 3.9 %reshape.169 = bf16[128,8,896]{2,1,0:T(8,128)(2,1)} reshape(bf16[256,3584]{1,0:T(8,128)(2,1)} %fusion.21) | data formatting | bytes 3670016 | tf_op jit(solution)/shard_map/reshape | solution.py:69
  101.9 3.9 %reshape.173 = bf16[256,3584,1,1]{1,0,2,3:T(8,128)(2,1)} reshape(bf16[128,8,896]{2,1,0:T(8,128)(2,1)} %all-to-all-done.2) | data formatting | bytes 3670016 | tf_op jit(solution)/shard_map/reshape | solution.py:67
  105.8 5.6 %all-to-all-done = bf16[128,8,896]{2,1,0:T(8,128)(2,1)S(1)} async-done(((bf16[128,8,896]{2,1,0:T(8,128)(2,1)}), bf16[128,8,896]{2,1,0:T(8,128)(2,1)S(1)}, u32[]{:S(2)}, u32[]{:S(2)}) %all-to-all-start) | async-done | bytes 1835040 | tf_op jit(solution)/shard_map/all_to_all | solution.py:60
  111.4 5.4 %all-to-all-start.5 = ((bf16[128,8,896]{2,1,0:T(8,128)(2,1)}), bf16[128,8,896]{2,1,0:T(8,128)(2,1)}, u32[]{:S(2)}, u32[]{:S(2)}) async-start(bf16[128,8,896]{2,1,0:T(8,128)(2,1)} %reshape.169), calls=%async_computation.5 | async-start | bytes 3670016 | tf_op jit(solution)/shard_map/all_to_all | solution.py:68
  116.8 7.9 %fusion.2 = f32[256,2,2,512]{3,0,2,1:T(8,128)S(1)} fusion(bf16[2,3584,2,512]{3,2,1,0:T(2,128)(2,1)} %bitcast.93, bf16[256,3584,1,1]{1,0,2,3:T(8,128)(2,1)} %reshape.173), kind=kOutput, calls=%fused_computation.2 | convolution fusion | flops 3758096384 | bytes 18612224 | tf_op jit(solution)/shard_map/rd,hdgu->rhgu/dot_general | solution.py:12
  124.7 6.5 %fusion.24 = bf16[256,3584]{1,0:T(8,128)(2,1)} fusion(bf16[1,2,512,3584]{3,2,1,0:T(8,128)(2,1)} %param.11, f32[256,2,2,512]{3,0,2,1:T(8,128)S(1)} %fusion.2), kind=kOutput, calls=%fused_computation.16 | convolution fusion | flops 1881538560 | bytes 11272192 | tf_op jit(solution)/shard_map/rhu,hud->rd/dot_general | solution.py:16
  131.2 3.9 %reshape.165 = bf16[128,8,896]{2,1,0:T(8,128)(2,1)} reshape(bf16[256,3584]{1,0:T(8,128)(2,1)} %fusion.24) | data formatting | bytes 3670016 | tf_op jit(solution)/shard_map/reshape | solution.py:69
  135.1 2.1 reshape.171
  137.1 7.2 %all-to-all-done.5 = bf16[128,8,896]{2,1,0:T(8,128)(2,1)} async-done(((bf16[128,8,896]{2,1,0:T(8,128)(2,1)}), bf16[128,8,896]{2,1,0:T(8,128)(2,1)}, u32[]{:S(2)}, u32[]{:S(2)}) %all-to-all-start.5) | async-done | bytes 1835040 | tf_op jit(solution)/shard_map/all_to_all | solution.py:68
  144.3 4.4 %all-to-all-start.3 = ((bf16[128,8,896]{2,1,0:T(8,128)(2,1)}), bf16[128,8,896]{2,1,0:T(8,128)(2,1)S(1)}, u32[]{:S(2)}, u32[]{:S(2)}) async-start(bf16[128,8,896]{2,1,0:T(8,128)(2,1)} %reshape.165), calls=%async_computation.3 | async-start | bytes 3670016 | tf_op jit(solution)/shard_map/all_to_all | solution.py:68
  148.7 7.9 %fusion.4 = f32[256,2,2,512]{3,0,2,1:T(8,128)S(1)} fusion(bf16[2,3584,2,512]{3,2,1,0:T(2,128)(2,1)} %bitcast.94, bf16[256,3584,1,1]{1,0,2,3:T(8,128)(2,1)} %reshape.171), kind=kOutput, calls=%fused_computation.4 | convolution fusion | flops 3758096384 | bytes 18612224 | tf_op jit(solution)/shard_map/rd,hdgu->rhgu/dot_general | solution.py:12
  156.6 6.5 %fusion.27 = bf16[256,3584]{1,0:T(8,128)(2,1)} fusion(bf16[1,2,512,3584]{3,2,1,0:T(8,128)(2,1)} %param.11, f32[256,2,2,512]{3,0,2,1:T(8,128)S(1)} %fusion.4), kind=kOutput, calls=%fused_computation.17 | convolution fusion | flops 1881538560 | bytes 11272192 | tf_op jit(solution)/shard_map/rhu,hud->rd/dot_general | solution.py:16
  163.1 3.9 %reshape.161 = bf16[128,8,896]{2,1,0:T(8,128)(2,1)} reshape(bf16[256,3584]{1,0:T(8,128)(2,1)} %fusion.27) | data formatting | bytes 3670016 | tf_op jit(solution)/shard_map/reshape | solution.py:69
  167.0 9.5 %all-to-all-done.3 = bf16[128,8,896]{2,1,0:T(8,128)(2,1)S(1)} async-done(((bf16[128,8,896]{2,1,0:T(8,128)(2,1)}), bf16[128,8,896]{2,1,0:T(8,128)(2,1)S(1)}, u32[]{:S(2)}, u32[]{:S(2)}) %all-to-all-start.3) | async-done | bytes 1835040 | tf_op jit(solution)/shard_map/all_to_all | solution.py:68
  176.5 1.3 copy-done
  177.8 4.4 %all-to-all-start.1 = ((bf16[128,8,896]{2,1,0:T(8,128)(2,1)}), bf16[128,8,896]{2,1,0:T(8,128)(2,1)S(1)}, u32[]{:S(2)}, u32[]{:S(2)}) async-start(bf16[128,8,896]{2,1,0:T(8,128)(2,1)} %reshape.161), calls=%async_computation.1 | async-start | bytes 3670016 | tf_op jit(solution)/shard_map/all_to_all | solution.py:68
  186.4 4.1 %fusion.30 = f32[512,896]{1,0:T(8,128)} fusion(bf16[128,8,896]{2,1,0:T(8,128)(2,1)} %all-to-all-done.5, bf16[256,1024]{1,0:T(8,128)(2,1)S(1)} %get-tuple-element.45, bf16[256,1024]{1,0:T(8,128)(2,1)S(1)} %get-tuple-element.46), kind=kOutput, calls=%fused_computation.24 | convolution fusion | flops 941621248 | bytes 4718592 | tf_op jit(solution)/shard_map/dot_general | solution.py:78
  190.5 2.5 %fusion.33 = f32[512,896]{1,0:T(8,128)} fusion(bf16[128,8,896]{2,1,0:T(8,128)(2,1)S(1)} %copy-done.1, bf16[256,1024]{1,0:T(8,128)(2,1)S(1)} %get-tuple-element.43, bf16[256,1024]{1,0:T(8,128)(2,1)S(1)} %get-tuple-element.44), kind=kOutput, calls=%fused_computation.27 | convolution fusion | flops 941621248 | bytes 4718592 | tf_op jit(solution)/shard_map/dot_general | solution.py:78
  193.0 17.0 %all-to-all-done.1 = bf16[128,8,896]{2,1,0:T(8,128)(2,1)S(1)} async-done(((bf16[128,8,896]{2,1,0:T(8,128)(2,1)}), bf16[128,8,896]{2,1,0:T(8,128)(2,1)S(1)}, u32[]{:S(2)}, u32[]{:S(2)}) %all-to-all-start.1) | async-done | bytes 1835040 | tf_op jit(solution)/shard_map/all_to_all | solution.py:68
  210.0 3.3 %add_add_fusion = f32[512,896]{1,0:T(8,128)S(1)} fusion(f32[512,896]{1,0:T(8,128)} %fusion.30, f32[512,896]{1,0:T(8,128)} %fusion.33, bf16[128,8,896]{2,1,0:T(8,128)(2,1)S(1)} %all-to-all-done.1, bf16[256,1024]{1,0:T(8,128)(2,1)S(1)} %get-tuple-element.39, bf16[256,1024]{1,0:T(8,128)(2,1)S(1)} %get-tuple-element.40), kind=kOutput, calls=%fused_computation.34 | convolution fusion | flops 942538752 | bytes 8388608 | tf_op jit(solution)/shard_map/dot_general | solution.py:78
  (40 shorter events, 9.2 us)
Async XLA Ops:
  0.0 2.7 %copy-start.3 = (s32[128]{0:T(128)S(1)}, s32[128]{0:T(128)}, u32[]{:S(2)}) copy-start(s32[128]{0:T(128)} %param.9) | copy-start | bytes 1540
  7.1 39.1 %all-to-all-start.4 = ((bf16[128,8,896]{2,1,0:T(8,128)(2,1)}), bf16[128,8,896]{2,1,0:T(8,128)(2,1)S(1)}, u32[]{:S(2)}, u32[]{:S(2)}) async-start(bf16[128,8,896]{2,1,0:T(8,128)(2,1)} %convert_bitcast_fusion), calls=%async_computation.4 | async-start | bytes 3670016 | tf_op jit(solution)/shard_map/all_to_all | solution.py:60
  46.3 32.9 %all-to-all-start.2 = ((bf16[128,8,896]{2,1,0:T(8,128)(2,1)}), bf16[128,8,896]{2,1,0:T(8,128)(2,1)}, u32[]{:S(2)}, u32[]{:S(2)}) async-start(bf16[128,8,896]{2,1,0:T(8,128)(2,1)} %convert_bitcast_fusion.1), calls=%async_computation.2 | async-start | bytes 3670016 | tf_op jit(solution)/shard_map/all_to_all | solution.py:60
  79.2 32.2 %all-to-all-start = ((bf16[128,8,896]{2,1,0:T(8,128)(2,1)}), bf16[128,8,896]{2,1,0:T(8,128)(2,1)S(1)}, u32[]{:S(2)}, u32[]{:S(2)}) async-start(bf16[128,8,896]{2,1,0:T(8,128)(2,1)} %convert_bitcast_fusion.2), calls=%async_computation | async-start | bytes 3670016 | tf_op jit(solution)/shard_map/all_to_all | solution.py:60
  111.4 32.9 %all-to-all-start.5 = ((bf16[128,8,896]{2,1,0:T(8,128)(2,1)}), bf16[128,8,896]{2,1,0:T(8,128)(2,1)}, u32[]{:S(2)}, u32[]{:S(2)}) async-start(bf16[128,8,896]{2,1,0:T(8,128)(2,1)} %reshape.169), calls=%async_computation.5 | async-start | bytes 3670016 | tf_op jit(solution)/shard_map/all_to_all | solution.py:68
  144.3 32.2 %all-to-all-start.3 = ((bf16[128,8,896]{2,1,0:T(8,128)(2,1)}), bf16[128,8,896]{2,1,0:T(8,128)(2,1)S(1)}, u32[]{:S(2)}, u32[]{:S(2)}) async-start(bf16[128,8,896]{2,1,0:T(8,128)(2,1)} %reshape.165), calls=%async_computation.3 | async-start | bytes 3670016 | tf_op jit(solution)/shard_map/all_to_all | solution.py:68
  167.0 15.2 %copy-start.2 = (f32[64,8]{0,1:T(8,128)S(1)}, f32[64,8]{0,1:T(8,128)}, u32[]{:S(2)}) copy-start(f32[64,8]{0,1:T(8,128)} %param.8) | copy-start | bytes 6148
  176.5 1.3 copy-start
  177.8 32.2 %all-to-all-start.1 = ((bf16[128,8,896]{2,1,0:T(8,128)(2,1)}), bf16[128,8,896]{2,1,0:T(8,128)(2,1)S(1)}, u32[]{:S(2)}, u32[]{:S(2)}) async-start(bf16[128,8,896]{2,1,0:T(8,128)(2,1)} %reshape.161), calls=%async_computation.1 | async-start | bytes 3670016 | tf_op jit(solution)/shard_map/all_to_all | solution.py:68
  186.3 4.2 %copy-start.1 = (bf16[128,8,896]{2,1,0:T(8,128)(2,1)S(1)}, bf16[128,8,896]{2,1,0:T(8,128)(2,1)}, u32[]{:S(2)}) copy-start(bf16[128,8,896]{2,1,0:T(8,128)(2,1)} %copy-done) | copy-start | bytes 5505028

commit v5 on v4

--- a/solution.py
+++ b/solution.py
@@ -4,7 +4,7 @@
 from jax.sharding import PartitionSpec as P
 
 MOST = 6
-CHUNK = 2
+CHUNKS = (2, 4)
 PIECES = 4
 
 
@@ -23,8 +23,7 @@
     experts = lax.axis_size("expert")
     tok_dev, top_count = expert_ids.shape
     d_model = tokens.shape[1]
-    slot_count = MOST
-    capacity = experts * slot_count
+    assert sum(CHUNKS) == MOST
     expert_range = jnp.arange(experts, dtype=jnp.int32)
     placed = (host[:, None] == expert_range[None, :]).astype(jnp.int32)
     holder = jnp.sum(placed * expert_range[:, None], axis=0)
@@ -32,21 +31,22 @@
     onehot = (flat_experts[:, None] == expert_range[None, :]).astype(jnp.int32)
     within = jnp.sum(jnp.cumsum(onehot, axis=0) * onehot, axis=1) - 1
     target = jnp.sum(onehot * holder[None, :], axis=1)
-    chunk_rows = experts * CHUNK
     piece = d_model // PIECES
-    chunk_of = (within // CHUNK).reshape(tok_dev, top_count)
-    row_of = (target * CHUNK + within % CHUNK).reshape(tok_dev, top_count)
+    within_rep = jnp.repeat(within.reshape(tok_dev, top_count), PIECES, axis=0)
+    target_rep = jnp.repeat(target.reshape(tok_dev, top_count), PIECES, axis=0)
     token_pieces = tokens.reshape(tok_dev * PIECES, piece)
     piece_rows = jnp.arange(tok_dev * PIECES, dtype=jnp.int32)
-    piece_cols = jnp.arange(chunk_rows * PIECES, dtype=jnp.int32)
-    same_piece = (piece_rows[:, None] % PIECES) == (piece_cols[None, :] % PIECES)
-    slot_col = piece_cols[None, :] // PIECES
-    chunk_rep = jnp.repeat(chunk_of, PIECES, axis=0)
-    row_rep = jnp.repeat(row_of, PIECES, axis=0)
     gate_rep = jnp.repeat(gate_weights, PIECES, axis=0)
     both = None
-    for chunk in range(slot_count // CHUNK):
-        slot_id = jnp.where(chunk_rep == chunk, row_rep, -1)
+    first_slot = 0
+    for chunk_slots in CHUNKS:
+        chunk_rows = experts * chunk_slots
+        piece_cols = jnp.arange(chunk_rows * PIECES, dtype=jnp.int32)
+        same_piece = (piece_rows[:, None] % PIECES) == (piece_cols[None, :] % PIECES)
+        slot_col = piece_cols[None, :] // PIECES
+        inside = (within_rep >= first_slot) & (within_rep < first_slot + chunk_slots)
+        slot_id = jnp.where(inside, target_rep * chunk_slots + within_rep - first_slot, -1)
+        first_slot += chunk_slots
         taken = jnp.zeros((tok_dev * PIECES, chunk_rows * PIECES), jnp.bool_)
         combine = jnp.zeros((tok_dev * PIECES, chunk_rows * PIECES), jnp.float32)
         for k in range(top_count):
@@ -58,7 +58,7 @@
         dispatch = taken.T.astype(jnp.bfloat16)
         outgoing = jnp.dot(dispatch, token_pieces, preferred_element_type=jnp.float32).astype(jnp.bfloat16)
         received = lax.all_to_all(
-            outgoing.reshape(experts, CHUNK * PIECES, piece),
+            outgoing.reshape(experts, chunk_slots * PIECES, piece),
             "expert",
             split_axis=0,
             concat_axis=0,
@@ -66,7 +66,7 @@
         )
         expert_out = expert_ffn(received.reshape(chunk_rows, d_model), w_in[0], w_out[0])
         answered = lax.all_to_all(
-            expert_out.reshape(experts, CHUNK * PIECES, piece),
+            expert_out.reshape(experts, chunk_slots * PIECES, piece),
             "expert",
             split_axis=0,
             concat_axis=0,

time: 215 us -> 201 us (0.935)
  matrix products: 62 us -> 50.1 us
  waiting for transfers between devices: 85.1 us -> 90.7 us
  starting transfers between devices: 35.5 us -> 31.3 us
  local copies, waits for them, and re-layouts: 27.2 us -> 23.4 us
    dot_general x3 -> x2, matrix products: 19.6 us -> 13.8 us  [expert_ffn(): jnp.einsum('rhu,hud->rd', hidden, second_weights, preferred_element_type=...]
    all_to_all x6 -> x4, waiting for transfers between devices: 85.1 us -> 90.7 us  [the longest x2 47.6 us: local(): lax.all_to_all(expert_out.reshape(experts, chunk_slots * PIECES, piece),...]
    all_to_all x6 -> x4, starting transfers between devices: 35.5 us -> 31.3 us  [the longest x2 16.5 us: local(): lax.all_to_all(outgoing.reshape(experts, chunk_slots * PIECES, piece), 'e...]
    dot_general x3 -> x2, matrix products: 23.6 us -> 20.1 us  [expert_ffn(): jnp.einsum('rd,hdgu->rhgu', rows, first_weights, preferred_element_type=j...]
    reshape x3 -> x2, local copies, waits for them, and re-layouts: 11.7 us -> 8.82 us  [local(): expert_out.reshape(experts, chunk_slots * PIECES, piece)]
    dot_general x3 -> x2, matrix products: 9.98 us -> 8.38 us  [local(): part = jnp.dot(stacked, answered, preferred_element_type=jnp.float32)]
    dot_general x3 -> x2, matrix products: 8.94 us -> 7.85 us  [local(): jnp.dot(dispatch, token_pieces, preferred_element_type=jnp.float32)]
    reshape x3 -> x2, local copies, waits for them, and re-layouts: 8.02 us -> 8.83 us  [local(): received.reshape(chunk_rows, d_model)]
  transfers between devices with their start and end apart: 6 -> 4, of which waited for: 6 -> 3; matrix products, arithmetic and copies ran while one was open for 38% -> 33% of each run, Pallas kernels for 0% -> 0%
where the time goes in v5:
time: 201 us; the launch traced here: 200 us
  waiting for transfers between devices  90.7 us (45%)
  matrix products  50.1 us (25%)
  starting transfers between devices  31.3 us (16%)
  local copies, waits for them, and re-layouts  23.4 us (12%)
  other arithmetic  4.26 us (2%)
    all_to_all x2, waiting for transfers between devices, local(): lax.all_to_all(expert_out.reshape(experts, chunk_slots * PIECES, piece),...  47.6 us
    all_to_all x2, waiting for transfers between devices, local(): lax.all_to_all(outgoing.reshape(experts, chunk_slots * PIECES, piece), 'e...  43.1 us
    dot_general x2, matrix products, expert_ffn(): jnp.einsum('rd,hdgu->rhgu', rows, first_weights, preferred_element_type=j...  20.1 us
    all_to_all x2, starting transfers between devices, local(): lax.all_to_all(outgoing.reshape(experts, chunk_slots * PIECES, piece), 'e...  16.5 us
    all_to_all x2, starting transfers between devices, local(): lax.all_to_all(expert_out.reshape(experts, chunk_slots * PIECES, piece),...  14.8 us
    dot_general x2, matrix products, expert_ffn(): jnp.einsum('rhu,hud->rd', hidden, second_weights, preferred_element_type=...  13.8 us
    reshape x2, local copies, waits for them, and re-layouts, local(): received.reshape(chunk_rows, d_model)  8.83 us
    reshape x2, local copies, waits for them, and re-layouts, local(): expert_out.reshape(experts, chunk_slots * PIECES, piece)  8.82 us
  transfers between devices with their start and end apart: 4, of which 3 were waited for; matrix products, arithmetic and copies ran while one was open for 33% of the time, Pallas kernels for 0%

profile of v5, /device:TPU:1, one launch (start us, length us, event | category | flops | bytes accessed | tf_op | source)
XLA Modules:
  0.0 200.0 jit_solution(18188186005858302343)
XLA Ops:
  0.0 0.8 copy.27
  1.0 1.3 reshape.221
  2.3 0.1 copy.29
  2.4 0.2 fusion.76
  2.7 0.1 select_reduce_fusion.1
  2.8 0.3 fusion.75
  3.2 0.1 and.138
  3.4 0.6 slice_reduce_fusion.7
  4.0 4.8 %convolution_convert_fusion = bf16[2048,896]{1,0:T(8,128)(2,1)} fusion(bf16[256,896]{1,0:T(8,128)(2,1)S(1)} %reshape.221, s32[2048]{0:T(1024)S(1)} %get-tuple-element.39, s32[2048]{0:T(1024)S(1)} %get-tuple-element.40, s32[256]{0:T(256)S(1)} %get-tuple-element.22, s32[256]{0:T(256)S(1)} %get-tuple-element.23, s32[256]{0:T(256)S(1)} %get-tuple-element.24, ...), kind=kOutput, calls=%fused_computation.12 | convolution fusion | flops 950272000 | bytes 4154368 | tf_op jit(solution)/shard_map/dot_general | solution.py:59
  8.8 11.9 %all-to-all-start.2 = ((bf16[128,16,896]{2,1,0:T(8,128)(2,1)}), bf16[128,16,896]{2,1,0:T(8,128)(2,1)}, u32[]{:S(2)}, u32[]{:S(2)}) async-start(bf16[128,16,896]{2,1,0:T(8,128)(2,1)} %bitcast.59), calls=%async_computation.2 | async-start | bytes 7340032 | tf_op jit(solution)/shard_map/all_to_all | solution.py:60
  21.0 0.6 slice_reduce_fusion.23
  21.6 3.1 %convert_bitcast_fusion = bf16[128,8,896]{2,1,0:T(8,128)(2,1)} fusion(bf16[256,896]{1,0:T(8,128)(2,1)S(1)} %reshape.221, s32[1024]{0:T(1024)S(1)} %get-tuple-element.41, s32[1024]{0:T(1024)S(1)} %get-tuple-element.42, s32[256]{0:T(256)S(1)} %get-tuple-element.6, s32[256]{0:T(256)S(1)} %get-tuple-element.7, s32[256]{0:T(256)S(1)} %get-tuple-element.8, ...), kind=kOutput, calls=%fused_computation.47 | convolution fusion | flops 475136000 | bytes 2311168 | tf_op jit(solution)/shard_map/dot_general | solution.py:59
  24.6 43.1 %all-to-all-done.2 = bf16[128,16,896]{2,1,0:T(8,128)(2,1)} async-done(((bf16[128,16,896]{2,1,0:T(8,128)(2,1)}), bf16[128,16,896]{2,1,0:T(8,128)(2,1)}, u32[]{:S(2)}, u32[]{:S(2)}) %all-to-all-start.2) | async-done | bytes 3670048 | tf_op jit(solution)/shard_map/all_to_all | solution.py:60
  67.7 4.6 %all-to-all-start = ((bf16[128,8,896]{2,1,0:T(8,128)(2,1)}), bf16[128,8,896]{2,1,0:T(8,128)(2,1)S(1)}, u32[]{:S(2)}, u32[]{:S(2)}) async-start(bf16[128,8,896]{2,1,0:T(8,128)(2,1)} %convert_bitcast_fusion), calls=%async_computation | async-start | bytes 3670016 | tf_op jit(solution)/shard_map/all_to_all | solution.py:60
  72.3 6.7 %reshape.232 = bf16[512,3584,1,1]{1,0,2,3:T(8,128)(2,1)} reshape(bf16[128,16,896]{2,1,0:T(8,128)(2,1)} %all-to-all-done.2) | data formatting | bytes 7340032 | tf_op jit(solution)/shard_map/reshape | solution.py:67
  79.1 12.2 %fusion = f32[512,2,2,512]{3,0,2,1:T(8,128)S(1)} fusion(bf16[2,3584,2,512]{3,2,1,0:T(2,128)(2,1)} %bitcast.63, bf16[512,3584,1,1]{1,0,2,3:T(8,128)(2,1)} %reshape.232), kind=kOutput, calls=%fused_computation | convolution fusion | flops 7516192768 | bytes 22544384 | tf_op jit(solution)/shard_map/rd,hdgu->rhgu/dot_general | solution.py:12
  91.3 8.6 %bitcast_convert_fusion = bf16[512,3584]{1,0:T(8,128)(2,1)} fusion(bf16[1,2,512,3584]{3,2,1,0:T(8,128)(2,1)} %param.11, f32[512,2,2,512]{3,0,2,1:T(8,128)S(1)} %fusion), kind=kOutput, calls=%fused_computation.4 | convolution fusion | flops 3763077120 | bytes 15204352 | tf_op jit(solution)/shard_map/rhu,hud->rd/dot_general | solution.py:16
  99.9 6.7 %reshape.228 = bf16[128,16,896]{2,1,0:T(8,128)(2,1)} reshape(bf16[512,3584]{1,0:T(8,128)(2,1)} %bitcast_convert_fusion) | data formatting | bytes 7340032 | tf_op jit(solution)/shard_map/reshape | solution.py:69
  106.6 10.1 %all-to-all-start.3 = ((bf16[128,16,896]{2,1,0:T(8,128)(2,1)}), bf16[128,16,896]{2,1,0:T(8,128)(2,1)}, u32[]{:S(2)}, u32[]{:S(2)}) async-start(bf16[128,16,896]{2,1,0:T(8,128)(2,1)} %reshape.228), calls=%async_computation.3 | async-start | bytes 7340032 | tf_op jit(solution)/shard_map/all_to_all | solution.py:68
  116.8 2.1 %reshape.230 = bf16[256,3584,1,1]{1,0,2,3:T(8,128)(2,1)} reshape(bf16[128,8,896]{2,1,0:T(8,128)(2,1)S(1)} %all-to-all-done) | data formatting | bytes 3670016 | tf_op jit(solution)/shard_map/reshape | solution.py:67
  118.9 7.8 %fusion.2 = f32[256,2,2,512]{3,0,2,1:T(8,128)S(1)} fusion(bf16[2,3584,2,512]{3,2,1,0:T(2,128)(2,1)} %bitcast.64, bf16[256,3584,1,1]{1,0,2,3:T(8,128)(2,1)} %reshape.230), kind=kOutput, calls=%fused_computation.2 | convolution fusion | flops 3758096384 | bytes 18612224 | tf_op jit(solution)/shard_map/rd,hdgu->rhgu/dot_general | solution.py:12
  126.7 5.2 %fusion.13 = bf16[256,3584]{1,0:T(8,128)(2,1)S(1)} fusion(bf16[1,2,512,3584]{3,2,1,0:T(8,128)(2,1)} %param.11, f32[256,2,2,512]{3,0,2,1:T(8,128)S(1)} %fusion.2), kind=kOutput, calls=%fused_computation.10 | convolution fusion | flops 1881538560 | bytes 11272192 | tf_op jit(solution)/shard_map/rhu,hud->rd/dot_general | solution.py:16
  132.0 2.1 %reshape.224 = bf16[128,8,896]{2,1,0:T(8,128)(2,1)} reshape(bf16[256,3584]{1,0:T(8,128)(2,1)S(1)} %fusion.13) | data formatting | bytes 3670016 | tf_op jit(solution)/shard_map/reshape | solution.py:69
  134.1 29.7 %all-to-all-done.3 = bf16[128,16,896]{2,1,0:T(8,128)(2,1)} async-done(((bf16[128,16,896]{2,1,0:T(8,128)(2,1)}), bf16[128,16,896]{2,1,0:T(8,128)(2,1)}, u32[]{:S(2)}, u32[]{:S(2)}) %all-to-all-start.3) | async-done | bytes 3670048 | tf_op jit(solution)/shard_map/all_to_all | solution.py:68
  163.8 4.6 %all-to-all-start.1 = ((bf16[128,8,896]{2,1,0:T(8,128)(2,1)}), bf16[128,8,896]{2,1,0:T(8,128)(2,1)S(1)}, u32[]{:S(2)}, u32[]{:S(2)}) async-start(bf16[128,8,896]{2,1,0:T(8,128)(2,1)} %reshape.224), calls=%async_computation.1 | async-start | bytes 3670016 | tf_op jit(solution)/shard_map/all_to_all | solution.py:68
  168.6 0.6 slice_reduce_fusion.22
  169.2 1.1 subtract_convert_fusion.1
  170.3 2.3 %subtract_convert_fusion = (bf16[256,2048]{1,0:T(8,128)(2,1)S(1)}, bf16[256,2048]{1,0:T(8,128)(2,1)S(1)}) fusion(f32[256]{0:T(256)S(1)} %get-tuple-element.14, s32[256]{0:T(256)S(1)} %get-tuple-element.22, f32[256]{0:T(256)S(1)} %get-tuple-element.15, s32[256]{0:T(256)S(1)} %get-tuple-element.23, f32[256]{0:T(256)S(1)} %get-tuple-element.16, ...), kind=kLoop, calls=%fused_computation.43 | loop fusion | flops 15204352 | bytes 2130944 | tf_op jit(solution)/shard_map/convert_element_type | solution.py:76
  172.6 5.6 %fusion.25 = f32[512,896]{1,0:T(8,128)} fusion(bf16[2048,896]{1,0:T(8,128)(2,1)} %bitcast.17, bf16[256,2048]{1,0:T(8,128)(2,1)S(1)} %get-tuple-element.33, bf16[256,2048]{1,0:T(8,128)(2,1)S(1)} %get-tuple-element.34), kind=kOutput, calls=%fused_computation.39 | convolution fusion | flops 1883242496 | bytes 7602176 | tf_op jit(solution)/shard_map/dot_general | solution.py:78
  178.2 17.9 %all-to-all-done.1 = bf16[128,8,896]{2,1,0:T(8,128)(2,1)S(1)} async-done(((bf16[128,8,896]{2,1,0:T(8,128)(2,1)}), bf16[128,8,896]{2,1,0:T(8,128)(2,1)S(1)}, u32[]{:S(2)}, u32[]{:S(2)}) %all-to-all-start.1) | async-done | bytes 1835040 | tf_op jit(solution)/shard_map/all_to_all | solution.py:68
  196.1 2.8 %fusion.32 = f32[512,896]{1,0:T(8,128)S(1)} fusion(f32[512,896]{1,0:T(8,128)} %fusion.25, bf16[128,8,896]{2,1,0:T(8,128)(2,1)S(1)} %all-to-all-done.1, bf16[256,1024]{1,0:T(8,128)(2,1)S(1)} %get-tuple-element.31, bf16[256,1024]{1,0:T(8,128)(2,1)S(1)} %get-tuple-element.32), kind=kOutput, calls=%fused_computation.48 | convolution fusion | flops 942080000 | bytes 6553600 | tf_op jit(solution)/shard_map/dot_general | solution.py:78
  198.9 1.0 convert_element_type.72
  (26 shorter events, 0.9 us)
Async XLA Ops:
  0.0 2.7 %copy-start.1 = (s32[128]{0:T(128)S(1)}, s32[128]{0:T(128)}, u32[]{:S(2)}) copy-start(s32[128]{0:T(128)} %param.9) | copy-start | bytes 1540
  8.8 58.9 %all-to-all-start.2 = ((bf16[128,16,896]{2,1,0:T(8,128)(2,1)}), bf16[128,16,896]{2,1,0:T(8,128)(2,1)}, u32[]{:S(2)}, u32[]{:S(2)}) async-start(bf16[128,16,896]{2,1,0:T(8,128)(2,1)} %bitcast.59), calls=%async_computation.2 | async-start | bytes 7340032 | tf_op jit(solution)/shard_map/all_to_all | solution.py:60
  67.7 38.9 %all-to-all-start = ((bf16[128,8,896]{2,1,0:T(8,128)(2,1)}), bf16[128,8,896]{2,1,0:T(8,128)(2,1)S(1)}, u32[]{:S(2)}, u32[]{:S(2)}) async-start(bf16[128,8,896]{2,1,0:T(8,128)(2,1)} %convert_bitcast_fusion), calls=%async_computation | async-start | bytes 3670016 | tf_op jit(solution)/shard_map/all_to_all | solution.py:60
  106.6 57.2 %all-to-all-start.3 = ((bf16[128,16,896]{2,1,0:T(8,128)(2,1)}), bf16[128,16,896]{2,1,0:T(8,128)(2,1)}, u32[]{:S(2)}, u32[]{:S(2)}) async-start(bf16[128,16,896]{2,1,0:T(8,128)(2,1)} %reshape.228), calls=%async_computation.3 | async-start | bytes 7340032 | tf_op jit(solution)/shard_map/all_to_all | solution.py:68
  134.1 34.4 %copy-start = (f32[64,8]{0,1:T(8,128)S(1)}, f32[64,8]{0,1:T(8,128)}, u32[]{:S(2)}) copy-start(f32[64,8]{0,1:T(8,128)} %param.8) | copy-start | bytes 6148
  163.8 32.3 %all-to-all-start.1 = ((bf16[128,8,896]{2,1,0:T(8,128)(2,1)}), bf16[128,8,896]{2,1,0:T(8,128)(2,1)S(1)}, u32[]{:S(2)}, u32[]{:S(2)}) async-start(bf16[128,8,896]{2,1,0:T(8,128)(2,1)} %reshape.224), calls=%async_computation.1 | async-start | bytes 3670016 | tf_op jit(solution)/shard_map/all_to_all | solution.py:68

commit v6 on v5

v6 whole, which is shorter than its diff:
```python
import jax
import jax.numpy as jnp
from jax import lax
from jax.sharding import PartitionSpec as P

MOST = 6
CHUNKS = ((4, 2), (2, 4))


def expert_ffn(rows, first_weights, second_weights):
    projected = jnp.einsum(
        "rd,hdgu->rhgu", rows, first_weights, preferred_element_type=jnp.float32
    )
    hidden = (jax.nn.silu(projected[:, :, 0]) * projected[:, :, 1]).astype(jnp.bfloat16)
    output = jnp.einsum(
        "rhu,hud->rd", hidden, second_weights, preferred_element_type=jnp.float32
    )
    return output.astype(jnp.bfloat16)


def local(tokens, expert_ids, gate_weights, host, w_in, w_out):
    experts = lax.axis_size("expert")
    tok_dev, top_count = expert_ids.shape
    d_model = tokens.shape[1]
    assert sum(slots for slots, _ in CHUNKS) == MOST
    expert_range = jnp.arange(experts, dtype=jnp.int32)
    placed = (host[:, None] == expert_range[None, :]).astype(jnp.int32)
    holder = jnp.sum(placed * expert_range[:, None], axis=0)
    flat_experts = expert_ids.reshape(-1)
    onehot = (flat_experts[:, None] == expert_range[None, :]).astype(jnp.int32)
    within = jnp.sum(jnp.cumsum(onehot, axis=0) * onehot, axis=1) - 1
    target = jnp.sum(onehot * holder[None, :], axis=1)
    within_of = within.reshape(tok_dev, top_count)
    target_of = target.reshape(tok_dev, top_count)
    weighted = None
    first_slot = 0
    for chunk_slots, pieces in CHUNKS:
        piece = d_model // pieces
        chunk_rows = experts * chunk_slots
        within_rep = jnp.repeat(within_of, pieces, axis=0)
        target_rep = jnp.repeat(target_of, pieces, axis=0)
        gate_rep = jnp.repeat(gate_weights, pieces, axis=0)
        token_pieces = tokens.reshape(tok_dev * pieces, piece)
        piece_rows = jnp.arange(tok_dev * pieces, dtype=jnp.int32)
        piece_cols = jnp.arange(chunk_rows * pieces, dtype=jnp.int32)
        same_piece = (piece_rows[:, None] % pieces) == (piece_cols[None, :] % pieces)
        slot_col = piece_cols[None, :] // pieces
        inside = (within_rep >= first_slot) & (within_rep < first_slot + chunk_slots)
        slot_id = jnp.where(inside, target_rep * chunk_slots + within_rep - first_slot, -1)
        first_slot += chunk_slots
        taken = jnp.zeros((tok_dev * pieces, chunk_rows * pieces), jnp.bool_)
        combine = jnp.zeros((tok_dev * pieces, chunk_rows * pieces), jnp.float32)
        for k in range(top_count):
            match = slot_id[:, k : k + 1] == slot_col
            taken = taken | match
            combine = combine + jnp.where(match, gate_rep[:, k : k + 1], jnp.float32(0.0))
        taken = taken & same_piece
        combine = jnp.where(same_piece, combine, jnp.float32(0.0))
        dispatch = taken.T.astype(jnp.bfloat16)
        outgoing = jnp.dot(dispatch, token_pieces, preferred_element_type=jnp.float32).astype(jnp.bfloat16)
        received = lax.all_to_all(
            outgoing.reshape(experts, chunk_slots * pieces, piece),
            "expert",
            split_axis=0,
            concat_axis=0,
            tiled=True,
        )
        expert_out = expert_ffn(received.reshape(chunk_rows, d_model), w_in[0], w_out[0])
        answered = lax.all_to_all(
            expert_out.reshape(experts, chunk_slots * pieces, piece),
            "expert",
            split_axis=0,
            concat_axis=0,
            tiled=True,
        ).reshape(chunk_rows * pieces, piece)
        combine_hi = combine.astype(jnp.bfloat16)
        combine_lo = (combine - combine_hi.astype(jnp.float32)).astype(jnp.bfloat16)
        stacked = jnp.concatenate([combine_hi, combine_lo], axis=0)
        part = jnp.dot(stacked, answered, preferred_element_type=jnp.float32)
        half = tok_dev * pieces
        part = (part[:half] + part[half:]).reshape(tok_dev, d_model)
        weighted = part if weighted is None else weighted + part
    return weighted.astype(jnp.bfloat16)


def solution(mesh):
    in_specs = (
        P("expert", None),
        P("expert", None),
        P("expert", None),
        P(),
        P("expert", None, None, None, None),
        P("expert", None, None, None),
    )
    out_specs = P("expert", None)
    return jax.shard_map(local, mesh=mesh, in_specs=in_specs, out_specs=out_specs, check_vma=False)
```

time: 201 us -> 200 us (level)
  matrix products: 50.1 us -> 44.8 us
  waiting for transfers between devices: 90.7 us -> 95.9 us
    all_to_all x4, waiting for transfers between devices: 90.7 us -> 95.9 us  [the longest x2 53.2 us: local(): lax.all_to_all(outgoing.reshape(experts, chunk_slots * pieces, piece), 'e...]
    dot_general x2, matrix products: 8.38 us -> 4.4 us  [local(): part = jnp.dot(stacked, answered, preferred_element_type=jnp.float32)]
    reshape x3 -> x6, local copies, waits for them, and re-layouts: 10.1 us -> 10.4 us  [the longest x2 8.5 us: local(): expert_out.reshape(experts, chunk_slots * pieces, piece)]
  transfers between devices with their start and end apart: 4 -> 4, of which waited for: 3 -> 3; matrix products, arithmetic and copies ran while one was open for 33% -> 30% of each run, Pallas kernels for 0% -> 0%
where the time goes in v6:
time: 200 us; the launch traced here: 199 us
  waiting for transfers between devices  95.9 us (48%)
  matrix products  44.8 us (22%)
  starting transfers between devices  31.8 us (16%)
  local copies, waits for them, and re-layouts  22.4 us (11%)
  other arithmetic  4.16 us (2%)
    all_to_all x2, waiting for transfers between devices, local(): lax.all_to_all(outgoing.reshape(experts, chunk_slots * pieces, piece), 'e...  53.2 us
    all_to_all x2, waiting for transfers between devices, local(): lax.all_to_all(expert_out.reshape(experts, chunk_slots * pieces, piece),...  42.7 us
    dot_general x2, matrix products, expert_ffn(): jnp.einsum('rd,hdgu->rhgu', rows, first_weights, preferred_element_type=j...  20.1 us
    all_to_all x2, starting transfers between devices, local(): lax.all_to_all(outgoing.reshape(experts, chunk_slots * pieces, piece), 'e...  16.9 us
    all_to_all x2, starting transfers between devices, local(): lax.all_to_all(expert_out.reshape(experts, chunk_slots * pieces, piece),...  14.9 us
    dot_general x2, matrix products, expert_ffn(): jnp.einsum('rhu,hud->rd', hidden, second_weights, preferred_element_type=...  13.8 us
    reshape x2, local copies, waits for them, and re-layouts, local(): received.reshape(chunk_rows, d_model)  8.51 us
    reshape x2, local copies, waits for them, and re-layouts, local(): expert_out.reshape(experts, chunk_slots * pieces, piece)  8.5 us
  transfers between devices with their start and end apart: 4, of which 3 were waited for; matrix products, arithmetic and copies ran while one was open for 30% of the time, Pallas kernels for 0%

profile of v6, /device:TPU:1, one launch (start us, length us, event | category | flops | bytes accessed | tf_op | source)
XLA Modules:
  0.0 199.4 jit_solution(4554799486420046953)
XLA Ops:
  0.0 0.8 copy.27
  1.0 0.8 select_reduce_fusion.1
  1.8 0.2 fusion.63
  2.2 0.3 select_reduce_fusion
  2.5 1.3 reshape.250
  4.0 0.6 slice_reduce_fusion.15
  4.7 3.0 %convert_bitcast_fusion = bf16[128,8,896]{2,1,0:T(8,128)(2,1)} fusion(bf16[256,896]{1,0:T(8,128)(2,1)S(1)} %reshape.250, s32[1024]{0:T(1024)S(1)} %get-tuple-element.49, s32[1024]{0:T(1024)S(1)} %get-tuple-element.50, s32[256]{0:T(256)S(1)} %get-tuple-element.14, s32[256]{0:T(256)S(1)} %get-tuple-element.15, s32[256]{0:T(256)S(1)} %get-tuple-element.16, ...), kind=kOutput, calls=%fused_computation.21 | convolution fusion | flops 475136000 | bytes 2311168 | tf_op jit(solution)/shard_map/dot_general | solution.py:60
  7.6 11.5 %all-to-all-start.2 = ((bf16[128,8,896]{2,1,0:T(8,128)(2,1)}), bf16[128,8,896]{2,1,0:T(8,128)(2,1)S(1)}, u32[]{:S(2)}, u32[]{:S(2)}) async-start(bf16[128,8,896]{2,1,0:T(8,128)(2,1)} %convert_bitcast_fusion), calls=%async_computation.2 | async-start | bytes 3670016 | tf_op jit(solution)/shard_map/all_to_all | solution.py:61
  19.6 0.4 slice_reduce_fusion.31
  20.0 3.5 %fusion.19 = bf16[128,8,1792]{2,1,0:T(8,128)(2,1)} fusion(bf16[128,1792]{1,0:T(8,128)(2,1)S(1)} %reshape.243, s32[1024]{0:T(1024)S(1)} %get-tuple-element.47, s32[1024]{0:T(1024)S(1)} %get-tuple-element.48, s32[128]{0:T(128)S(1)} %get-tuple-element.30, s32[128]{0:T(128)S(1)} %get-tuple-element.31, s32[128]{0:T(128)S(1)} %get-tuple-element.32, ...), kind=kOutput, calls=%fused_computation.15 | convolution fusion | flops 473825280 | bytes 4141568 | tf_op jit(solution)/shard_map/dot_general | solution.py:60
  23.4 23.4 %all-to-all-done.2 = bf16[128,8,896]{2,1,0:T(8,128)(2,1)S(1)} async-done(((bf16[128,8,896]{2,1,0:T(8,128)(2,1)}), bf16[128,8,896]{2,1,0:T(8,128)(2,1)S(1)}, u32[]{:S(2)}, u32[]{:S(2)}) %all-to-all-start.2) | async-done | bytes 1835040 | tf_op jit(solution)/shard_map/all_to_all | solution.py:61
  46.8 5.4 %all-to-all-start = ((bf16[128,8,1792]{2,1,0:T(8,128)(2,1)}), bf16[128,8,1792]{2,1,0:T(8,128)(2,1)}, u32[]{:S(2)}, u32[]{:S(2)}) async-start(bf16[128,8,1792]{2,1,0:T(8,128)(2,1)} %fusion.19), calls=%async_computation | async-start | bytes 7340032 | tf_op jit(solution)/shard_map/all_to_all | solution.py:61
  52.2 2.1 %reshape.258 = bf16[256,3584,1,1]{1,0,2,3:T(8,128)(2,1)} reshape(bf16[128,8,896]{2,1,0:T(8,128)(2,1)S(1)} %all-to-all-done.2) | data formatting | bytes 3670016 | tf_op jit(solution)/shard_map/reshape | solution.py:68
  54.3 7.8 %fusion = f32[256,2,2,512]{3,0,2,1:T(8,128)S(1)} fusion(bf16[2,3584,2,512]{3,2,1,0:T(2,128)(2,1)} %bitcast.64, bf16[256,3584,1,1]{1,0,2,3:T(8,128)(2,1)} %reshape.258), kind=kOutput, calls=%fused_computation | convolution fusion | flops 3758096384 | bytes 18612224 | tf_op jit(solution)/shard_map/rd,hdgu->rhgu/dot_general | solution.py:11
  62.2 5.2 %fusion.13 = bf16[256,3584]{1,0:T(8,128)(2,1)S(1)} fusion(bf16[1,2,512,3584]{3,2,1,0:T(8,128)(2,1)} %param.11, f32[256,2,2,512]{3,0,2,1:T(8,128)S(1)} %fusion), kind=kOutput, calls=%fused_computation.10 | convolution fusion | flops 1881538560 | bytes 11272192 | tf_op jit(solution)/shard_map/rhu,hud->rd/dot_general | solution.py:15
  67.4 2.1 %reshape.253 = bf16[128,8,896]{2,1,0:T(8,128)(2,1)} reshape(bf16[256,3584]{1,0:T(8,128)(2,1)S(1)} %fusion.13) | data formatting | bytes 3670016 | tf_op jit(solution)/shard_map/reshape | solution.py:70
  69.5 29.9 %all-to-all-done = bf16[128,8,1792]{2,1,0:T(8,128)(2,1)} async-done(((bf16[128,8,1792]{2,1,0:T(8,128)(2,1)}), bf16[128,8,1792]{2,1,0:T(8,128)(2,1)}, u32[]{:S(2)}, u32[]{:S(2)}) %all-to-all-start) | async-done | bytes 3670048 | tf_op jit(solution)/shard_map/all_to_all | solution.py:61
  99.4 4.6 %all-to-all-start.3 = ((bf16[128,8,896]{2,1,0:T(8,128)(2,1)}), bf16[128,8,896]{2,1,0:T(8,128)(2,1)S(1)}, u32[]{:S(2)}, u32[]{:S(2)}) async-start(bf16[128,8,896]{2,1,0:T(8,128)(2,1)} %reshape.253), calls=%async_computation.3 | async-start | bytes 3670016 | tf_op jit(solution)/shard_map/all_to_all | solution.py:69
  104.0 6.4 %reshape.256 = bf16[512,3584,1,1]{1,0,2,3:T(8,128)(2,1)} reshape(bf16[128,8,1792]{2,1,0:T(8,128)(2,1)} %all-to-all-done) | data formatting | bytes 7340032 | tf_op jit(solution)/shard_map/reshape | solution.py:68
  110.4 12.2 %fusion.2 = f32[512,2,2,512]{3,0,2,1:T(8,128)S(1)} fusion(bf16[2,3584,2,512]{3,2,1,0:T(2,128)(2,1)} %bitcast.65, bf16[512,3584,1,1]{1,0,2,3:T(8,128)(2,1)} %reshape.256), kind=kOutput, calls=%fused_computation.2 | convolution fusion | flops 7516192768 | bytes 22544384 | tf_op jit(solution)/shard_map/rd,hdgu->rhgu/dot_general | solution.py:11
  122.7 8.6 %bitcast_convert_fusion = bf16[512,3584]{1,0:T(8,128)(2,1)} fusion(bf16[1,2,512,3584]{3,2,1,0:T(8,128)(2,1)} %param.11, f32[512,2,2,512]{3,0,2,1:T(8,128)S(1)} %fusion.2), kind=kOutput, calls=%fused_computation.4 | convolution fusion | flops 3763077120 | bytes 15204352 | tf_op jit(solution)/shard_map/rhu,hud->rd/dot_general | solution.py:15
  131.3 6.4 %reshape.246 = bf16[128,8,1792]{2,1,0:T(8,128)(2,1)} reshape(bf16[512,3584]{1,0:T(8,128)(2,1)} %bitcast_convert_fusion) | data formatting | bytes 7340032 | tf_op jit(solution)/shard_map/reshape | solution.py:70
  137.7 10.3 %all-to-all-start.1 = ((bf16[128,8,1792]{2,1,0:T(8,128)(2,1)}), bf16[128,8,1792]{2,1,0:T(8,128)(2,1)}, u32[]{:S(2)}, u32[]{:S(2)}) async-start(bf16[128,8,1792]{2,1,0:T(8,128)(2,1)} %reshape.246), calls=%async_computation.1 | async-start | bytes 7340032 | tf_op jit(solution)/shard_map/all_to_all | solution.py:69
  148.1 0.4 slice_reduce_fusion.30
  148.5 0.6 slice_reduce_fusion.14
  149.1 0.5 subtract_convert_fusion.1
  149.7 1.1 subtract_convert_fusion
  150.8 1.3 fusion.21
  152.3 42.7 %all-to-all-done.1 = bf16[128,8,1792]{2,1,0:T(8,128)(2,1)} async-done(((bf16[128,8,1792]{2,1,0:T(8,128)(2,1)}), bf16[128,8,1792]{2,1,0:T(8,128)(2,1)}, u32[]{:S(2)}, u32[]{:S(2)}) %all-to-all-start.1) | async-done | bytes 3670048 | tf_op jit(solution)/shard_map/all_to_all | solution.py:69
  195.0 3.1 %fusion.16 = f32[256,1792]{1,0:T(8,128)S(1)} fusion(bf16[128,8,1792]{2,1,0:T(8,128)(2,1)} %all-to-all-done.1, bf16[128,1024]{1,0:T(8,128)(2,1)S(1)} %get-tuple-element.41, bf16[128,1024]{1,0:T(8,128)(2,1)S(1)} %get-tuple-element.42), kind=kOutput, calls=%fused_computation.12 | convolution fusion | flops 940572672 | bytes 6029312 | tf_op jit(solution)/shard_map/dot_general | solution.py:79
  198.2 0.3 reshape.248
  198.5 0.9 add_convert_fusion
  (33 shorter events, 1.5 us)
Async XLA Ops:
  4.7 14.5 %copy-start = (bf16[64,3584]{1,0:T(8,128)(2,1)S(1)}, bf16[64,3584]{1,0:T(8,128)(2,1)}, u32[]{:S(2)}) copy-start(bf16[64,3584]{1,0:T(8,128)(2,1)} %param.6) | copy-start | bytes 1376260
  7.6 39.1 %all-to-all-start.2 = ((bf16[128,8,896]{2,1,0:T(8,128)(2,1)}), bf16[128,8,896]{2,1,0:T(8,128)(2,1)S(1)}, u32[]{:S(2)}, u32[]{:S(2)}) async-start(bf16[128,8,896]{2,1,0:T(8,128)(2,1)} %convert_bitcast_fusion), calls=%async_computation.2 | async-start | bytes 3670016 | tf_op jit(solution)/shard_map/all_to_all | solution.py:61
  46.8 52.6 %all-to-all-start = ((bf16[128,8,1792]{2,1,0:T(8,128)(2,1)}), bf16[128,8,1792]{2,1,0:T(8,128)(2,1)}, u32[]{:S(2)}, u32[]{:S(2)}) async-start(bf16[128,8,1792]{2,1,0:T(8,128)(2,1)} %fusion.19), calls=%async_computation | async-start | bytes 7340032 | tf_op jit(solution)/shard_map/all_to_all | solution.py:61
  99.4 38.3 %all-to-all-start.3 = ((bf16[128,8,896]{2,1,0:T(8,128)(2,1)}), bf16[128,8,896]{2,1,0:T(8,128)(2,1)S(1)}, u32[]{:S(2)}, u32[]{:S(2)}) async-start(bf16[128,8,896]{2,1,0:T(8,128)(2,1)} %reshape.253), calls=%async_computation.3 | async-start | bytes 3670016 | tf_op jit(solution)/shard_map/all_to_all | solution.py:69
  137.7 10.3 %copy-start.1 = (f32[64,8]{0,1:T(8,128)S(1)}, f32[64,8]{0,1:T(8,128)}, u32[]{:S(2)}) copy-start(f32[64,8]{0,1:T(8,128)} %param.8) | copy-start | bytes 6148
  137.7 57.3 %all-to-all-start.1 = ((bf16[128,8,1792]{2,1,0:T(8,128)(2,1)}), bf16[128,8,1792]{2,1,0:T(8,128)(2,1)}, u32[]{:S(2)}, u32[]{:S(2)}) async-start(bf16[128,8,1792]{2,1,0:T(8,128)(2,1)} %reshape.246), calls=%async_computation.1 | async-start | bytes 7340032 | tf_op jit(solution)/shard_map/all_to_all | solution.py:69

commit v7 on v6

--- a/solution.py
+++ b/solution.py
@@ -12,6 +12,7 @@
         "rd,hdgu->rhgu", rows, first_weights, preferred_element_type=jnp.float32
     )
     hidden = (jax.nn.silu(projected[:, :, 0]) * projected[:, :, 1]).astype(jnp.bfloat16)
+    hidden = lax.optimization_barrier(hidden)
     output = jnp.einsum(
         "rhu,hud->rd", hidden, second_weights, preferred_element_type=jnp.float32
     )

time: 200 us -> 201 us (level)
  no operation moved by 1% of the time
where the time goes in v7:
time: 201 us; the launch traced here: 200 us
  waiting for transfers between devices  95.6 us (48%)
  matrix products  44.7 us (22%)
  starting transfers between devices  31.8 us (16%)
  local copies, waits for them, and re-layouts  22.4 us (11%)
  other arithmetic  5.14 us (3%)
    all_to_all x2, waiting for transfers between devices, local(): lax.all_to_all(outgoing.reshape(experts, chunk_slots * pieces, piece), 'e...  53 us
    all_to_all x2, waiting for transfers between devices, local(): lax.all_to_all(expert_out.reshape(experts, chunk_slots * pieces, piece),...  42.7 us
    dot_general x2, matrix products, expert_ffn(): jnp.einsum('rd,hdgu->rhgu', rows, first_weights, preferred_element_type=j...  20.1 us
    all_to_all x2, starting transfers between devices, local(): lax.all_to_all(outgoing.reshape(experts, chunk_slots * pieces, piece), 'e...  16.9 us
    all_to_all x2, starting transfers between devices, local(): lax.all_to_all(expert_out.reshape(experts, chunk_slots * pieces, piece),...  14.9 us
    dot_general x2, matrix products, expert_ffn(): jnp.einsum('rhu,hud->rd', hidden, second_weights, preferred_element_type=...  13.8 us
    reshape x2, local copies, waits for them, and re-layouts, local(): received.reshape(chunk_rows, d_model)  8.51 us
    reshape x2, local copies, waits for them, and re-layouts, local(): expert_out.reshape(experts, chunk_slots * pieces, piece)  8.5 us
  transfers between devices with their start and end apart: 4, of which 3 were waited for; matrix products, arithmetic and copies ran while one was open for 30% of the time, Pallas kernels for 0%

profile of v7, /device:TPU:1, one launch (start us, length us, event | category | flops | bytes accessed | tf_op | source)
XLA Modules:
  0.0 200.0 jit_solution(6376873311110377069)
XLA Ops:
  0.0 0.8 copy.33
  1.0 0.8 select_reduce_fusion.1
  2.2 0.3 select_reduce_fusion
  2.5 1.3 reshape.248
  4.0 0.6 slice_reduce_fusion.15
  4.7 3.0 %convert_bitcast_fusion = bf16[128,8,896]{2,1,0:T(8,128)(2,1)} fusion(bf16[256,896]{1,0:T(8,128)(2,1)S(1)} %reshape.248, s32[1024]{0:T(1024)S(1)} %get-tuple-element.49, s32[1024]{0:T(1024)S(1)} %get-tuple-element.50, s32[256]{0:T(256)S(1)} %get-tuple-element.14, s32[256]{0:T(256)S(1)} %get-tuple-element.15, s32[256]{0:T(256)S(1)} %get-tuple-element.16, ...), kind=kOutput, calls=%fused_computation.23 | convolution fusion | flops 475136000 | bytes 2311168 | tf_op jit(solution)/shard_map/dot_general | solution.py:61
  7.6 11.5 %all-to-all-start.2 = ((bf16[128,8,896]{2,1,0:T(8,128)(2,1)}), bf16[128,8,896]{2,1,0:T(8,128)(2,1)S(1)}, u32[]{:S(2)}, u32[]{:S(2)}) async-start(bf16[128,8,896]{2,1,0:T(8,128)(2,1)} %convert_bitcast_fusion), calls=%async_computation.2 | async-start | bytes 3670016 | tf_op jit(solution)/shard_map/all_to_all | solution.py:62
  19.6 0.4 slice_reduce_fusion.31
  20.0 3.5 %fusion.19 = bf16[128,8,1792]{2,1,0:T(8,128)(2,1)} fusion(bf16[128,1792]{1,0:T(8,128)(2,1)S(1)} %reshape.241, s32[1024]{0:T(1024)S(1)} %get-tuple-element.47, s32[1024]{0:T(1024)S(1)} %get-tuple-element.48, s32[128]{0:T(128)S(1)} %get-tuple-element.30, s32[128]{0:T(128)S(1)} %get-tuple-element.31, s32[128]{0:T(128)S(1)} %get-tuple-element.32, ...), kind=kOutput, calls=%fused_computation.15 | convolution fusion | flops 473825280 | bytes 4141568 | tf_op jit(solution)/shard_map/dot_general | solution.py:61
  23.4 23.4 %all-to-all-done.2 = bf16[128,8,896]{2,1,0:T(8,128)(2,1)S(1)} async-done(((bf16[128,8,896]{2,1,0:T(8,128)(2,1)}), bf16[128,8,896]{2,1,0:T(8,128)(2,1)S(1)}, u32[]{:S(2)}, u32[]{:S(2)}) %all-to-all-start.2) | async-done | bytes 1835040 | tf_op jit(solution)/shard_map/all_to_all | solution.py:62
  46.8 5.4 %all-to-all-start = ((bf16[128,8,1792]{2,1,0:T(8,128)(2,1)}), bf16[128,8,1792]{2,1,0:T(8,128)(2,1)}, u32[]{:S(2)}, u32[]{:S(2)}) async-start(bf16[128,8,1792]{2,1,0:T(8,128)(2,1)} %fusion.19), calls=%async_computation | async-start | bytes 7340032 | tf_op jit(solution)/shard_map/all_to_all | solution.py:62
  52.2 2.1 %reshape.256 = bf16[256,3584,1,1]{1,0,2,3:T(8,128)(2,1)} reshape(bf16[128,8,896]{2,1,0:T(8,128)(2,1)S(1)} %all-to-all-done.2) | data formatting | bytes 3670016 | tf_op jit(solution)/shard_map/reshape | solution.py:69
  54.3 7.8 %fusion = f32[256,2,2,512]{3,0,2,1:T(8,128)S(1)} fusion(bf16[2,3584,2,512]{3,2,1,0:T(2,128)(2,1)} %bitcast.84, bf16[256,3584,1,1]{1,0,2,3:T(8,128)(2,1)} %reshape.256), kind=kOutput, calls=%fused_computation | convolution fusion | flops 3758096384 | bytes 18612224 | tf_op jit(solution)/shard_map/rd,hdgu->rhgu/dot_general | solution.py:11
  62.2 0.3 fusion.33
  62.5 5.2 %fusion.13 = bf16[256,3584]{1,0:T(8,128)(2,1)S(1)} fusion(bf16[256,2,512]{2,0,1:T(8,128)(2,1)S(1)} %fusion.33, bf16[1,2,512,3584]{3,2,1,0:T(8,128)(2,1)} %param.11), kind=kOutput, calls=%fused_computation.10 | convolution fusion | flops 1879965696 | bytes 9699328 | tf_op jit(solution)/shard_map/rhu,hud->rd/dot_general | solution.py:16
  67.7 2.1 %reshape.251 = bf16[128,8,896]{2,1,0:T(8,128)(2,1)} reshape(bf16[256,3584]{1,0:T(8,128)(2,1)S(1)} %fusion.13) | data formatting | bytes 3670016 | tf_op jit(solution)/shard_map/reshape | solution.py:71
  69.8 29.6 %all-to-all-done = bf16[128,8,1792]{2,1,0:T(8,128)(2,1)} async-done(((bf16[128,8,1792]{2,1,0:T(8,128)(2,1)}), bf16[128,8,1792]{2,1,0:T(8,128)(2,1)}, u32[]{:S(2)}, u32[]{:S(2)}) %all-to-all-start) | async-done | bytes 3670048 | tf_op jit(solution)/shard_map/all_to_all | solution.py:62
  99.4 4.6 %all-to-all-start.3 = ((bf16[128,8,896]{2,1,0:T(8,128)(2,1)}), bf16[128,8,896]{2,1,0:T(8,128)(2,1)S(1)}, u32[]{:S(2)}, u32[]{:S(2)}) async-start(bf16[128,8,896]{2,1,0:T(8,128)(2,1)} %reshape.251), calls=%async_computation.3 | async-start | bytes 3670016 | tf_op jit(solution)/shard_map/all_to_all | solution.py:70
  104.0 6.4 %reshape.254 = bf16[512,3584,1,1]{1,0,2,3:T(8,128)(2,1)} reshape(bf16[128,8,1792]{2,1,0:T(8,128)(2,1)} %all-to-all-done) | data formatting | bytes 7340032 | tf_op jit(solution)/shard_map/reshape | solution.py:69
  110.4 12.2 %fusion.2 = f32[512,2,2,512]{3,0,2,1:T(8,128)S(1)} fusion(bf16[2,3584,2,512]{3,2,1,0:T(2,128)(2,1)} %bitcast.85, bf16[512,3584,1,1]{1,0,2,3:T(8,128)(2,1)} %reshape.254), kind=kOutput, calls=%fused_computation.2 | convolution fusion | flops 7516192768 | bytes 22544384 | tf_op jit(solution)/shard_map/rd,hdgu->rhgu/dot_general | solution.py:11
  122.7 0.7 fusion.21
  123.4 8.6 %bitcast_convert_fusion = bf16[512,3584]{1,0:T(8,128)(2,1)} fusion(bf16[512,2,512]{2,0,1:T(8,128)(2,1)S(1)} %fusion.21, bf16[1,2,512,3584]{3,2,1,0:T(8,128)(2,1)} %param.11), kind=kOutput, calls=%fused_computation.4 | convolution fusion | flops 3759931392 | bytes 12058624 | tf_op jit(solution)/shard_map/rhu,hud->rd/dot_general | solution.py:16
  131.9 6.4 %reshape.244 = bf16[128,8,1792]{2,1,0:T(8,128)(2,1)} reshape(bf16[512,3584]{1,0:T(8,128)(2,1)} %bitcast_convert_fusion) | data formatting | bytes 7340032 | tf_op jit(solution)/shard_map/reshape | solution.py:71
  138.4 10.3 %all-to-all-start.1 = ((bf16[128,8,1792]{2,1,0:T(8,128)(2,1)}), bf16[128,8,1792]{2,1,0:T(8,128)(2,1)}, u32[]{:S(2)}, u32[]{:S(2)}) async-start(bf16[128,8,1792]{2,1,0:T(8,128)(2,1)} %reshape.244), calls=%async_computation.1 | async-start | bytes 7340032 | tf_op jit(solution)/shard_map/all_to_all | solution.py:70
  148.8 0.4 slice_reduce_fusion.30
  149.2 0.6 slice_reduce_fusion.14
  149.8 0.5 subtract_convert_fusion.1
  150.3 1.1 subtract_convert_fusion
  151.5 1.3 fusion.22
  153.0 42.7 %all-to-all-done.1 = bf16[128,8,1792]{2,1,0:T(8,128)(2,1)} async-done(((bf16[128,8,1792]{2,1,0:T(8,128)(2,1)}), bf16[128,8,1792]{2,1,0:T(8,128)(2,1)}, u32[]{:S(2)}, u32[]{:S(2)}) %all-to-all-start.1) | async-done | bytes 3670048 | tf_op jit(solution)/shard_map/all_to_all | solution.py:70
  195.7 3.1 %fusion.16 = f32[256,1792]{1,0:T(8,128)S(1)} fusion(bf16[128,8,1792]{2,1,0:T(8,128)(2,1)} %all-to-all-done.1, bf16[128,1024]{1,0:T(8,128)(2,1)S(1)} %get-tuple-element.41, bf16[128,1024]{1,0:T(8,128)(2,1)S(1)} %get-tuple-element.42), kind=kOutput, calls=%fused_computation.12 | convolution fusion | flops 940572672 | bytes 6029312 | tf_op jit(solution)/shard_map/dot_general | solution.py:80
  199.2 0.9 add_convert_fusion
  (35 shorter events, 2.0 us)
Async XLA Ops:
  4.7 14.5 %copy-start = (bf16[64,3584]{1,0:T(8,128)(2,1)S(1)}, bf16[64,3584]{1,0:T(8,128)(2,1)}, u32[]{:S(2)}) copy-start(bf16[64,3584]{1,0:T(8,128)(2,1)} %param.6) | copy-start | bytes 1376260
  7.6 39.1 %all-to-all-start.2 = ((bf16[128,8,896]{2,1,0:T(8,128)(2,1)}), bf16[128,8,896]{2,1,0:T(8,128)(2,1)S(1)}, u32[]{:S(2)}, u32[]{:S(2)}) async-start(bf16[128,8,896]{2,1,0:T(8,128)(2,1)} %convert_bitcast_fusion), calls=%async_computation.2 | async-start | bytes 3670016 | tf_op jit(solution)/shard_map/all_to_all | solution.py:62
  46.8 52.6 %all-to-all-start = ((bf16[128,8,1792]{2,1,0:T(8,128)(2,1)}), bf16[128,8,1792]{2,1,0:T(8,128)(2,1)}, u32[]{:S(2)}, u32[]{:S(2)}) async-start(bf16[128,8,1792]{2,1,0:T(8,128)(2,1)} %fusion.19), calls=%async_computation | async-start | bytes 7340032 | tf_op jit(solution)/shard_map/all_to_all | solution.py:62
  99.4 39.0 %all-to-all-start.3 = ((bf16[128,8,896]{2,1,0:T(8,128)(2,1)}), bf16[128,8,896]{2,1,0:T(8,128)(2,1)S(1)}, u32[]{:S(2)}, u32[]{:S(2)}) async-start(bf16[128,8,896]{2,1,0:T(8,128)(2,1)} %reshape.251), calls=%async_computation.3 | async-start | bytes 3670016 | tf_op jit(solution)/shard_map/all_to_all | solution.py:70
  138.4 10.3 %copy-start.1 = (f32[64,8]{0,1:T(8,128)S(1)}, f32[64,8]{0,1:T(8,128)}, u32[]{:S(2)}) copy-start(f32[64,8]{0,1:T(8,128)} %param.8) | copy-start | bytes 6148
  138.4 57.3 %all-to-all-start.1 = ((bf16[128,8,1792]{2,1,0:T(8,128)(2,1)}), bf16[128,8,1792]{2,1,0:T(8,128)(2,1)}, u32[]{:S(2)}, u32[]{:S(2)}) async-start(bf16[128,8,1792]{2,1,0:T(8,128)(2,1)} %reshape.244), calls=%async_computation.1 | async-start | bytes 7340032 | tf_op jit(solution)/shard_map/all_to_all | solution.py:70

commit v8 on v6

--- a/solution.py
+++ b/solution.py
@@ -12,8 +12,11 @@
         "rd,hdgu->rhgu", rows, first_weights, preferred_element_type=jnp.float32
     )
     hidden = (jax.nn.silu(projected[:, :, 0]) * projected[:, :, 1]).astype(jnp.bfloat16)
-    output = jnp.einsum(
-        "rhu,hud->rd", hidden, second_weights, preferred_element_type=jnp.float32
+    units = hidden.shape[1] * hidden.shape[2]
+    output = jnp.dot(
+        hidden.reshape(hidden.shape[0], units),
+        second_weights.reshape(units, second_weights.shape[2]),
+        preferred_element_type=jnp.float32,
     )
     return output.astype(jnp.bfloat16)
 

time: 200 us -> 202 us (1.010)
  other arithmetic: 4.16 us -> 7.35 us
    convert_element_type x0 -> x2, other arithmetic: none -> 3.2 us  [expert_ffn(): (jax.nn.silu(projected[:, :, 0]) * projected[:, :, 1]).astype(jnp.bfloat16)]
    dot_general x2, matrix products: 13.8 us -> 10.8 us  [expert_ffn(): jnp.dot(hidden.reshape(hidden.shape[0], units), second_weights.reshape(un...]
  transfers between devices with their start and end apart: 4 -> 4, of which waited for: 3 -> 3; matrix products, arithmetic and copies ran while one was open for 30% -> 31% of each run, Pallas kernels for 0% -> 0%
where the time goes in v8:
time: 202 us
  waiting for transfers between devices  93.9 us (46%)
  matrix products  44.7 us (22%)
  starting transfers between devices  32.7 us (16%)
  local copies, waits for them, and re-layouts  22.7 us (11%)
  other arithmetic  7.35 us (4%)
    all_to_all x2, waiting for transfers between devices, local(): lax.all_to_all(outgoing.reshape(experts, chunk_slots * pieces, piece), 'e...  52.7 us
    all_to_all x2, waiting for transfers between devices, local(): lax.all_to_all(expert_out.reshape(experts, chunk_slots * pieces, piece),...  41.2 us
    dot_general x2, matrix products, expert_ffn(): jnp.einsum('rd,hdgu->rhgu', rows, first_weights, preferred_element_type=j...  21.6 us
    all_to_all x2, starting transfers between devices, local(): lax.all_to_all(outgoing.reshape(experts, chunk_slots * pieces, piece), 'e...  16.9 us
    all_to_all x2, starting transfers between devices, local(): lax.all_to_all(expert_out.reshape(experts, chunk_slots * pieces, piece),...  15.7 us
    dot_general x2, matrix products, expert_ffn(): jnp.dot(hidden.reshape(hidden.shape[0], units), second_weights.reshape(un...  10.8 us
    reshape x2, local copies, waits for them, and re-layouts, local(): received.reshape(chunk_rows, d_model)  8.64 us
    reshape x2, local copies, waits for them, and re-layouts, local(): expert_out.reshape(experts, chunk_slots * pieces, piece)  8.45 us
  transfers between devices with their start and end apart: 4, of which 3 were waited for; matrix products, arithmetic and copies ran while one was open for 31% of the time, Pallas kernels for 0%

profile of v8, /device:TPU:1, one launch (start us, length us, event | category | flops | bytes accessed | tf_op | source)
XLA Modules:
  0.0 201.6 jit_solution(15943202246517713158)
XLA Ops:
  0.0 0.8 copy.29
  1.0 0.8 select_reduce_fusion.1
  2.2 0.3 select_reduce_fusion
  2.5 1.3 reshape.256
  4.0 0.6 slice_reduce_fusion.15
  4.7 3.0 %convert_bitcast_fusion = bf16[128,8,896]{2,1,0:T(8,128)(2,1)} fusion(bf16[256,896]{1,0:T(8,128)(2,1)S(1)} %reshape.256, s32[1024]{0:T(1024)S(1)} %get-tuple-element.49, s32[1024]{0:T(1024)S(1)} %get-tuple-element.50, s32[256]{0:T(256)S(1)} %get-tuple-element.14, s32[256]{0:T(256)S(1)} %get-tuple-element.15, s32[256]{0:T(256)S(1)} %get-tuple-element.16, ...), kind=kOutput, calls=%fused_computation.16 | convolution fusion | flops 475136000 | bytes 2311168 | tf_op jit(solution)/shard_map/dot_general | solution.py:63
  7.6 11.5 %all-to-all-start.2 = ((bf16[128,8,896]{2,1,0:T(8,128)(2,1)}), bf16[128,8,896]{2,1,0:T(8,128)(2,1)S(1)}, u32[]{:S(2)}, u32[]{:S(2)}) async-start(bf16[128,8,896]{2,1,0:T(8,128)(2,1)} %convert_bitcast_fusion), calls=%async_computation.2 | async-start | bytes 3670016 | tf_op jit(solution)/shard_map/all_to_all | solution.py:64
  19.6 0.4 slice_reduce_fusion.31
  20.0 3.5 %fusion.7 = bf16[128,8,1792]{2,1,0:T(8,128)(2,1)} fusion(bf16[128,1792]{1,0:T(8,128)(2,1)S(1)} %reshape.249, s32[1024]{0:T(1024)S(1)} %get-tuple-element.47, s32[1024]{0:T(1024)S(1)} %get-tuple-element.48, s32[128]{0:T(128)S(1)} %get-tuple-element.30, s32[128]{0:T(128)S(1)} %get-tuple-element.31, s32[128]{0:T(128)S(1)} %get-tuple-element.32, ...), kind=kOutput, calls=%fused_computation.10 | convolution fusion | flops 473825280 | bytes 4141568 | tf_op jit(solution)/shard_map/dot_general | solution.py:63
  23.4 23.4 %all-to-all-done.2 = bf16[128,8,896]{2,1,0:T(8,128)(2,1)S(1)} async-done(((bf16[128,8,896]{2,1,0:T(8,128)(2,1)}), bf16[128,8,896]{2,1,0:T(8,128)(2,1)S(1)}, u32[]{:S(2)}, u32[]{:S(2)}) %all-to-all-start.2) | async-done | bytes 1835040 | tf_op jit(solution)/shard_map/all_to_all | solution.py:64
  46.8 5.5 %all-to-all-start = ((bf16[128,8,1792]{2,1,0:T(8,128)(2,1)}), bf16[128,8,1792]{2,1,0:T(8,128)(2,1)}, u32[]{:S(2)}, u32[]{:S(2)}) async-start(bf16[128,8,1792]{2,1,0:T(8,128)(2,1)} %fusion.7), calls=%async_computation | async-start | bytes 7340032 | tf_op jit(solution)/shard_map/all_to_all | solution.py:64
  52.3 2.1 %reshape.263 = bf16[256,3584,1,1]{1,0,2,3:T(8,128)(2,1)} reshape(bf16[128,8,896]{2,1,0:T(8,128)(2,1)S(1)} %all-to-all-done.2) | data formatting | bytes 3670016 | tf_op jit(solution)/shard_map/reshape | solution.py:71
  54.4 7.9 %fusion.2 = f32[256,2,2,512]{3,0,2,1:T(8,128)S(1)} fusion(bf16[2,3584,2,512]{3,2,1,0:T(2,128)(2,1)} %bitcast.54, bf16[256,3584,1,1]{1,0,2,3:T(8,128)(2,1)} %reshape.263), kind=kOutput, calls=%fused_computation.2 | convolution fusion | flops 3758096384 | bytes 18612224 | tf_op jit(solution)/shard_map/rd,hdgu->rhgu/dot_general | solution.py:11
  62.3 0.3 fusion.19
  62.8 5.2 %convolution_convert_fusion.1 = bf16[256,3584]{1,0:T(8,128)(2,1)S(1)} fusion(bf16[256,1024]{0,1:T(8,128)(2,1)S(1)} %bitcast.49, bf16[1024,3584]{1,0:T(8,128)(2,1)} %bitcast.41), kind=kOutput, calls=%fused_computation.5 | convolution fusion | flops 1879965696 | bytes 9699328 | tf_op jit(solution)/shard_map/dot_general | solution.py:16
  68.0 2.0 %reshape.259 = bf16[128,8,896]{2,1,0:T(8,128)(2,1)} reshape(bf16[256,3584]{1,0:T(8,128)(2,1)S(1)} %convolution_convert_fusion.1) | data formatting | bytes 3670016 | tf_op jit(solution)/shard_map/reshape | solution.py:73
  70.1 29.3 %all-to-all-done = bf16[128,8,1792]{2,1,0:T(8,128)(2,1)} async-done(((bf16[128,8,1792]{2,1,0:T(8,128)(2,1)}), bf16[128,8,1792]{2,1,0:T(8,128)(2,1)}, u32[]{:S(2)}, u32[]{:S(2)}) %all-to-all-start) | async-done | bytes 3670048 | tf_op jit(solution)/shard_map/all_to_all | solution.py:64
  99.4 5.4 %all-to-all-start.3 = ((bf16[128,8,896]{2,1,0:T(8,128)(2,1)}), bf16[128,8,896]{2,1,0:T(8,128)(2,1)}, u32[]{:S(2)}, u32[]{:S(2)}) async-start(bf16[128,8,896]{2,1,0:T(8,128)(2,1)} %reshape.259), calls=%async_computation.3 | async-start | bytes 3670016 | tf_op jit(solution)/shard_map/all_to_all | solution.py:72
  104.8 6.5 %reshape.262 = bf16[512,3584,1,1]{1,0,2,3:T(8,128)(2,1)} reshape(bf16[128,8,1792]{2,1,0:T(8,128)(2,1)} %all-to-all-done) | data formatting | bytes 7340032 | tf_op jit(solution)/shard_map/reshape | solution.py:71
  111.4 13.6 %fusion = f32[512,2,2,512]{0,3,2,1:T(8,128)} fusion(bf16[2,3584,2,512]{3,2,1,0:T(2,128)(2,1)} %bitcast.55, bf16[512,3584,1,1]{1,0,2,3:T(8,128)(2,1)} %reshape.262), kind=kOutput, calls=%fused_computation | convolution fusion | flops 7516192768 | bytes 22544384 | tf_op jit(solution)/shard_map/rd,hdgu->rhgu/dot_general | solution.py:11
  125.0 2.9 %fusion.8 = bf16[512,2,1,512]{0,3,2,1:T(8,128)(2,1)S(1)} fusion(f32[512,2,2,512]{0,3,2,1:T(8,128)} %fusion), kind=kLoop, calls=%fused_computation.12 | loop fusion | flops 3145728 | bytes 5242880 | tf_op jit(solution)/shard_map/convert_element_type | solution.py:14
  127.9 5.6 %convolution_convert_fusion = bf16[512,3584]{1,0:T(8,128)(2,1)} fusion(bf16[512,1024]{0,1:T(8,128)(2,1)S(1)} %bitcast.51, bf16[1024,3584]{1,0:T(8,128)(2,1)S(1)} %bitcast.44), kind=kOutput, calls=%fused_computation.4 | convolution fusion | flops 3759931392 | bytes 12058624 | tf_op jit(solution)/shard_map/dot_general | solution.py:16
  133.5 6.4 %reshape.252 = bf16[128,8,1792]{2,1,0:T(8,128)(2,1)} reshape(bf16[512,3584]{1,0:T(8,128)(2,1)} %convolution_convert_fusion) | data formatting | bytes 7340032 | tf_op jit(solution)/shard_map/reshape | solution.py:73
  139.9 10.3 %all-to-all-start.1 = ((bf16[128,8,1792]{2,1,0:T(8,128)(2,1)}), bf16[128,8,1792]{2,1,0:T(8,128)(2,1)}, u32[]{:S(2)}, u32[]{:S(2)}) async-start(bf16[128,8,1792]{2,1,0:T(8,128)(2,1)} %reshape.252), calls=%async_computation.1 | async-start | bytes 7340032 | tf_op jit(solution)/shard_map/all_to_all | solution.py:72
  150.4 0.4 slice_reduce_fusion.30
  150.8 0.6 slice_reduce_fusion.14
  151.4 0.5 subtract_convert_fusion.1
  151.9 1.1 subtract_convert_fusion
  153.1 2.8 %fusion.9 = f32[512,896]{1,0:T(8,128)S(1)} fusion(bf16[128,8,896]{2,1,0:T(8,128)(2,1)} %all-to-all-done.3, bf16[256,1024]{1,0:T(8,128)(2,1)S(1)} %get-tuple-element.39, bf16[256,1024]{1,0:T(8,128)(2,1)S(1)} %get-tuple-element.40), kind=kOutput, calls=%fused_computation.13 | convolution fusion | flops 941621248 | bytes 4718592 | tf_op jit(solution)/shard_map/dot_general | solution.py:82
  156.1 41.2 %all-to-all-done.1 = bf16[128,8,1792]{2,1,0:T(8,128)(2,1)} async-done(((bf16[128,8,1792]{2,1,0:T(8,128)(2,1)}), bf16[128,8,1792]{2,1,0:T(8,128)(2,1)}, u32[]{:S(2)}, u32[]{:S(2)}) %all-to-all-start.1) | async-done | bytes 3670048 | tf_op jit(solution)/shard_map/all_to_all | solution.py:72
  197.2 3.1 %fusion.4 = f32[256,1792]{1,0:T(8,128)S(1)} fusion(bf16[128,8,1792]{2,1,0:T(8,128)(2,1)} %all-to-all-done.1, bf16[128,1024]{1,0:T(8,128)(2,1)S(1)} %get-tuple-element.41, bf16[128,1024]{1,0:T(8,128)(2,1)S(1)} %get-tuple-element.42), kind=kOutput, calls=%fused_computation.7 | convolution fusion | flops 940572672 | bytes 6029312 | tf_op jit(solution)/shard_map/dot_general | solution.py:82
  200.8 0.9 add_convert_fusion
  (41 shorter events, 2.2 us)
Async XLA Ops:
  4.7 14.5 %copy-start = (bf16[64,3584]{1,0:T(8,128)(2,1)S(1)}, bf16[64,3584]{1,0:T(8,128)(2,1)}, u32[]{:S(2)}) copy-start(bf16[64,3584]{1,0:T(8,128)(2,1)} %param.6) | copy-start | bytes 1376260
  7.6 39.1 %all-to-all-start.2 = ((bf16[128,8,896]{2,1,0:T(8,128)(2,1)}), bf16[128,8,896]{2,1,0:T(8,128)(2,1)S(1)}, u32[]{:S(2)}, u32[]{:S(2)}) async-start(bf16[128,8,896]{2,1,0:T(8,128)(2,1)} %convert_bitcast_fusion), calls=%async_computation.2 | async-start | bytes 3670016 | tf_op jit(solution)/shard_map/all_to_all | solution.py:64
  46.8 52.6 %all-to-all-start = ((bf16[128,8,1792]{2,1,0:T(8,128)(2,1)}), bf16[128,8,1792]{2,1,0:T(8,128)(2,1)}, u32[]{:S(2)}, u32[]{:S(2)}) async-start(bf16[128,8,1792]{2,1,0:T(8,128)(2,1)} %fusion.7), calls=%async_computation | async-start | bytes 7340032 | tf_op jit(solution)/shard_map/all_to_all | solution.py:64
  99.4 40.5 %all-to-all-start.3 = ((bf16[128,8,896]{2,1,0:T(8,128)(2,1)}), bf16[128,8,896]{2,1,0:T(8,128)(2,1)}, u32[]{:S(2)}, u32[]{:S(2)}) async-start(bf16[128,8,896]{2,1,0:T(8,128)(2,1)} %reshape.259), calls=%async_computation.3 | async-start | bytes 3670016 | tf_op jit(solution)/shard_map/all_to_all | solution.py:72
  104.8 23.1 %slice-start = ((s8[7340032]{0:T(1024)(128)(4,1)}), s8[3145728]{0:T(1024)(128)(4,1)S(1)}, s32[]{:S(2)}) async-start(s8[7340032]{0:T(1024)(128)(4,1)} %bitcast.42), calls=%async_computation.4 | async-start | bytes 6291456
  111.4 16.5 %slice-start.1 = ((s8[7340032]{0:T(1024)(128)(4,1)}), s8[4194304]{0:T(1024)(128)(4,1)S(1)}, s32[]{:S(2)}) async-start(s8[7340032]{0:T(1024)(128)(4,1)} %bitcast.42), calls=%async_computation.5 | async-start | bytes 8388608
  139.9 10.3 %copy-start.1 = (f32[64,8]{0,1:T(8,128)S(1)}, f32[64,8]{0,1:T(8,128)}, u32[]{:S(2)}) copy-start(f32[64,8]{0,1:T(8,128)} %param.8) | copy-start | bytes 6148
  139.9 57.3 %all-to-all-start.1 = ((bf16[128,8,1792]{2,1,0:T(8,128)(2,1)}), bf16[128,8,1792]{2,1,0:T(8,128)(2,1)}, u32[]{:S(2)}, u32[]{:S(2)}) async-start(bf16[128,8,1792]{2,1,0:T(8,128)(2,1)} %reshape.252), calls=%async_computation.1 | async-start | bytes 7340032 | tf_op jit(solution)/shard_map/all_to_all | solution.py:72

commit v9 on v6

--- a/solution.py
+++ b/solution.py
@@ -12,9 +12,11 @@
         "rd,hdgu->rhgu", rows, first_weights, preferred_element_type=jnp.float32
     )
     hidden = (jax.nn.silu(projected[:, :, 0]) * projected[:, :, 1]).astype(jnp.bfloat16)
-    output = jnp.einsum(
-        "rhu,hud->rd", hidden, second_weights, preferred_element_type=jnp.float32
-    )
+    output = jnp.dot(hidden[:, 0], second_weights[0], preferred_element_type=jnp.float32)
+    for half in range(1, hidden.shape[1]):
+        output = output + jnp.dot(
+            hidden[:, half], second_weights[half], preferred_element_type=jnp.float32
+        )
     return output.astype(jnp.bfloat16)
 
 

time: 200 us -> 201 us (level)
  local copies, waits for them, and re-layouts: 22.4 us -> 27.8 us
  waiting for transfers between devices: 95.9 us -> 91.8 us
  matrix products: 44.8 us -> 42.3 us
    dot_general x2 -> x4, matrix products: 13.8 us -> 9.61 us  [the longest x2 6.4 us: expert_ffn(): jnp.dot(hidden[:, half], second_weights[half], preferred_element_type=jnp...]
    all_to_all x2, waiting for transfers between devices: 53.2 us -> 50.6 us  [local(): lax.all_to_all(outgoing.reshape(experts, chunk_slots * pieces, piece), 'e...]
    reshape x2, local copies, waits for them, and re-layouts: 8.51 us -> 10.7 us  [local(): received.reshape(chunk_rows, d_model)]
  transfers between devices with their start and end apart: 4 -> 4, of which waited for: 3 -> 3; matrix products, arithmetic and copies ran while one was open for 30% -> 31% of each run, Pallas kernels for 0% -> 0%
where the time goes in v9:
time: 201 us; the launch traced here: 200 us
  waiting for transfers between devices  91.8 us (46%)
  matrix products  42.3 us (21%)
  starting transfers between devices  32.8 us (16%)
  local copies, waits for them, and re-layouts  27.8 us (14%)
  other arithmetic  5.18 us (3%)
    all_to_all x2, waiting for transfers between devices, local(): lax.all_to_all(outgoing.reshape(experts, chunk_slots * pieces, piece), 'e...  50.6 us
    all_to_all x2, waiting for transfers between devices, local(): lax.all_to_all(expert_out.reshape(experts, chunk_slots * pieces, piece),...  41.2 us
    dot_general x2, matrix products, expert_ffn(): jnp.einsum('rd,hdgu->rhgu', rows, first_weights, preferred_element_type=j...  20.4 us
    all_to_all x2, starting transfers between devices, local(): lax.all_to_all(outgoing.reshape(experts, chunk_slots * pieces, piece), 'e...  16.9 us
    all_to_all x2, starting transfers between devices, local(): lax.all_to_all(expert_out.reshape(experts, chunk_slots * pieces, piece),...  15.9 us
    reshape x2, local copies, waits for them, and re-layouts, local(): received.reshape(chunk_rows, d_model)  10.7 us
    reshape x2, local copies, waits for them, and re-layouts, local(): expert_out.reshape(experts, chunk_slots * pieces, piece)  10.3 us
    dot_general x2, matrix products, local(): jnp.dot(dispatch, token_pieces, preferred_element_type=jnp.float32)  6.46 us
  transfers between devices with their start and end apart: 4, of which 3 were waited for; matrix products, arithmetic and copies ran while one was open for 31% of the time, Pallas kernels for 0%

profile of v9, /device:TPU:1, one launch (start us, length us, event | category | flops | bytes accessed | tf_op | source)
XLA Modules:
  0.0 200.2 jit_solution(17002525681700235198)
XLA Ops:
  0.0 0.8 copy.33
  1.0 0.8 select_reduce_fusion.1
  2.5 1.3 reshape.252
  4.0 0.6 slice_reduce_fusion.15
  4.7 3.0 %convert_bitcast_fusion = bf16[128,8,896]{2,1,0:T(8,128)(2,1)} fusion(bf16[256,896]{1,0:T(8,128)(2,1)S(1)} %reshape.252, s32[1024]{0:T(1024)S(1)} %get-tuple-element.49, s32[1024]{0:T(1024)S(1)} %get-tuple-element.50, s32[256]{0:T(256)S(1)} %get-tuple-element.14, s32[256]{0:T(256)S(1)} %get-tuple-element.15, s32[256]{0:T(256)S(1)} %get-tuple-element.16, ...), kind=kOutput, calls=%fused_computation.29 | convolution fusion | flops 475136000 | bytes 2311168 | tf_op jit(solution)/shard_map/dot_general | solution.py:62
  7.6 11.5 %all-to-all-start.2 = ((bf16[128,8,896]{2,1,0:T(8,128)(2,1)}), bf16[128,8,896]{2,1,0:T(8,128)(2,1)S(1)}, u32[]{:S(2)}, u32[]{:S(2)}) async-start(bf16[128,8,896]{2,1,0:T(8,128)(2,1)} %convert_bitcast_fusion), calls=%async_computation.2 | async-start | bytes 3670016 | tf_op jit(solution)/shard_map/all_to_all | solution.py:63
  19.6 0.4 slice_reduce_fusion.31
  20.0 3.5 %fusion.14 = bf16[128,8,1792]{2,1,0:T(8,128)(2,1)} fusion(bf16[128,1792]{1,0:T(8,128)(2,1)S(1)} %reshape.245, s32[1024]{0:T(1024)S(1)} %get-tuple-element.47, s32[1024]{0:T(1024)S(1)} %get-tuple-element.48, s32[128]{0:T(128)S(1)} %get-tuple-element.30, s32[128]{0:T(128)S(1)} %get-tuple-element.31, s32[128]{0:T(128)S(1)} %get-tuple-element.32, ...), kind=kOutput, calls=%fused_computation.17 | convolution fusion | flops 473825280 | bytes 4141568 | tf_op jit(solution)/shard_map/dot_general | solution.py:62
  23.4 23.4 %all-to-all-done.2 = bf16[128,8,896]{2,1,0:T(8,128)(2,1)S(1)} async-done(((bf16[128,8,896]{2,1,0:T(8,128)(2,1)}), bf16[128,8,896]{2,1,0:T(8,128)(2,1)S(1)}, u32[]{:S(2)}, u32[]{:S(2)}) %all-to-all-start.2) | async-done | bytes 1835040 | tf_op jit(solution)/shard_map/all_to_all | solution.py:63
  46.8 1.3 copy-done
  48.1 5.4 %all-to-all-start = ((bf16[128,8,1792]{2,1,0:T(8,128)(2,1)}), bf16[128,8,1792]{2,1,0:T(8,128)(2,1)}, u32[]{:S(2)}, u32[]{:S(2)}) async-start(bf16[128,8,1792]{2,1,0:T(8,128)(2,1)} %fusion.14), calls=%async_computation | async-start | bytes 7340032 | tf_op jit(solution)/shard_map/all_to_all | solution.py:63
  53.6 4.1 %reshape.259 = bf16[256,3584,1,1]{1,0,2,3:T(8,128)(2,1)} reshape(bf16[128,8,896]{2,1,0:T(8,128)(2,1)} %copy-done) | data formatting | bytes 3670016 | tf_op jit(solution)/shard_map/reshape | solution.py:70
  57.7 8.0 %fusion = f32[256,2,2,512]{3,0,2,1:T(8,128)S(1)} fusion(bf16[2,3584,2,512]{3,2,1,0:T(2,128)(2,1)} %bitcast.91, bf16[256,3584,1,1]{1,0,2,3:T(8,128)(2,1)} %reshape.259), kind=kOutput, calls=%fused_computation | convolution fusion | flops 3758096384 | bytes 18612224 | tf_op jit(solution)/shard_map/rd,hdgu->rhgu/dot_general | solution.py:11
  66.0 1.1 fusion.9
  67.2 2.4 %fusion.4 = bf16[256,3584]{1,0:T(8,128)(2,1)} fusion(f32[256,3584]{1,0:T(8,128)S(1)} %fusion.9, bf16[1,2,512,3584]{3,2,1,0:T(8,128)(2,1)S(1)} %bitcast.81, bf16[256,2,512]{2,0,1:T(8,128)(2,1)S(1)} %fusion.32), kind=kOutput, calls=%fused_computation.6 | convolution fusion | flops 941359104 | bytes 9437184 | tf_op jit(solution)/shard_map/dot_general | solution.py:17
  69.6 3.9 %reshape.255 = bf16[128,8,896]{2,1,0:T(8,128)(2,1)} reshape(bf16[256,3584]{1,0:T(8,128)(2,1)} %fusion.4) | data formatting | bytes 3670016 | tf_op jit(solution)/shard_map/reshape | solution.py:72
  73.5 27.2 %all-to-all-done = bf16[128,8,1792]{2,1,0:T(8,128)(2,1)} async-done(((bf16[128,8,1792]{2,1,0:T(8,128)(2,1)}), bf16[128,8,1792]{2,1,0:T(8,128)(2,1)}, u32[]{:S(2)}, u32[]{:S(2)}) %all-to-all-start) | async-done | bytes 3670048 | tf_op jit(solution)/shard_map/all_to_all | solution.py:63
  100.7 5.6 %all-to-all-start.3 = ((bf16[128,8,896]{2,1,0:T(8,128)(2,1)}), bf16[128,8,896]{2,1,0:T(8,128)(2,1)}, u32[]{:S(2)}, u32[]{:S(2)}) async-start(bf16[128,8,896]{2,1,0:T(8,128)(2,1)} %reshape.255), calls=%async_computation.3 | async-start | bytes 3670016 | tf_op jit(solution)/shard_map/all_to_all | solution.py:71
  106.3 6.6 %reshape.258 = bf16[512,3584,1,1]{1,0,2,3:T(8,128)(2,1)} reshape(bf16[128,8,1792]{2,1,0:T(8,128)(2,1)} %all-to-all-done) | data formatting | bytes 7340032 | tf_op jit(solution)/shard_map/reshape | solution.py:70
  112.9 12.4 %fusion.2 = f32[512,2,2,512]{3,0,2,1:T(8,128)S(1)} fusion(bf16[2,3584,2,512]{3,2,1,0:T(2,128)(2,1)} %bitcast.92, bf16[512,3584,1,1]{1,0,2,3:T(8,128)(2,1)} %reshape.258), kind=kOutput, calls=%fused_computation.2 | convolution fusion | flops 7516192768 | bytes 22544384 | tf_op jit(solution)/shard_map/rd,hdgu->rhgu/dot_general | solution.py:11
  125.3 0.7 fusion.20
  126.0 2.1 %fusion.11 = f32[512,3584]{1,0:T(8,128)S(1)} fusion(bf16[1,2,512,3584]{3,2,1,0:T(8,128)(2,1)S(1)} %bitcast.83, bf16[512,2,512]{2,0,1:T(8,128)(2,1)S(1)} %fusion.20), kind=kOutput, calls=%fused_computation.14 | convolution fusion | flops 1879048192 | bytes 11534336 | tf_op jit(solution)/shard_map/dot_general | solution.py:15
  128.1 4.0 %add_convert_fusion = bf16[512,3584]{1,0:T(8,128)(2,1)} fusion(f32[512,3584]{1,0:T(8,128)S(1)} %fusion.11, bf16[1,2,512,3584]{3,2,1,0:T(8,128)(2,1)S(1)} %bitcast.83, bf16[512,2,512]{2,0,1:T(8,128)(2,1)S(1)} %fusion.20), kind=kOutput, calls=%fused_computation.4 | convolution fusion | flops 1882718208 | bytes 15204352 | tf_op jit(solution)/shard_map/dot_general | solution.py:17
  132.1 6.4 %reshape.248 = bf16[128,8,1792]{2,1,0:T(8,128)(2,1)} reshape(bf16[512,3584]{1,0:T(8,128)(2,1)} %add_convert_fusion) | data formatting | bytes 7340032 | tf_op jit(solution)/shard_map/reshape | solution.py:72
  138.5 10.3 %all-to-all-start.1 = ((bf16[128,8,1792]{2,1,0:T(8,128)(2,1)}), bf16[128,8,1792]{2,1,0:T(8,128)(2,1)}, u32[]{:S(2)}, u32[]{:S(2)}) async-start(bf16[128,8,1792]{2,1,0:T(8,128)(2,1)} %reshape.248), calls=%async_computation.1 | async-start | bytes 7340032 | tf_op jit(solution)/shard_map/all_to_all | solution.py:71
  149.3 0.6 slice_reduce_fusion.14
  150.0 0.5 subtract_convert_fusion.1
  150.5 1.1 subtract_convert_fusion
  151.6 2.8 %fusion.21 = f32[512,896]{1,0:T(8,128)S(1)} fusion(bf16[128,8,896]{2,1,0:T(8,128)(2,1)} %all-to-all-done.3, bf16[256,1024]{1,0:T(8,128)(2,1)S(1)} %get-tuple-element.39, bf16[256,1024]{1,0:T(8,128)(2,1)S(1)} %get-tuple-element.40), kind=kOutput, calls=%fused_computation.26 | convolution fusion | flops 941621248 | bytes 4718592 | tf_op jit(solution)/shard_map/dot_general | solution.py:81
  154.6 41.2 %all-to-all-done.1 = bf16[128,8,1792]{2,1,0:T(8,128)(2,1)} async-done(((bf16[128,8,1792]{2,1,0:T(8,128)(2,1)}), bf16[128,8,1792]{2,1,0:T(8,128)(2,1)}, u32[]{:S(2)}, u32[]{:S(2)}) %all-to-all-start.1) | async-done | bytes 3670048 | tf_op jit(solution)/shard_map/all_to_all | solution.py:71
  195.8 3.1 %fusion.5 = f32[256,1792]{1,0:T(8,128)S(1)} fusion(bf16[128,8,1792]{2,1,0:T(8,128)(2,1)} %all-to-all-done.1, bf16[128,1024]{1,0:T(8,128)(2,1)S(1)} %get-tuple-element.41, bf16[128,1024]{1,0:T(8,128)(2,1)S(1)} %get-tuple-element.42), kind=kOutput, calls=%fused_computation.8 | convolution fusion | flops 940572672 | bytes 6029312 | tf_op jit(solution)/shard_map/dot_general | solution.py:81
  199.3 0.9 add_convert_fusion.1
  (49 shorter events, 3.0 us)
Async XLA Ops:
  4.7 14.5 %copy-start.1 = (bf16[64,3584]{1,0:T(8,128)(2,1)S(1)}, bf16[64,3584]{1,0:T(8,128)(2,1)}, u32[]{:S(2)}) copy-start(bf16[64,3584]{1,0:T(8,128)(2,1)} %param.6) | copy-start | bytes 1376260
  7.6 39.1 %all-to-all-start.2 = ((bf16[128,8,896]{2,1,0:T(8,128)(2,1)}), bf16[128,8,896]{2,1,0:T(8,128)(2,1)S(1)}, u32[]{:S(2)}, u32[]{:S(2)}) async-start(bf16[128,8,896]{2,1,0:T(8,128)(2,1)} %convert_bitcast_fusion), calls=%async_computation.2 | async-start | bytes 3670016 | tf_op jit(solution)/shard_map/all_to_all | solution.py:63
  46.8 1.3 copy-start
  48.1 52.6 %all-to-all-start = ((bf16[128,8,1792]{2,1,0:T(8,128)(2,1)}), bf16[128,8,1792]{2,1,0:T(8,128)(2,1)}, u32[]{:S(2)}, u32[]{:S(2)}) async-start(bf16[128,8,1792]{2,1,0:T(8,128)(2,1)} %fusion.14), calls=%async_computation | async-start | bytes 7340032 | tf_op jit(solution)/shard_map/all_to_all | solution.py:63
  53.6 12.4 %slice-start = ((s8[7340032]{0:T(1024)(128)(4,1)}), s8[3145728]{0:T(1024)(128)(4,1)S(1)}, s32[]{:S(2)}) async-start(s8[7340032]{0:T(1024)(128)(4,1)} %bitcast.80), calls=%async_computation.4 | async-start | bytes 6291456
  57.7 8.3 %slice-start.1 = ((s8[7340032]{0:T(1024)(128)(4,1)}), s8[4194304]{0:T(1024)(128)(4,1)S(1)}, s32[]{:S(2)}) async-start(s8[7340032]{0:T(1024)(128)(4,1)} %bitcast.80), calls=%async_computation.5 | async-start | bytes 8388608
  100.7 37.8 %all-to-all-start.3 = ((bf16[128,8,896]{2,1,0:T(8,128)(2,1)}), bf16[128,8,896]{2,1,0:T(8,128)(2,1)}, u32[]{:S(2)}, u32[]{:S(2)}) async-start(bf16[128,8,896]{2,1,0:T(8,128)(2,1)} %reshape.255), calls=%async_computation.3 | async-start | bytes 3670016 | tf_op jit(solution)/shard_map/all_to_all | solution.py:71
  106.3 19.7 %slice-start.2 = ((s8[7340032]{0:T(1024)(128)(4,1)}), s8[3145728]{0:T(1024)(128)(4,1)S(1)}, s32[]{:S(2)}) async-start(s8[7340032]{0:T(1024)(128)(4,1)} %bitcast.82), calls=%async_computation.6 | async-start | bytes 6291456
  112.9 13.1 %slice-start.3 = ((s8[7340032]{0:T(1024)(128)(4,1)}), s8[4194304]{0:T(1024)(128)(4,1)S(1)}, s32[]{:S(2)}) async-start(s8[7340032]{0:T(1024)(128)(4,1)} %bitcast.82), calls=%async_computation.7 | async-start | bytes 8388608
  138.5 10.3 %copy-start.2 = (f32[64,8]{0,1:T(8,128)S(1)}, f32[64,8]{0,1:T(8,128)}, u32[]{:S(2)}) copy-start(f32[64,8]{0,1:T(8,128)} %param.8) | copy-start | bytes 6148
  138.5 57.3 %all-to-all-start.1 = ((bf16[128,8,1792]{2,1,0:T(8,128)(2,1)}), bf16[128,8,1792]{2,1,0:T(8,128)(2,1)}, u32[]{:S(2)}, u32[]{:S(2)}) async-start(bf16[128,8,1792]{2,1,0:T(8,128)(2,1)} %reshape.248), calls=%async_computation.1 | async-start | bytes 7340032 | tf_op jit(solution)/shard_map/all_to_all | solution.py:71

commit v10 on v9

--- a/solution.py
+++ b/solution.py
@@ -7,11 +7,16 @@
 CHUNKS = ((4, 2), (2, 4))
 
 
-def expert_ffn(rows, first_weights, second_weights):
+def expert_ffn(rows, first_weights, second_weights, split_halves):
     projected = jnp.einsum(
         "rd,hdgu->rhgu", rows, first_weights, preferred_element_type=jnp.float32
     )
     hidden = (jax.nn.silu(projected[:, :, 0]) * projected[:, :, 1]).astype(jnp.bfloat16)
+    if not split_halves:
+        output = jnp.einsum(
+            "rhu,hud->rd", hidden, second_weights, preferred_element_type=jnp.float32
+        )
+        return output.astype(jnp.bfloat16)
     output = jnp.dot(hidden[:, 0], second_weights[0], preferred_element_type=jnp.float32)
     for half in range(1, hidden.shape[1]):
         output = output + jnp.dot(
@@ -67,7 +72,9 @@
             concat_axis=0,
             tiled=True,
         )
-        expert_out = expert_ffn(received.reshape(chunk_rows, d_model), w_in[0], w_out[0])
+        expert_out = expert_ffn(
+            received.reshape(chunk_rows, d_model), w_in[0], w_out[0], chunk_slots > 2
+        )
         answered = lax.all_to_all(
             expert_out.reshape(experts, chunk_slots * pieces, piece),
             "expert",

time: 201 us -> 201 us (level)
    dot_general x0 -> x1, matrix products: none -> 3.4 us  [expert_ffn(): jnp.einsum('rhu,hud->rd', hidden, second_weights, preferred_element_type=...]
    dot_general x2 -> x1, matrix products: 6.4 us -> 3.99 us  [expert_ffn(): jnp.dot(hidden[:, half], second_weights[half], preferred_element_type=jnp...]
where the time goes in v10:
time: 201 us; the launch traced here: 200 us
  waiting for transfers between devices  92.2 us (46%)
  matrix products  42.2 us (21%)
  starting transfers between devices  32.7 us (16%)
  local copies, waits for them, and re-layouts  27.8 us (14%)
  other arithmetic  4.86 us (2%)
    all_to_all x2, waiting for transfers between devices, local(): lax.all_to_all(outgoing.reshape(experts, chunk_slots * pieces, piece), 'e...  51 us
    all_to_all x2, waiting for transfers between devices, local(): lax.all_to_all(expert_out.reshape(experts, chunk_slots * pieces, piece),...  41.2 us
    dot_general x2, matrix products, expert_ffn(): jnp.einsum('rd,hdgu->rhgu', rows, first_weights, preferred_element_type=j...  20.4 us
    all_to_all x2, starting transfers between devices, local(): lax.all_to_all(outgoing.reshape(experts, chunk_slots * pieces, piece), 'e...  16.9 us
    all_to_all x2, starting transfers between devices, local(): lax.all_to_all(expert_out.reshape(experts, chunk_slots * pieces, piece),...  15.7 us
    reshape x2, local copies, waits for them, and re-layouts, local(): received.reshape(chunk_rows, d_model)  10.7 us
    reshape x2, local copies, waits for them, and re-layouts, local(): expert_out.reshape(experts, chunk_slots * pieces, piece)  10.3 us
    dot_general x2, matrix products, local(): jnp.dot(dispatch, token_pieces, preferred_element_type=jnp.float32)  6.46 us
  transfers between devices with their start and end apart: 4, of which 3 were waited for; matrix products, arithmetic and copies ran while one was open for 31% of the time, Pallas kernels for 0%

profile of v10, /device:TPU:1, one launch (start us, length us, event | category | flops | bytes accessed | tf_op | source)
XLA Modules:
  0.0 200.0 jit_solution(8410785390483928675)
XLA Ops:
  0.0 0.8 copy.30
  1.0 0.8 select_reduce_fusion.1
  2.5 1.3 reshape.253
  4.0 0.6 slice_reduce_fusion.15
  4.7 3.0 %convert_bitcast_fusion = bf16[128,8,896]{2,1,0:T(8,128)(2,1)} fusion(bf16[256,896]{1,0:T(8,128)(2,1)S(1)} %reshape.253, s32[1024]{0:T(1024)S(1)} %get-tuple-element.49, s32[1024]{0:T(1024)S(1)} %get-tuple-element.50, s32[256]{0:T(256)S(1)} %get-tuple-element.14, s32[256]{0:T(256)S(1)} %get-tuple-element.15, s32[256]{0:T(256)S(1)} %get-tuple-element.16, ...), kind=kOutput, calls=%fused_computation.26 | convolution fusion | flops 475136000 | bytes 2311168 | tf_op jit(solution)/shard_map/dot_general | solution.py:67
  7.6 11.5 %all-to-all-start.2 = ((bf16[128,8,896]{2,1,0:T(8,128)(2,1)}), bf16[128,8,896]{2,1,0:T(8,128)(2,1)S(1)}, u32[]{:S(2)}, u32[]{:S(2)}) async-start(bf16[128,8,896]{2,1,0:T(8,128)(2,1)} %convert_bitcast_fusion), calls=%async_computation.2 | async-start | bytes 3670016 | tf_op jit(solution)/shard_map/all_to_all | solution.py:68
  19.6 0.4 slice_reduce_fusion.31
  20.0 3.5 %fusion.20 = bf16[128,8,1792]{2,1,0:T(8,128)(2,1)} fusion(bf16[128,1792]{1,0:T(8,128)(2,1)S(1)} %reshape.246, s32[1024]{0:T(1024)S(1)} %get-tuple-element.47, s32[1024]{0:T(1024)S(1)} %get-tuple-element.48, s32[128]{0:T(128)S(1)} %get-tuple-element.30, s32[128]{0:T(128)S(1)} %get-tuple-element.31, s32[128]{0:T(128)S(1)} %get-tuple-element.32, ...), kind=kOutput, calls=%fused_computation.18 | convolution fusion | flops 473825280 | bytes 4141568 | tf_op jit(solution)/shard_map/dot_general | solution.py:67
  23.4 23.4 %all-to-all-done.2 = bf16[128,8,896]{2,1,0:T(8,128)(2,1)S(1)} async-done(((bf16[128,8,896]{2,1,0:T(8,128)(2,1)}), bf16[128,8,896]{2,1,0:T(8,128)(2,1)S(1)}, u32[]{:S(2)}, u32[]{:S(2)}) %all-to-all-start.2) | async-done | bytes 1835040 | tf_op jit(solution)/shard_map/all_to_all | solution.py:68
  46.8 1.3 copy-done
  48.1 5.4 %all-to-all-start = ((bf16[128,8,1792]{2,1,0:T(8,128)(2,1)}), bf16[128,8,1792]{2,1,0:T(8,128)(2,1)}, u32[]{:S(2)}, u32[]{:S(2)}) async-start(bf16[128,8,1792]{2,1,0:T(8,128)(2,1)} %fusion.20), calls=%async_computation | async-start | bytes 7340032 | tf_op jit(solution)/shard_map/all_to_all | solution.py:68
  53.6 4.1 %reshape.260 = bf16[256,3584,1,1]{1,0,2,3:T(8,128)(2,1)} reshape(bf16[128,8,896]{2,1,0:T(8,128)(2,1)} %copy-done) | data formatting | bytes 3670016 | tf_op jit(solution)/shard_map/reshape | solution.py:76
  57.7 8.0 %fusion = f32[256,2,2,512]{3,0,2,1:T(8,128)S(1)} fusion(bf16[2,3584,2,512]{3,2,1,0:T(2,128)(2,1)} %bitcast.83, bf16[256,3584,1,1]{1,0,2,3:T(8,128)(2,1)} %reshape.260), kind=kOutput, calls=%fused_computation | convolution fusion | flops 3758096384 | bytes 18612224 | tf_op jit(solution)/shard_map/rd,hdgu->rhgu/dot_general | solution.py:11
  65.7 3.4 %fusion.9 = bf16[256,3584]{1,0:T(8,128)(2,1)} fusion(bf16[1,2,512,3584]{3,2,1,0:T(8,128)(2,1)S(1)} %bitcast.75, f32[256,2,2,512]{3,0,2,1:T(8,128)S(1)} %fusion), kind=kOutput, calls=%fused_computation.8 | convolution fusion | flops 1881538560 | bytes 11272192 | tf_op jit(solution)/shard_map/rhu,hud->rd/dot_general | solution.py:16
  69.1 3.9 %reshape.256 = bf16[128,8,896]{2,1,0:T(8,128)(2,1)} reshape(bf16[256,3584]{1,0:T(8,128)(2,1)} %fusion.9) | data formatting | bytes 3670016 | tf_op jit(solution)/shard_map/reshape | solution.py:79
  73.0 27.7 %all-to-all-done = bf16[128,8,1792]{2,1,0:T(8,128)(2,1)} async-done(((bf16[128,8,1792]{2,1,0:T(8,128)(2,1)}), bf16[128,8,1792]{2,1,0:T(8,128)(2,1)}, u32[]{:S(2)}, u32[]{:S(2)}) %all-to-all-start) | async-done | bytes 3670048 | tf_op jit(solution)/shard_map/all_to_all | solution.py:68
  100.7 5.4 %all-to-all-start.3 = ((bf16[128,8,896]{2,1,0:T(8,128)(2,1)}), bf16[128,8,896]{2,1,0:T(8,128)(2,1)}, u32[]{:S(2)}, u32[]{:S(2)}) async-start(bf16[128,8,896]{2,1,0:T(8,128)(2,1)} %reshape.256), calls=%async_computation.3 | async-start | bytes 3670016 | tf_op jit(solution)/shard_map/all_to_all | solution.py:78
  106.2 6.6 %reshape.259 = bf16[512,3584,1,1]{1,0,2,3:T(8,128)(2,1)} reshape(bf16[128,8,1792]{2,1,0:T(8,128)(2,1)} %all-to-all-done) | data formatting | bytes 7340032 | tf_op jit(solution)/shard_map/reshape | solution.py:76
  112.7 12.4 %fusion.2 = f32[512,2,2,512]{3,0,2,1:T(8,128)S(1)} fusion(bf16[2,3584,2,512]{3,2,1,0:T(2,128)(2,1)} %bitcast.84, bf16[512,3584,1,1]{1,0,2,3:T(8,128)(2,1)} %reshape.259), kind=kOutput, calls=%fused_computation.2 | convolution fusion | flops 7516192768 | bytes 22544384 | tf_op jit(solution)/shard_map/rd,hdgu->rhgu/dot_general | solution.py:11
  125.1 0.7 fusion.22
  125.9 2.1 %fusion.15 = f32[512,3584]{1,0:T(8,128)S(1)} fusion(bf16[1,2,512,3584]{3,2,1,0:T(8,128)(2,1)S(1)} %bitcast.77, bf16[512,2,512]{2,0,1:T(8,128)(2,1)S(1)} %fusion.22), kind=kOutput, calls=%fused_computation.13 | convolution fusion | flops 1879048192 | bytes 11534336 | tf_op jit(solution)/shard_map/dot_general | solution.py:20
  127.9 4.0 %add_convert_fusion = bf16[512,3584]{1,0:T(8,128)(2,1)} fusion(f32[512,3584]{1,0:T(8,128)S(1)} %fusion.15, bf16[1,2,512,3584]{3,2,1,0:T(8,128)(2,1)S(1)} %bitcast.77, bf16[512,2,512]{2,0,1:T(8,128)(2,1)S(1)} %fusion.22), kind=kOutput, calls=%fused_computation.6 | convolution fusion | flops 1882718208 | bytes 15204352 | tf_op jit(solution)/shard_map/dot_general | solution.py:22
  131.9 6.4 %reshape.249 = bf16[128,8,1792]{2,1,0:T(8,128)(2,1)} reshape(bf16[512,3584]{1,0:T(8,128)(2,1)} %add_convert_fusion) | data formatting | bytes 7340032 | tf_op jit(solution)/shard_map/reshape | solution.py:79
  138.3 10.3 %all-to-all-start.1 = ((bf16[128,8,1792]{2,1,0:T(8,128)(2,1)}), bf16[128,8,1792]{2,1,0:T(8,128)(2,1)}, u32[]{:S(2)}, u32[]{:S(2)}) async-start(bf16[128,8,1792]{2,1,0:T(8,128)(2,1)} %reshape.249), calls=%async_computation.1 | async-start | bytes 7340032 | tf_op jit(solution)/shard_map/all_to_all | solution.py:78
  148.8 0.4 slice_reduce_fusion.30
  149.2 0.6 slice_reduce_fusion.14
  149.8 0.5 subtract_convert_fusion.1
  150.3 1.1 subtract_convert_fusion
  151.5 2.8 %fusion.23 = f32[512,896]{1,0:T(8,128)S(1)} fusion(bf16[128,8,896]{2,1,0:T(8,128)(2,1)} %all-to-all-done.3, bf16[256,1024]{1,0:T(8,128)(2,1)S(1)} %get-tuple-element.39, bf16[256,1024]{1,0:T(8,128)(2,1)S(1)} %get-tuple-element.40), kind=kOutput, calls=%fused_computation.23 | convolution fusion | flops 941621248 | bytes 4718592 | tf_op jit(solution)/shard_map/dot_general | solution.py:88
  154.5 41.2 %all-to-all-done.1 = bf16[128,8,1792]{2,1,0:T(8,128)(2,1)} async-done(((bf16[128,8,1792]{2,1,0:T(8,128)(2,1)}), bf16[128,8,1792]{2,1,0:T(8,128)(2,1)}, u32[]{:S(2)}, u32[]{:S(2)}) %all-to-all-start.1) | async-done | bytes 3670048 | tf_op jit(solution)/shard_map/all_to_all | solution.py:78
  195.7 3.1 %fusion.12 = f32[256,1792]{1,0:T(8,128)S(1)} fusion(bf16[128,8,1792]{2,1,0:T(8,128)(2,1)} %all-to-all-done.1, bf16[128,1024]{1,0:T(8,128)(2,1)S(1)} %get-tuple-element.41, bf16[128,1024]{1,0:T(8,128)(2,1)S(1)} %get-tuple-element.42), kind=kOutput, calls=%fused_computation.10 | convolution fusion | flops 940572672 | bytes 6029312 | tf_op jit(solution)/shard_map/dot_general | solution.py:88
  199.2 0.9 add_convert_fusion.1
  (47 shorter events, 2.3 us)
Async XLA Ops:
  4.7 14.5 %copy-start.1 = (bf16[64,3584]{1,0:T(8,128)(2,1)S(1)}, bf16[64,3584]{1,0:T(8,128)(2,1)}, u32[]{:S(2)}) copy-start(bf16[64,3584]{1,0:T(8,128)(2,1)} %param.6) | copy-start | bytes 1376260
  7.6 39.1 %all-to-all-start.2 = ((bf16[128,8,896]{2,1,0:T(8,128)(2,1)}), bf16[128,8,896]{2,1,0:T(8,128)(2,1)S(1)}, u32[]{:S(2)}, u32[]{:S(2)}) async-start(bf16[128,8,896]{2,1,0:T(8,128)(2,1)} %convert_bitcast_fusion), calls=%async_computation.2 | async-start | bytes 3670016 | tf_op jit(solution)/shard_map/all_to_all | solution.py:68
  46.8 1.3 copy-start
  48.1 52.6 %all-to-all-start = ((bf16[128,8,1792]{2,1,0:T(8,128)(2,1)}), bf16[128,8,1792]{2,1,0:T(8,128)(2,1)}, u32[]{:S(2)}, u32[]{:S(2)}) async-start(bf16[128,8,1792]{2,1,0:T(8,128)(2,1)} %fusion.20), calls=%async_computation | async-start | bytes 7340032 | tf_op jit(solution)/shard_map/all_to_all | solution.py:68
  53.6 12.1 %slice-start = ((s8[7340032]{0:T(1024)(128)(4,1)}), s8[3145728]{0:T(1024)(128)(4,1)S(1)}, s32[]{:S(2)}) async-start(s8[7340032]{0:T(1024)(128)(4,1)} %bitcast.74), calls=%async_computation.4 | async-start | bytes 6291456
  57.7 8.0 %slice-start.1 = ((s8[7340032]{0:T(1024)(128)(4,1)}), s8[4194304]{0:T(1024)(128)(4,1)S(1)}, s32[]{:S(2)}) async-start(s8[7340032]{0:T(1024)(128)(4,1)} %bitcast.74), calls=%async_computation.5 | async-start | bytes 8388608
  100.7 37.6 %all-to-all-start.3 = ((bf16[128,8,896]{2,1,0:T(8,128)(2,1)}), bf16[128,8,896]{2,1,0:T(8,128)(2,1)}, u32[]{:S(2)}, u32[]{:S(2)}) async-start(bf16[128,8,896]{2,1,0:T(8,128)(2,1)} %reshape.256), calls=%async_computation.3 | async-start | bytes 3670016 | tf_op jit(solution)/shard_map/all_to_all | solution.py:78
  106.1 19.7 %slice-start.2 = ((s8[7340032]{0:T(1024)(128)(4,1)}), s8[3145728]{0:T(1024)(128)(4,1)S(1)}, s32[]{:S(2)}) async-start(s8[7340032]{0:T(1024)(128)(4,1)} %bitcast.76), calls=%async_computation.6 | async-start | bytes 6291456
  112.7 13.1 %slice-start.3 = ((s8[7340032]{0:T(1024)(128)(4,1)}), s8[4194304]{0:T(1024)(128)(4,1)S(1)}, s32[]{:S(2)}) async-start(s8[7340032]{0:T(1024)(128)(4,1)} %bitcast.76), calls=%async_computation.7 | async-start | bytes 8388608
  138.3 10.3 %copy-start.2 = (f32[64,8]{0,1:T(8,128)S(1)}, f32[64,8]{0,1:T(8,128)}, u32[]{:S(2)}) copy-start(f32[64,8]{0,1:T(8,128)} %param.8) | copy-start | bytes 6148
  138.3 57.3 %all-to-all-start.1 = ((bf16[128,8,1792]{2,1,0:T(8,128)(2,1)}), bf16[128,8,1792]{2,1,0:T(8,128)(2,1)}, u32[]{:S(2)}, u32[]{:S(2)}) async-start(bf16[128,8,1792]{2,1,0:T(8,128)(2,1)} %reshape.249), calls=%async_computation.1 | async-start | bytes 7340032 | tf_op jit(solution)/shard_map/all_to_all | solution.py:78

commit v11 on v6

--- a/solution.py
+++ b/solution.py
@@ -73,12 +73,9 @@
             concat_axis=0,
             tiled=True,
         ).reshape(chunk_rows * pieces, piece)
-        combine_hi = combine.astype(jnp.bfloat16)
-        combine_lo = (combine - combine_hi.astype(jnp.float32)).astype(jnp.bfloat16)
-        stacked = jnp.concatenate([combine_hi, combine_lo], axis=0)
-        part = jnp.dot(stacked, answered, preferred_element_type=jnp.float32)
-        half = tok_dev * pieces
-        part = (part[:half] + part[half:]).reshape(tok_dev, d_model)
+        part = jnp.dot(
+            combine.astype(jnp.bfloat16), answered, preferred_element_type=jnp.float32
+        ).reshape(tok_dev, d_model)
         weighted = part if weighted is None else weighted + part
     return weighted.astype(jnp.bfloat16)
 

time: 200 us -> 200 us (level)
  transfers between devices with their start and end apart: 4 -> 4, of which waited for: 3 -> 3; matrix products, arithmetic and copies ran while one was open for 30% -> 29% of each run, Pallas kernels for 0% -> 0%
where the time goes in v11:
time: 200 us; the launch traced here: 199 us
  waiting for transfers between devices  97.5 us (49%)
  matrix products  44.9 us (22%)
  starting transfers between devices  31.8 us (16%)
  local copies, waits for them, and re-layouts  22.4 us (11%)
  other arithmetic  2.3 us (1%)
    all_to_all x2, waiting for transfers between devices, local(): lax.all_to_all(outgoing.reshape(experts, chunk_slots * pieces, piece), 'e...  53.2 us
    all_to_all x2, waiting for transfers between devices, local(): lax.all_to_all(expert_out.reshape(experts, chunk_slots * pieces, piece),...  44.3 us
    dot_general x2, matrix products, expert_ffn(): jnp.einsum('rd,hdgu->rhgu', rows, first_weights, preferred_element_type=j...  20.1 us
    all_to_all x2, starting transfers between devices, local(): lax.all_to_all(outgoing.reshape(experts, chunk_slots * pieces, piece), 'e...  16.9 us
    all_to_all x2, starting transfers between devices, local(): lax.all_to_all(expert_out.reshape(experts, chunk_slots * pieces, piece),...  14.9 us
    dot_general x2, matrix products, expert_ffn(): jnp.einsum('rhu,hud->rd', hidden, second_weights, preferred_element_type=...  13.8 us
    reshape x2, local copies, waits for them, and re-layouts, local(): received.reshape(chunk_rows, d_model)  8.51 us
    reshape x2, local copies, waits for them, and re-layouts, local(): expert_out.reshape(experts, chunk_slots * pieces, piece)  8.5 us
  transfers between devices with their start and end apart: 4, of which 3 were waited for; matrix products, arithmetic and copies ran while one was open for 29% of the time, Pallas kernels for 0%

profile of v11, /device:TPU:1, one launch (start us, length us, event | category | flops | bytes accessed | tf_op | source)
XLA Modules:
  0.0 199.2 jit_solution(9978343849801246808)
XLA Ops:
  0.0 0.8 copy.27
  1.0 0.8 select_reduce_fusion.1
  1.8 0.2 fusion.90
  2.2 0.3 select_reduce_fusion
  2.5 1.3 reshape.250
  4.0 0.6 slice_reduce_fusion.15
  4.7 3.0 %convert_bitcast_fusion = bf16[128,8,896]{2,1,0:T(8,128)(2,1)} fusion(bf16[256,896]{1,0:T(8,128)(2,1)S(1)} %reshape.250, s32[1024]{0:T(1024)S(1)} %get-tuple-element.45, s32[1024]{0:T(1024)S(1)} %get-tuple-element.46, s32[256]{0:T(256)S(1)} %get-tuple-element.14, s32[256]{0:T(256)S(1)} %get-tuple-element.15, s32[256]{0:T(256)S(1)} %get-tuple-element.16, ...), kind=kOutput, calls=%fused_computation.21 | convolution fusion | flops 475136000 | bytes 2311168 | tf_op jit(solution)/shard_map/dot_general | solution.py:60
  7.6 11.5 %all-to-all-start.2 = ((bf16[128,8,896]{2,1,0:T(8,128)(2,1)}), bf16[128,8,896]{2,1,0:T(8,128)(2,1)S(1)}, u32[]{:S(2)}, u32[]{:S(2)}) async-start(bf16[128,8,896]{2,1,0:T(8,128)(2,1)} %convert_bitcast_fusion), calls=%async_computation.2 | async-start | bytes 3670016 | tf_op jit(solution)/shard_map/all_to_all | solution.py:61
  19.2 0.2 reshape.243
  19.6 0.4 slice_reduce_fusion.31
  20.0 3.5 %fusion.19 = bf16[128,8,1792]{2,1,0:T(8,128)(2,1)} fusion(bf16[128,1792]{1,0:T(8,128)(2,1)S(1)} %reshape.243, s32[1024]{0:T(1024)S(1)} %get-tuple-element.43, s32[1024]{0:T(1024)S(1)} %get-tuple-element.44, s32[128]{0:T(128)S(1)} %get-tuple-element.30, s32[128]{0:T(128)S(1)} %get-tuple-element.31, s32[128]{0:T(128)S(1)} %get-tuple-element.32, ...), kind=kOutput, calls=%fused_computation.15 | convolution fusion | flops 473825280 | bytes 4141568 | tf_op jit(solution)/shard_map/dot_general | solution.py:60
  23.4 23.4 %all-to-all-done.2 = bf16[128,8,896]{2,1,0:T(8,128)(2,1)S(1)} async-done(((bf16[128,8,896]{2,1,0:T(8,128)(2,1)}), bf16[128,8,896]{2,1,0:T(8,128)(2,1)S(1)}, u32[]{:S(2)}, u32[]{:S(2)}) %all-to-all-start.2) | async-done | bytes 1835040 | tf_op jit(solution)/shard_map/all_to_all | solution.py:61
  46.8 5.4 %all-to-all-start = ((bf16[128,8,1792]{2,1,0:T(8,128)(2,1)}), bf16[128,8,1792]{2,1,0:T(8,128)(2,1)}, u32[]{:S(2)}, u32[]{:S(2)}) async-start(bf16[128,8,1792]{2,1,0:T(8,128)(2,1)} %fusion.19), calls=%async_computation | async-start | bytes 7340032 | tf_op jit(solution)/shard_map/all_to_all | solution.py:61
  52.2 2.1 %reshape.258 = bf16[256,3584,1,1]{1,0,2,3:T(8,128)(2,1)} reshape(bf16[128,8,896]{2,1,0:T(8,128)(2,1)S(1)} %all-to-all-done.2) | data formatting | bytes 3670016 | tf_op jit(solution)/shard_map/reshape | solution.py:68
  54.3 7.8 %fusion = f32[256,2,2,512]{3,0,2,1:T(8,128)S(1)} fusion(bf16[2,3584,2,512]{3,2,1,0:T(2,128)(2,1)} %bitcast.64, bf16[256,3584,1,1]{1,0,2,3:T(8,128)(2,1)} %reshape.258), kind=kOutput, calls=%fused_computation | convolution fusion | flops 3758096384 | bytes 18612224 | tf_op jit(solution)/shard_map/rd,hdgu->rhgu/dot_general | solution.py:11
  62.2 5.2 %fusion.13 = bf16[256,3584]{1,0:T(8,128)(2,1)S(1)} fusion(bf16[1,2,512,3584]{3,2,1,0:T(8,128)(2,1)} %param.11, f32[256,2,2,512]{3,0,2,1:T(8,128)S(1)} %fusion), kind=kOutput, calls=%fused_computation.10 | convolution fusion | flops 1881538560 | bytes 11272192 | tf_op jit(solution)/shard_map/rhu,hud->rd/dot_general | solution.py:15
  67.4 2.1 %reshape.253 = bf16[128,8,896]{2,1,0:T(8,128)(2,1)} reshape(bf16[256,3584]{1,0:T(8,128)(2,1)S(1)} %fusion.13) | data formatting | bytes 3670016 | tf_op jit(solution)/shard_map/reshape | solution.py:70
  69.5 29.9 %all-to-all-done = bf16[128,8,1792]{2,1,0:T(8,128)(2,1)} async-done(((bf16[128,8,1792]{2,1,0:T(8,128)(2,1)}), bf16[128,8,1792]{2,1,0:T(8,128)(2,1)}, u32[]{:S(2)}, u32[]{:S(2)}) %all-to-all-start) | async-done | bytes 3670048 | tf_op jit(solution)/shard_map/all_to_all | solution.py:61
  99.4 4.6 %all-to-all-start.3 = ((bf16[128,8,896]{2,1,0:T(8,128)(2,1)}), bf16[128,8,896]{2,1,0:T(8,128)(2,1)S(1)}, u32[]{:S(2)}, u32[]{:S(2)}) async-start(bf16[128,8,896]{2,1,0:T(8,128)(2,1)} %reshape.253), calls=%async_computation.3 | async-start | bytes 3670016 | tf_op jit(solution)/shard_map/all_to_all | solution.py:69
  104.0 6.4 %reshape.256 = bf16[512,3584,1,1]{1,0,2,3:T(8,128)(2,1)} reshape(bf16[128,8,1792]{2,1,0:T(8,128)(2,1)} %all-to-all-done) | data formatting | bytes 7340032 | tf_op jit(solution)/shard_map/reshape | solution.py:68
  110.4 12.2 %fusion.2 = f32[512,2,2,512]{3,0,2,1:T(8,128)S(1)} fusion(bf16[2,3584,2,512]{3,2,1,0:T(2,128)(2,1)} %bitcast.65, bf16[512,3584,1,1]{1,0,2,3:T(8,128)(2,1)} %reshape.256), kind=kOutput, calls=%fused_computation.2 | convolution fusion | flops 7516192768 | bytes 22544384 | tf_op jit(solution)/shard_map/rd,hdgu->rhgu/dot_general | solution.py:11
  122.7 8.6 %bitcast_convert_fusion = bf16[512,3584]{1,0:T(8,128)(2,1)} fusion(bf16[1,2,512,3584]{3,2,1,0:T(8,128)(2,1)} %param.11, f32[512,2,2,512]{3,0,2,1:T(8,128)S(1)} %fusion.2), kind=kOutput, calls=%fused_computation.4 | convolution fusion | flops 3763077120 | bytes 15204352 | tf_op jit(solution)/shard_map/rhu,hud->rd/dot_general | solution.py:15
  131.3 6.4 %reshape.246 = bf16[128,8,1792]{2,1,0:T(8,128)(2,1)} reshape(bf16[512,3584]{1,0:T(8,128)(2,1)} %bitcast_convert_fusion) | data formatting | bytes 7340032 | tf_op jit(solution)/shard_map/reshape | solution.py:70
  137.7 10.3 %all-to-all-start.1 = ((bf16[128,8,1792]{2,1,0:T(8,128)(2,1)}), bf16[128,8,1792]{2,1,0:T(8,128)(2,1)}, u32[]{:S(2)}, u32[]{:S(2)}) async-start(bf16[128,8,1792]{2,1,0:T(8,128)(2,1)} %reshape.246), calls=%async_computation.1 | async-start | bytes 7340032 | tf_op jit(solution)/shard_map/all_to_all | solution.py:69
  148.1 0.4 slice_reduce_fusion.30
  148.5 0.6 slice_reduce_fusion.14
  149.1 1.5 fusion.21
  150.6 0.1 reshape.255
  150.7 44.3 %all-to-all-done.1 = bf16[128,8,1792]{2,1,0:T(8,128)(2,1)} async-done(((bf16[128,8,1792]{2,1,0:T(8,128)(2,1)}), bf16[128,8,1792]{2,1,0:T(8,128)(2,1)}, u32[]{:S(2)}, u32[]{:S(2)}) %all-to-all-start.1) | async-done | bytes 3670048 | tf_op jit(solution)/shard_map/all_to_all | solution.py:69
  195.0 3.1 %fusion.16 = f32[128,1792]{1,0:T(8,128)S(1)} fusion(bf16[128,8,1792]{2,1,0:T(8,128)(2,1)} %all-to-all-done.1, f32[128]{0:T(128)S(1)} %get-tuple-element.22, f32[128]{0:T(128)S(1)} %get-tuple-element.23, f32[128]{0:T(128)S(1)} %get-tuple-element.24, f32[128]{0:T(128)S(1)} %get-tuple-element.25, f32[128]{0:T(128)S(1)} %get-tuple-element.26, ...), kind=kOutput, calls=%fused_computation.12 | convolution fusion | flops 473169920 | bytes 4604416 | tf_op jit(solution)/shard_map/dot_general | solution.py:76
  198.1 0.3 reshape.248
  198.4 0.9 add_convert_fusion
  (29 shorter events, 1.0 us)
Async XLA Ops:
  4.7 14.5 %copy-start = (bf16[64,3584]{1,0:T(8,128)(2,1)S(1)}, bf16[64,3584]{1,0:T(8,128)(2,1)}, u32[]{:S(2)}) copy-start(bf16[64,3584]{1,0:T(8,128)(2,1)} %param.6) | copy-start | bytes 1376260
  7.6 39.1 %all-to-all-start.2 = ((bf16[128,8,896]{2,1,0:T(8,128)(2,1)}), bf16[128,8,896]{2,1,0:T(8,128)(2,1)S(1)}, u32[]{:S(2)}, u32[]{:S(2)}) async-start(bf16[128,8,896]{2,1,0:T(8,128)(2,1)} %convert_bitcast_fusion), calls=%async_computation.2 | async-start | bytes 3670016 | tf_op jit(solution)/shard_map/all_to_all | solution.py:61
  46.8 52.6 %all-to-all-start = ((bf16[128,8,1792]{2,1,0:T(8,128)(2,1)}), bf16[128,8,1792]{2,1,0:T(8,128)(2,1)}, u32[]{:S(2)}, u32[]{:S(2)}) async-start(bf16[128,8,1792]{2,1,0:T(8,128)(2,1)} %fusion.19), calls=%async_computation | async-start | bytes 7340032 | tf_op jit(solution)/shard_map/all_to_all | solution.py:61
  99.4 38.3 %all-to-all-start.3 = ((bf16[128,8,896]{2,1,0:T(8,128)(2,1)}), bf16[128,8,896]{2,1,0:T(8,128)(2,1)S(1)}, u32[]{:S(2)}, u32[]{:S(2)}) async-start(bf16[128,8,896]{2,1,0:T(8,128)(2,1)} %reshape.253), calls=%async_computation.3 | async-start | bytes 3670016 | tf_op jit(solution)/shard_map/all_to_all | solution.py:69
  137.7 10.3 %copy-start.1 = (f32[64,8]{0,1:T(8,128)S(1)}, f32[64,8]{0,1:T(8,128)}, u32[]{:S(2)}) copy-start(f32[64,8]{0,1:T(8,128)} %param.8) | copy-start | bytes 6148
  137.7 57.3 %all-to-all-start.1 = ((bf16[128,8,1792]{2,1,0:T(8,128)(2,1)}), bf16[128,8,1792]{2,1,0:T(8,128)(2,1)}, u32[]{:S(2)}, u32[]{:S(2)}) async-start(bf16[128,8,1792]{2,1,0:T(8,128)(2,1)} %reshape.246), calls=%async_computation.1 | async-start | bytes 7340032 | tf_op jit(solution)/shard_map/all_to_all | solution.py:69

commit v12 on v10

--- a/solution.py
+++ b/solution.py
@@ -82,12 +82,9 @@
             concat_axis=0,
             tiled=True,
         ).reshape(chunk_rows * pieces, piece)
-        combine_hi = combine.astype(jnp.bfloat16)
-        combine_lo = (combine - combine_hi.astype(jnp.float32)).astype(jnp.bfloat16)
-        stacked = jnp.concatenate([combine_hi, combine_lo], axis=0)
-        part = jnp.dot(stacked, answered, preferred_element_type=jnp.float32)
-        half = tok_dev * pieces
-        part = (part[:half] + part[half:]).reshape(tok_dev, d_model)
+        part = jnp.dot(
+            combine.astype(jnp.bfloat16), answered, preferred_element_type=jnp.float32
+        ).reshape(tok_dev, d_model)
         weighted = part if weighted is None else weighted + part
     return weighted.astype(jnp.bfloat16)
 

time: 201 us -> 201 us (level)
  transfers between devices with their start and end apart: 4 -> 4, of which waited for: 3 -> 3; matrix products, arithmetic and copies ran while one was open for 31% -> 30% of each run, Pallas kernels for 0% -> 0%
where the time goes in v12:
time: 201 us; the launch traced here: 200 us
  waiting for transfers between devices  93.8 us (47%)
  matrix products  42.4 us (21%)
  starting transfers between devices  32.6 us (16%)
  local copies, waits for them, and re-layouts  27.8 us (14%)
  other arithmetic  3 us (1%)
    all_to_all x2, waiting for transfers between devices, local(): lax.all_to_all(outgoing.reshape(experts, chunk_slots * pieces, piece), 'e...  51 us
    all_to_all x2, waiting for transfers between devices, local(): lax.all_to_all(expert_out.reshape(experts, chunk_slots * pieces, piece),...  42.8 us
    dot_general x2, matrix products, expert_ffn(): jnp.einsum('rd,hdgu->rhgu', rows, first_weights, preferred_element_type=j...  20.4 us
    all_to_all x2, starting transfers between devices, local(): lax.all_to_all(outgoing.reshape(experts, chunk_slots * pieces, piece), 'e...  16.9 us
    all_to_all x2, starting transfers between devices, local(): lax.all_to_all(expert_out.reshape(experts, chunk_slots * pieces, piece),...  15.7 us
    reshape x2, local copies, waits for them, and re-layouts, local(): received.reshape(chunk_rows, d_model)  10.7 us
    reshape x2, local copies, waits for them, and re-layouts, local(): expert_out.reshape(experts, chunk_slots * pieces, piece)  10.3 us
    dot_general x2, matrix products, local(): jnp.dot(dispatch, token_pieces, preferred_element_type=jnp.float32)  6.46 us
  transfers between devices with their start and end apart: 4, of which 3 were waited for; matrix products, arithmetic and copies ran while one was open for 30% of the time, Pallas kernels for 0%

profile of v12, /device:TPU:1, one launch (start us, length us, event | category | flops | bytes accessed | tf_op | source)
XLA Modules:
  0.0 199.9 jit_solution(204491014469076615)
XLA Ops:
  0.0 0.8 copy.30
  1.0 0.8 select_reduce_fusion.1
  2.2 0.3 select_reduce_fusion
  2.5 1.3 reshape.253
  4.0 0.6 slice_reduce_fusion.15
  4.7 3.0 %convert_bitcast_fusion = bf16[128,8,896]{2,1,0:T(8,128)(2,1)} fusion(bf16[256,896]{1,0:T(8,128)(2,1)S(1)} %reshape.253, s32[1024]{0:T(1024)S(1)} %get-tuple-element.45, s32[1024]{0:T(1024)S(1)} %get-tuple-element.46, s32[256]{0:T(256)S(1)} %get-tuple-element.14, s32[256]{0:T(256)S(1)} %get-tuple-element.15, s32[256]{0:T(256)S(1)} %get-tuple-element.16, ...), kind=kOutput, calls=%fused_computation.26 | convolution fusion | flops 475136000 | bytes 2311168 | tf_op jit(solution)/shard_map/dot_general | solution.py:67
  7.6 11.5 %all-to-all-start.2 = ((bf16[128,8,896]{2,1,0:T(8,128)(2,1)}), bf16[128,8,896]{2,1,0:T(8,128)(2,1)S(1)}, u32[]{:S(2)}, u32[]{:S(2)}) async-start(bf16[128,8,896]{2,1,0:T(8,128)(2,1)} %convert_bitcast_fusion), calls=%async_computation.2 | async-start | bytes 3670016 | tf_op jit(solution)/shard_map/all_to_all | solution.py:68
  19.6 0.4 slice_reduce_fusion.31
  20.0 3.5 %fusion.20 = bf16[128,8,1792]{2,1,0:T(8,128)(2,1)} fusion(bf16[128,1792]{1,0:T(8,128)(2,1)S(1)} %reshape.246, s32[1024]{0:T(1024)S(1)} %get-tuple-element.43, s32[1024]{0:T(1024)S(1)} %get-tuple-element.44, s32[128]{0:T(128)S(1)} %get-tuple-element.30, s32[128]{0:T(128)S(1)} %get-tuple-element.31, s32[128]{0:T(128)S(1)} %get-tuple-element.32, ...), kind=kOutput, calls=%fused_computation.18 | convolution fusion | flops 473825280 | bytes 4141568 | tf_op jit(solution)/shard_map/dot_general | solution.py:67
  23.4 23.4 %all-to-all-done.2 = bf16[128,8,896]{2,1,0:T(8,128)(2,1)S(1)} async-done(((bf16[128,8,896]{2,1,0:T(8,128)(2,1)}), bf16[128,8,896]{2,1,0:T(8,128)(2,1)S(1)}, u32[]{:S(2)}, u32[]{:S(2)}) %all-to-all-start.2) | async-done | bytes 1835040 | tf_op jit(solution)/shard_map/all_to_all | solution.py:68
  46.8 1.3 copy-done
  48.1 5.4 %all-to-all-start = ((bf16[128,8,1792]{2,1,0:T(8,128)(2,1)}), bf16[128,8,1792]{2,1,0:T(8,128)(2,1)}, u32[]{:S(2)}, u32[]{:S(2)}) async-start(bf16[128,8,1792]{2,1,0:T(8,128)(2,1)} %fusion.20), calls=%async_computation | async-start | bytes 7340032 | tf_op jit(solution)/shard_map/all_to_all | solution.py:68
  53.6 4.1 %reshape.260 = bf16[256,3584,1,1]{1,0,2,3:T(8,128)(2,1)} reshape(bf16[128,8,896]{2,1,0:T(8,128)(2,1)} %copy-done) | data formatting | bytes 3670016 | tf_op jit(solution)/shard_map/reshape | solution.py:76
  57.7 8.0 %fusion = f32[256,2,2,512]{3,0,2,1:T(8,128)S(1)} fusion(bf16[2,3584,2,512]{3,2,1,0:T(2,128)(2,1)} %bitcast.83, bf16[256,3584,1,1]{1,0,2,3:T(8,128)(2,1)} %reshape.260), kind=kOutput, calls=%fused_computation | convolution fusion | flops 3758096384 | bytes 18612224 | tf_op jit(solution)/shard_map/rd,hdgu->rhgu/dot_general | solution.py:11
  65.7 3.4 %fusion.9 = bf16[256,3584]{1,0:T(8,128)(2,1)} fusion(bf16[1,2,512,3584]{3,2,1,0:T(8,128)(2,1)S(1)} %bitcast.75, f32[256,2,2,512]{3,0,2,1:T(8,128)S(1)} %fusion), kind=kOutput, calls=%fused_computation.8 | convolution fusion | flops 1881538560 | bytes 11272192 | tf_op jit(solution)/shard_map/rhu,hud->rd/dot_general | solution.py:16
  69.1 3.9 %reshape.256 = bf16[128,8,896]{2,1,0:T(8,128)(2,1)} reshape(bf16[256,3584]{1,0:T(8,128)(2,1)} %fusion.9) | data formatting | bytes 3670016 | tf_op jit(solution)/shard_map/reshape | solution.py:79
  73.0 27.7 %all-to-all-done = bf16[128,8,1792]{2,1,0:T(8,128)(2,1)} async-done(((bf16[128,8,1792]{2,1,0:T(8,128)(2,1)}), bf16[128,8,1792]{2,1,0:T(8,128)(2,1)}, u32[]{:S(2)}, u32[]{:S(2)}) %all-to-all-start) | async-done | bytes 3670048 | tf_op jit(solution)/shard_map/all_to_all | solution.py:68
  100.7 5.4 %all-to-all-start.3 = ((bf16[128,8,896]{2,1,0:T(8,128)(2,1)}), bf16[128,8,896]{2,1,0:T(8,128)(2,1)}, u32[]{:S(2)}, u32[]{:S(2)}) async-start(bf16[128,8,896]{2,1,0:T(8,128)(2,1)} %reshape.256), calls=%async_computation.3 | async-start | bytes 3670016 | tf_op jit(solution)/shard_map/all_to_all | solution.py:78
  106.2 6.6 %reshape.259 = bf16[512,3584,1,1]{1,0,2,3:T(8,128)(2,1)} reshape(bf16[128,8,1792]{2,1,0:T(8,128)(2,1)} %all-to-all-done) | data formatting | bytes 7340032 | tf_op jit(solution)/shard_map/reshape | solution.py:76
  112.7 12.4 %fusion.2 = f32[512,2,2,512]{3,0,2,1:T(8,128)S(1)} fusion(bf16[2,3584,2,512]{3,2,1,0:T(2,128)(2,1)} %bitcast.84, bf16[512,3584,1,1]{1,0,2,3:T(8,128)(2,1)} %reshape.259), kind=kOutput, calls=%fused_computation.2 | convolution fusion | flops 7516192768 | bytes 22544384 | tf_op jit(solution)/shard_map/rd,hdgu->rhgu/dot_general | solution.py:11
  125.1 0.7 fusion.22
  125.9 2.1 %fusion.15 = f32[512,3584]{1,0:T(8,128)S(1)} fusion(bf16[1,2,512,3584]{3,2,1,0:T(8,128)(2,1)S(1)} %bitcast.77, bf16[512,2,512]{2,0,1:T(8,128)(2,1)S(1)} %fusion.22), kind=kOutput, calls=%fused_computation.13 | convolution fusion | flops 1879048192 | bytes 11534336 | tf_op jit(solution)/shard_map/dot_general | solution.py:20
  127.9 4.0 %add_convert_fusion = bf16[512,3584]{1,0:T(8,128)(2,1)} fusion(f32[512,3584]{1,0:T(8,128)S(1)} %fusion.15, bf16[1,2,512,3584]{3,2,1,0:T(8,128)(2,1)S(1)} %bitcast.77, bf16[512,2,512]{2,0,1:T(8,128)(2,1)S(1)} %fusion.22), kind=kOutput, calls=%fused_computation.6 | convolution fusion | flops 1882718208 | bytes 15204352 | tf_op jit(solution)/shard_map/dot_general | solution.py:22
  131.9 6.4 %reshape.249 = bf16[128,8,1792]{2,1,0:T(8,128)(2,1)} reshape(bf16[512,3584]{1,0:T(8,128)(2,1)} %add_convert_fusion) | data formatting | bytes 7340032 | tf_op jit(solution)/shard_map/reshape | solution.py:79
  138.3 10.3 %all-to-all-start.1 = ((bf16[128,8,1792]{2,1,0:T(8,128)(2,1)}), bf16[128,8,1792]{2,1,0:T(8,128)(2,1)}, u32[]{:S(2)}, u32[]{:S(2)}) async-start(bf16[128,8,1792]{2,1,0:T(8,128)(2,1)} %reshape.249), calls=%async_computation.1 | async-start | bytes 7340032 | tf_op jit(solution)/shard_map/all_to_all | solution.py:78
  148.8 0.4 slice_reduce_fusion.30
  149.2 0.6 slice_reduce_fusion.14
  149.8 2.9 %fusion.23 = f32[256,896]{1,0:T(8,128)S(1)} fusion(bf16[128,8,896]{2,1,0:T(8,128)(2,1)} %all-to-all-done.3, f32[256]{0:T(256)S(1)} %get-tuple-element.6, f32[256]{0:T(256)S(1)} %get-tuple-element.7, f32[256]{0:T(256)S(1)} %get-tuple-element.8, f32[256]{0:T(256)S(1)} %get-tuple-element.9, f32[256]{0:T(256)S(1)} %get-tuple-element.10, ...), kind=kOutput, calls=%fused_computation.23 | convolution fusion | flops 476577792 | bytes 2778112 | tf_op jit(solution)/shard_map/dot_general | solution.py:85
  152.9 42.8 %all-to-all-done.1 = bf16[128,8,1792]{2,1,0:T(8,128)(2,1)} async-done(((bf16[128,8,1792]{2,1,0:T(8,128)(2,1)}), bf16[128,8,1792]{2,1,0:T(8,128)(2,1)}, u32[]{:S(2)}, u32[]{:S(2)}) %all-to-all-start.1) | async-done | bytes 3670048 | tf_op jit(solution)/shard_map/all_to_all | solution.py:78
  195.7 3.1 %fusion.12 = f32[128,1792]{1,0:T(8,128)S(1)} fusion(bf16[128,8,1792]{2,1,0:T(8,128)(2,1)} %all-to-all-done.1, f32[128]{0:T(128)S(1)} %get-tuple-element.22, f32[128]{0:T(128)S(1)} %get-tuple-element.23, f32[128]{0:T(128)S(1)} %get-tuple-element.24, f32[128]{0:T(128)S(1)} %get-tuple-element.25, f32[128]{0:T(128)S(1)} %get-tuple-element.26, ...), kind=kOutput, calls=%fused_computation.10 | convolution fusion | flops 473169920 | bytes 4604416 | tf_op jit(solution)/shard_map/dot_general | solution.py:85
  198.8 0.3 reshape.251
  199.1 0.9 add_convert_fusion.1
  (43 shorter events, 1.5 us)
Async XLA Ops:
  4.7 14.5 %copy-start.1 = (bf16[64,3584]{1,0:T(8,128)(2,1)S(1)}, bf16[64,3584]{1,0:T(8,128)(2,1)}, u32[]{:S(2)}) copy-start(bf16[64,3584]{1,0:T(8,128)(2,1)} %param.6) | copy-start | bytes 1376260
  7.6 39.1 %all-to-all-start.2 = ((bf16[128,8,896]{2,1,0:T(8,128)(2,1)}), bf16[128,8,896]{2,1,0:T(8,128)(2,1)S(1)}, u32[]{:S(2)}, u32[]{:S(2)}) async-start(bf16[128,8,896]{2,1,0:T(8,128)(2,1)} %convert_bitcast_fusion), calls=%async_computation.2 | async-start | bytes 3670016 | tf_op jit(solution)/shard_map/all_to_all | solution.py:68
  46.8 1.3 copy-start
  48.1 52.6 %all-to-all-start = ((bf16[128,8,1792]{2,1,0:T(8,128)(2,1)}), bf16[128,8,1792]{2,1,0:T(8,128)(2,1)}, u32[]{:S(2)}, u32[]{:S(2)}) async-start(bf16[128,8,1792]{2,1,0:T(8,128)(2,1)} %fusion.20), calls=%async_computation | async-start | bytes 7340032 | tf_op jit(solution)/shard_map/all_to_all | solution.py:68
  53.6 12.1 %slice-start = ((s8[7340032]{0:T(1024)(128)(4,1)}), s8[3145728]{0:T(1024)(128)(4,1)S(1)}, s32[]{:S(2)}) async-start(s8[7340032]{0:T(1024)(128)(4,1)} %bitcast.74), calls=%async_computation.4 | async-start | bytes 6291456
  57.7 8.0 %slice-start.1 = ((s8[7340032]{0:T(1024)(128)(4,1)}), s8[4194304]{0:T(1024)(128)(4,1)S(1)}, s32[]{:S(2)}) async-start(s8[7340032]{0:T(1024)(128)(4,1)} %bitcast.74), calls=%async_computation.5 | async-start | bytes 8388608
  100.7 37.6 %all-to-all-start.3 = ((bf16[128,8,896]{2,1,0:T(8,128)(2,1)}), bf16[128,8,896]{2,1,0:T(8,128)(2,1)}, u32[]{:S(2)}, u32[]{:S(2)}) async-start(bf16[128,8,896]{2,1,0:T(8,128)(2,1)} %reshape.256), calls=%async_computation.3 | async-start | bytes 3670016 | tf_op jit(solution)/shard_map/all_to_all | solution.py:78
  106.2 19.7 %slice-start.2 = ((s8[7340032]{0:T(1024)(128)(4,1)}), s8[3145728]{0:T(1024)(128)(4,1)S(1)}, s32[]{:S(2)}) async-start(s8[7340032]{0:T(1024)(128)(4,1)} %bitcast.76), calls=%async_computation.6 | async-start | bytes 6291456
  112.7 13.1 %slice-start.3 = ((s8[7340032]{0:T(1024)(128)(4,1)}), s8[4194304]{0:T(1024)(128)(4,1)S(1)}, s32[]{:S(2)}) async-start(s8[7340032]{0:T(1024)(128)(4,1)} %bitcast.76), calls=%async_computation.7 | async-start | bytes 8388608
  138.3 10.3 %copy-start.2 = (f32[64,8]{0,1:T(8,128)S(1)}, f32[64,8]{0,1:T(8,128)}, u32[]{:S(2)}) copy-start(f32[64,8]{0,1:T(8,128)} %param.8) | copy-start | bytes 6148
  138.3 57.3 %all-to-all-start.1 = ((bf16[128,8,1792]{2,1,0:T(8,128)(2,1)}), bf16[128,8,1792]{2,1,0:T(8,128)(2,1)}, u32[]{:S(2)}, u32[]{:S(2)}) async-start(bf16[128,8,1792]{2,1,0:T(8,128)(2,1)} %reshape.249), calls=%async_computation.1 | async-start | bytes 7340032 | tf_op jit(solution)/shard_map/all_to_all | solution.py:78

commit v13 on v6

--- a/solution.py
+++ b/solution.py
@@ -28,7 +28,9 @@
     holder = jnp.sum(placed * expert_range[:, None], axis=0)
     flat_experts = expert_ids.reshape(-1)
     onehot = (flat_experts[:, None] == expert_range[None, :]).astype(jnp.int32)
-    within = jnp.sum(jnp.cumsum(onehot, axis=0) * onehot, axis=1) - 1
+    order = jnp.arange(flat_experts.shape[0], dtype=jnp.int32)
+    earlier = (flat_experts[None, :] == flat_experts[:, None]) & (order[None, :] < order[:, None])
+    within = jnp.sum(earlier.astype(jnp.int32), axis=1)
     target = jnp.sum(onehot * holder[None, :], axis=1)
     within_of = within.reshape(tok_dev, top_count)
     target_of = target.reshape(tok_dev, top_count)

time: 200 us -> 200 us (level)
  no operation moved by 1% of the time
where the time goes in v13:
time: 200 us; the launch traced here: 199 us
  waiting for transfers between devices  95.9 us (48%)
  matrix products  44.8 us (22%)
  starting transfers between devices  31.7 us (16%)
  local copies, waits for them, and re-layouts  22.2 us (11%)
  other arithmetic  4.08 us (2%)
    all_to_all x2, waiting for transfers between devices, local(): lax.all_to_all(outgoing.reshape(experts, chunk_slots * pieces, piece), 'e...  53.2 us
    all_to_all x2, waiting for transfers between devices, local(): lax.all_to_all(expert_out.reshape(experts, chunk_slots * pieces, piece),...  42.7 us
    dot_general x2, matrix products, expert_ffn(): jnp.einsum('rd,hdgu->rhgu', rows, first_weights, preferred_element_type=j...  20.1 us
    all_to_all x2, starting transfers between devices, local(): lax.all_to_all(outgoing.reshape(experts, chunk_slots * pieces, piece), 'e...  16.9 us
    all_to_all x2, starting transfers between devices, local(): lax.all_to_all(expert_out.reshape(experts, chunk_slots * pieces, piece),...  14.8 us
    dot_general x2, matrix products, expert_ffn(): jnp.einsum('rhu,hud->rd', hidden, second_weights, preferred_element_type=...  13.8 us
    reshape x2, local copies, waits for them, and re-layouts, local(): received.reshape(chunk_rows, d_model)  8.51 us
    reshape x2, local copies, waits for them, and re-layouts, local(): expert_out.reshape(experts, chunk_slots * pieces, piece)  8.5 us
  transfers between devices with their start and end apart: 4, of which 3 were waited for; matrix products, arithmetic and copies ran while one was open for 30% of the time, Pallas kernels for 0%

profile of v13, /device:TPU:1, one launch (start us, length us, event | category | flops | bytes accessed | tf_op | source)
XLA Modules:
  0.0 198.9 jit_solution(13293715187252078181)
XLA Ops:
  0.0 0.8 copy.21
  0.9 0.3 convert_reduce_fusion
  1.1 0.8 select_reduce_fusion.1
  1.9 0.2 select_reduce_fusion
  2.1 1.3 reshape.231
  3.7 0.6 slice_reduce_fusion.15
  4.3 3.0 %convert_bitcast_fusion = bf16[128,8,896]{2,1,0:T(8,128)(2,1)} fusion(bf16[256,896]{1,0:T(8,128)(2,1)S(1)} %reshape.231, s32[1024]{0:T(1024)S(1)} %get-tuple-element.47, s32[1024]{0:T(1024)S(1)} %get-tuple-element.48, s32[256]{0:T(256)S(1)} %get-tuple-element.14, s32[256]{0:T(256)S(1)} %get-tuple-element.15, s32[256]{0:T(256)S(1)} %get-tuple-element.16, ...), kind=kOutput, calls=%fused_computation.21 | convolution fusion | flops 475136000 | bytes 2311168 | tf_op jit(solution)/shard_map/dot_general | solution.py:62
  7.3 11.5 %all-to-all-start.2 = ((bf16[128,8,896]{2,1,0:T(8,128)(2,1)}), bf16[128,8,896]{2,1,0:T(8,128)(2,1)S(1)}, u32[]{:S(2)}, u32[]{:S(2)}) async-start(bf16[128,8,896]{2,1,0:T(8,128)(2,1)} %convert_bitcast_fusion), calls=%async_computation.2 | async-start | bytes 3670016 | tf_op jit(solution)/shard_map/all_to_all | solution.py:63
  19.2 0.4 slice_reduce_fusion.31
  19.6 3.5 %fusion.19 = bf16[128,8,1792]{2,1,0:T(8,128)(2,1)} fusion(bf16[128,1792]{1,0:T(8,128)(2,1)S(1)} %reshape.224, s32[1024]{0:T(1024)S(1)} %get-tuple-element.45, s32[1024]{0:T(1024)S(1)} %get-tuple-element.46, s32[128]{0:T(128)S(1)} %get-tuple-element.30, s32[128]{0:T(128)S(1)} %get-tuple-element.31, s32[128]{0:T(128)S(1)} %get-tuple-element.32, ...), kind=kOutput, calls=%fused_computation.15 | convolution fusion | flops 473825280 | bytes 4141568 | tf_op jit(solution)/shard_map/dot_general | solution.py:62
  23.1 23.4 %all-to-all-done.2 = bf16[128,8,896]{2,1,0:T(8,128)(2,1)S(1)} async-done(((bf16[128,8,896]{2,1,0:T(8,128)(2,1)}), bf16[128,8,896]{2,1,0:T(8,128)(2,1)S(1)}, u32[]{:S(2)}, u32[]{:S(2)}) %all-to-all-start.2) | async-done | bytes 1835040 | tf_op jit(solution)/shard_map/all_to_all | solution.py:63
  46.4 5.4 %all-to-all-start = ((bf16[128,8,1792]{2,1,0:T(8,128)(2,1)}), bf16[128,8,1792]{2,1,0:T(8,128)(2,1)}, u32[]{:S(2)}, u32[]{:S(2)}) async-start(bf16[128,8,1792]{2,1,0:T(8,128)(2,1)} %fusion.19), calls=%async_computation | async-start | bytes 7340032 | tf_op jit(solution)/shard_map/all_to_all | solution.py:63
  51.9 2.1 %reshape.239 = bf16[256,3584,1,1]{1,0,2,3:T(8,128)(2,1)} reshape(bf16[128,8,896]{2,1,0:T(8,128)(2,1)S(1)} %all-to-all-done.2) | data formatting | bytes 3670016 | tf_op jit(solution)/shard_map/reshape | solution.py:70
  54.0 7.8 %fusion = f32[256,2,2,512]{3,0,2,1:T(8,128)S(1)} fusion(bf16[2,3584,2,512]{3,2,1,0:T(2,128)(2,1)} %bitcast.50, bf16[256,3584,1,1]{1,0,2,3:T(8,128)(2,1)} %reshape.239), kind=kOutput, calls=%fused_computation | convolution fusion | flops 3758096384 | bytes 18612224 | tf_op jit(solution)/shard_map/rd,hdgu->rhgu/dot_general | solution.py:11
  61.8 5.2 %fusion.13 = bf16[256,3584]{1,0:T(8,128)(2,1)S(1)} fusion(bf16[1,2,512,3584]{3,2,1,0:T(8,128)(2,1)} %param.11, f32[256,2,2,512]{3,0,2,1:T(8,128)S(1)} %fusion), kind=kOutput, calls=%fused_computation.10 | convolution fusion | flops 1881538560 | bytes 11272192 | tf_op jit(solution)/shard_map/rhu,hud->rd/dot_general | solution.py:15
  67.1 2.1 %reshape.234 = bf16[128,8,896]{2,1,0:T(8,128)(2,1)} reshape(bf16[256,3584]{1,0:T(8,128)(2,1)S(1)} %fusion.13) | data formatting | bytes 3670016 | tf_op jit(solution)/shard_map/reshape | solution.py:72
  69.2 29.9 %all-to-all-done = bf16[128,8,1792]{2,1,0:T(8,128)(2,1)} async-done(((bf16[128,8,1792]{2,1,0:T(8,128)(2,1)}), bf16[128,8,1792]{2,1,0:T(8,128)(2,1)}, u32[]{:S(2)}, u32[]{:S(2)}) %all-to-all-start) | async-done | bytes 3670048 | tf_op jit(solution)/shard_map/all_to_all | solution.py:63
  99.1 4.6 %all-to-all-start.3 = ((bf16[128,8,896]{2,1,0:T(8,128)(2,1)}), bf16[128,8,896]{2,1,0:T(8,128)(2,1)S(1)}, u32[]{:S(2)}, u32[]{:S(2)}) async-start(bf16[128,8,896]{2,1,0:T(8,128)(2,1)} %reshape.234), calls=%async_computation.3 | async-start | bytes 3670016 | tf_op jit(solution)/shard_map/all_to_all | solution.py:71
  103.7 6.4 %reshape.237 = bf16[512,3584,1,1]{1,0,2,3:T(8,128)(2,1)} reshape(bf16[128,8,1792]{2,1,0:T(8,128)(2,1)} %all-to-all-done) | data formatting | bytes 7340032 | tf_op jit(solution)/shard_map/reshape | solution.py:70
  110.1 12.2 %fusion.2 = f32[512,2,2,512]{3,0,2,1:T(8,128)S(1)} fusion(bf16[2,3584,2,512]{3,2,1,0:T(2,128)(2,1)} %bitcast.51, bf16[512,3584,1,1]{1,0,2,3:T(8,128)(2,1)} %reshape.237), kind=kOutput, calls=%fused_computation.2 | convolution fusion | flops 7516192768 | bytes 22544384 | tf_op jit(solution)/shard_map/rd,hdgu->rhgu/dot_general | solution.py:11
  122.4 8.6 %bitcast_convert_fusion = bf16[512,3584]{1,0:T(8,128)(2,1)} fusion(bf16[1,2,512,3584]{3,2,1,0:T(8,128)(2,1)} %param.11, f32[512,2,2,512]{3,0,2,1:T(8,128)S(1)} %fusion.2), kind=kOutput, calls=%fused_computation.4 | convolution fusion | flops 3763077120 | bytes 15204352 | tf_op jit(solution)/shard_map/rhu,hud->rd/dot_general | solution.py:15
  130.9 6.4 %reshape.227 = bf16[128,8,1792]{2,1,0:T(8,128)(2,1)} reshape(bf16[512,3584]{1,0:T(8,128)(2,1)} %bitcast_convert_fusion) | data formatting | bytes 7340032 | tf_op jit(solution)/shard_map/reshape | solution.py:72
  137.4 10.1 %all-to-all-start.1 = ((bf16[128,8,1792]{2,1,0:T(8,128)(2,1)}), bf16[128,8,1792]{2,1,0:T(8,128)(2,1)}, u32[]{:S(2)}, u32[]{:S(2)}) async-start(bf16[128,8,1792]{2,1,0:T(8,128)(2,1)} %reshape.227), calls=%async_computation.1 | async-start | bytes 7340032 | tf_op jit(solution)/shard_map/all_to_all | solution.py:71
  147.6 0.4 slice_reduce_fusion.30
  148.0 0.6 slice_reduce_fusion.14
  148.6 0.5 subtract_convert_fusion.1
  149.2 1.1 subtract_convert_fusion
  150.3 1.3 fusion.21
  151.8 42.7 %all-to-all-done.1 = bf16[128,8,1792]{2,1,0:T(8,128)(2,1)} async-done(((bf16[128,8,1792]{2,1,0:T(8,128)(2,1)}), bf16[128,8,1792]{2,1,0:T(8,128)(2,1)}, u32[]{:S(2)}, u32[]{:S(2)}) %all-to-all-start.1) | async-done | bytes 3670048 | tf_op jit(solution)/shard_map/all_to_all | solution.py:71
  194.5 3.1 %fusion.16 = f32[256,1792]{1,0:T(8,128)S(1)} fusion(bf16[128,8,1792]{2,1,0:T(8,128)(2,1)} %all-to-all-done.1, bf16[128,1024]{1,0:T(8,128)(2,1)S(1)} %get-tuple-element.39, bf16[128,1024]{1,0:T(8,128)(2,1)S(1)} %get-tuple-element.40), kind=kOutput, calls=%fused_computation.12 | convolution fusion | flops 940572672 | bytes 6029312 | tf_op jit(solution)/shard_map/dot_general | solution.py:81
  197.8 0.3 reshape.229
  198.0 0.9 add_convert_fusion
  (25 shorter events, 1.2 us)
Async XLA Ops:
  4.3 14.5 %copy-start = (bf16[64,3584]{1,0:T(8,128)(2,1)S(1)}, bf16[64,3584]{1,0:T(8,128)(2,1)}, u32[]{:S(2)}) copy-start(bf16[64,3584]{1,0:T(8,128)(2,1)} %param.6) | copy-start | bytes 1376260
  7.3 39.1 %all-to-all-start.2 = ((bf16[128,8,896]{2,1,0:T(8,128)(2,1)}), bf16[128,8,896]{2,1,0:T(8,128)(2,1)S(1)}, u32[]{:S(2)}, u32[]{:S(2)}) async-start(bf16[128,8,896]{2,1,0:T(8,128)(2,1)} %convert_bitcast_fusion), calls=%async_computation.2 | async-start | bytes 3670016 | tf_op jit(solution)/shard_map/all_to_all | solution.py:63
  46.4 52.6 %all-to-all-start = ((bf16[128,8,1792]{2,1,0:T(8,128)(2,1)}), bf16[128,8,1792]{2,1,0:T(8,128)(2,1)}, u32[]{:S(2)}, u32[]{:S(2)}) async-start(bf16[128,8,1792]{2,1,0:T(8,128)(2,1)} %fusion.19), calls=%async_computation | async-start | bytes 7340032 | tf_op jit(solution)/shard_map/all_to_all | solution.py:63
  99.1 38.3 %all-to-all-start.3 = ((bf16[128,8,896]{2,1,0:T(8,128)(2,1)}), bf16[128,8,896]{2,1,0:T(8,128)(2,1)S(1)}, u32[]{:S(2)}, u32[]{:S(2)}) async-start(bf16[128,8,896]{2,1,0:T(8,128)(2,1)} %reshape.234), calls=%async_computation.3 | async-start | bytes 3670016 | tf_op jit(solution)/shard_map/all_to_all | solution.py:71
  137.4 10.2 %copy-start.1 = (f32[64,8]{0,1:T(8,128)S(1)}, f32[64,8]{0,1:T(8,128)}, u32[]{:S(2)}) copy-start(f32[64,8]{0,1:T(8,128)} %param.8) | copy-start | bytes 6148
  137.4 57.2 %all-to-all-start.1 = ((bf16[128,8,1792]{2,1,0:T(8,128)(2,1)}), bf16[128,8,1792]{2,1,0:T(8,128)(2,1)}, u32[]{:S(2)}, u32[]{:S(2)}) async-start(bf16[128,8,1792]{2,1,0:T(8,128)(2,1)} %reshape.227), calls=%async_computation.1 | async-start | bytes 7340032 | tf_op jit(solution)/shard_map/all_to_all | solution.py:71
